TPU v7x, 32 devices: a whole 2x2x4 slice. The times are simulated.
32 devices in a mesh: dp: 8 (over y, x, core), fsdp: 4 (over z).
Axes of the slice: x: 2, y: 2, z: 4, core: 2. Of those that a mesh axis runs over, the one named last changes fastest.
Arguments:
- activations: bfloat16 [8192, 4096], P(('dp', 'fsdp')), may hold values from -8 to 8
- cotangents: bfloat16 [8192, 4096], P('dp', 'fsdp'), may hold values from -8 to 8
- group_ids: int32 [32, 256], P(('dp', 'fsdp')), may hold values from 0 to 7, as said below
- weights: float32 [4096, 4096], P('fsdp', 'dp'), may hold values from -0.09375 to 0.09375
- first_moment: float32 [4096, 4096], P('fsdp', 'dp'), may hold values from -3 to 3
- second_moment: float32 [4096, 4096], P('fsdp', 'dp'), may hold values from 0.01 to 0.1
- fresh_noise: bfloat16 [4096, 4096], P('fsdp', 'dp'), may hold values from -6 to 6
- history: bfloat16 [16, 4096, 4096], P('dp', 'fsdp'), may hold values from -6 to 6
- slot_ids: int32 [16], P('dp'), may hold values from 0 to 15, each once
- band_coefs: float32 [16], replicated, may hold values from 0.3 to 1
- step_number: int32 [1], replicated, may hold values from 16 to 99999
- noise_mult: float32 [1], replicated, may hold values from 0.002 to 0.008
Outputs:
- new_weights: float32 [4096, 4096], P('fsdp', 'dp')
- new_first: float32 [4096, 4096], P('fsdp', 'dp')
- new_second: float32 [4096, 4096], P('fsdp', 'dp')
- noisy_mean: float32 [4096, 4096], P('fsdp', 'dp')
- gathered_weights: float32 [4096, 4096], P('fsdp')
- new_history: bfloat16 [16, 4096, 4096], P('dp', 'fsdp')
Inputs may be any that keep to these rules, and one draw needn't show every extreme that they name: `group_ids`: in each row the ids never fall; each of the 8 ids names 1 to 64 tokens, one of them exactly 64. `slot_ids`: each cycle position is held by exactly one entry.
All inputs are finite; a program needn't handle non-finite values.
Results may differ from a plain program's by a relative error of at most 0.002.
Values may be sent and summed in bfloat16 or wider, within the bound.
No kernel may reach another device: no remote copies, remote signals or barrier semaphores. Data moves between devices by JAX's collectives and lax.ppermute only.
A program may use at most 192 MiB of HBM per device.

v0:
```python
import jax
import jax.numpy as jnp
from jax import lax
from jax.sharding import PartitionSpec as P

D_IN = 4096
D_OUT = 4096
BAND = 16
GROUP_MOST = 64
EX_DEV = 8


def clip_bound():
    return ((GROUP_MOST * GROUP_MOST / 4.0 + GROUP_MOST) * D_IN * D_OUT) ** 0.5


def body(
    activations,
    cotangents,
    group_ids,
    weights,
    first_moment,
    second_moment,
    fresh_noise,
    history,
    slot_ids,
    band_coefs,
    step_number,
    noise_mult,
):
    clip = clip_bound()
    token_count = activations.shape[0]
    out_local = cotangents.shape[1]
    step_value = step_number[0]
    target = step_value % BAND
    full_fresh = lax.all_gather(fresh_noise, "dp", axis=1, tiled=True)
    new_history = jnp.where((slot_ids == target)[:, None, None], full_fresh[None], history)
    blocks = cotangents.reshape(cotangents.shape[0] // token_count, token_count, out_local)
    partial_gram = jnp.einsum("ati,asi->ats", blocks, blocks, preferred_element_type=jnp.float32)
    cotan_gram = lax.psum_scatter(partial_gram, "fsdp", scatter_dimension=0, tiled=True)[0]
    input_gram = lax.dot_general(
        activations, activations, (((1,), (1,)), ((), ())), preferred_element_type=jnp.float32
    )
    labels = group_ids[0]
    same = labels[:, None] == labels[None, :]
    row_terms = jnp.sum(jnp.where(same, input_gram * cotan_gram, 0.0), axis=1)
    squared = jnp.sum(jnp.where(same, row_terms[None, :], 0.0), axis=1)
    factor = clip / jnp.maximum(jnp.sqrt(squared), clip)
    scaled = (activations.astype(jnp.float32) * factor[:, None]).astype(jnp.bfloat16)
    gradient = lax.dot_general(
        cotangents,
        lax.all_gather(scaled, "fsdp", axis=0, tiled=True),
        (((0,), (0,)), ((), ())),
        preferred_element_type=jnp.float32,
    )
    lags = (step_value - slot_ids - 1) % BAND + 1
    columns = jnp.arange(BAND, dtype=jnp.int32)
    lag_weight = jnp.sum(
        jnp.where(columns[None, :] == lags[:, None], band_coefs[None, :], 0.0), axis=1
    )
    history_part = jnp.zeros(history.shape[1:], jnp.float32)
    for position in range(history.shape[0]):
        history_part = history_part + lag_weight[position] * history[position].astype(jnp.float32)
    noise_scale = noise_mult[0] * clip
    combined = lax.psum_scatter(
        gradient + noise_scale * history_part, "dp", scatter_dimension=1, tiled=True
    )
    examples = EX_DEV * lax.axis_size("dp") * lax.axis_size("fsdp")
    noisy_mean = (
        combined + noise_scale * band_coefs[0] * fresh_noise.astype(jnp.float32)
    ) / examples
    new_first = 0.9 * first_moment + 0.1 * noisy_mean
    new_second = 0.999 * second_moment + 0.001 * noisy_mean * noisy_mean
    step_float = step_value.astype(jnp.float32)
    corrected_first = new_first / (1.0 - jnp.power(jnp.float32(0.9), step_float))
    corrected_second = new_second / (1.0 - jnp.power(jnp.float32(0.999), step_float))
    new_weights = weights - 0.002 * corrected_first / (jnp.sqrt(corrected_second) + 1e-08)
    gathered_weights = lax.all_gather(new_weights, "dp", axis=1, tiled=True)
    return (new_weights, new_first, new_second, noisy_mean, gathered_weights, new_history)


def solution(mesh):
    in_specs = (
        P(("dp", "fsdp"), None),
        P("dp", "fsdp"),
        P(("dp", "fsdp"), None),
        P("fsdp", "dp"),
        P("fsdp", "dp"),
        P("fsdp", "dp"),
        P("fsdp", "dp"),
        P("dp", "fsdp", None),
        P("dp"),
        P(),
        P(),
        P(),
    )
    out_specs = (
        P("fsdp", "dp"),
        P("fsdp", "dp"),
        P("fsdp", "dp"),
        P("fsdp", "dp"),
        P("fsdp", None),
        P("dp", "fsdp", None),
    )
    return jax.shard_map(body, mesh=mesh, in_specs=in_specs, out_specs=out_specs, check_vma=False)
```

profile of v0, /device:TPU:0, one launch (start us, length us, event | category | flops | bytes accessed | tf_op | source)
XLA Modules:
  0.0 505.7 jit_solution(12465230712963849113)
XLA Ops:
  7.2 0.0 copy-start
  7.2 0.0 reduce-scatter.3.cloned.1.call-start
  7.2 1.5 copy-done
  8.8 0.0 copy-start.7
  8.8 1.7 fusion.8
  10.5 0.0 reduce-scatter.3.cloned.1.call-update
  10.5 0.0 all-gather.4.cloned.1.call-start
  10.6 30.3 %reduce-scatter.3.cloned.1.call-done = f32[1,256,256]{2,1,0:T(8,128)} async-done(((f32[4,256,256]{2,1,0:T(8,128)}), f32[1,256,256]{2,1,0:T(8,128)}) %reduce-scatter.3.cloned.1.call-update) | async-done | bytes 262160 | tf_op jit(solution)/shard_map/reduce_scatter | solution.py:40
  40.9 0.0 copy-done.7
  40.9 0.0 copy-start.6
  40.9 3.2 fusion.1
  44.1 0.2 fusion.2
  44.3 0.0 copy-done.6
  44.3 1.9 multiply_convert_fusion
  46.2 0.0 all-gather.4.cloned.1.call-update
  46.2 0.0 reduce-scatter.5.cloned.1.call-start
  46.9 12.1 %fusion.6 = (bf16[1,1024,4096]{2,1,0:T(8,128)(2,1)}, bf16[1,1024,4096]{2,1,0:T(8,128)(2,1)}) fusion(bf16[2,1024,4096]{2,1,0:T(8,128)(2,1)} %param.19), kind=kLoop, calls=%fused_computation.22 | loop fusion | bytes 33554432 | tf_op jit(solution)/shard_map/slice | solution.py:63
  59.1 11.9 %copy.41 = bf16[1,1024,4096]{1,2,0:T(8,128)(2,1)} copy(bf16[1,1024,4096]{2,1,0:T(8,128)(2,1)} %get-tuple-element.22) | data formatting | bytes 16777216
  71.0 0.0 copy-start.9
  71.0 0.0 copy-start.8
  71.0 12.0 %copy.40 = bf16[1,1024,4096]{1,2,0:T(8,128)(2,1)} copy(bf16[1,1024,4096]{2,1,0:T(8,128)(2,1)} %get-tuple-element.21) | data formatting | bytes 16777216
  83.6 0.0 copy-done.9
  83.7 0.0 copy-done.8
  83.7 0.2 fusion.3
  83.9 0.6 fusion.7
  84.5 110.1 %all-gather.4.cloned.1.call-done = bf16[1024,4096]{1,0:T(8,128)(2,1)} async-done(((bf16[256,4096]{1,0:T(8,128)(2,1)}), bf16[1024,4096]{1,0:T(8,128)(2,1)}) %all-gather.4.cloned.1.call-update) | async-done | bytes 8388624 | tf_op jit(solution)/shard_map/all_gather | solution.py:52
  194.5 22.8 %bitcast_add_fusion = f32[1024,4096]{0,1:T(8,128)} fusion(bf16[1,1024,4096]{1,2,0:T(8,128)(2,1)} %copy.41, bf16[1,1024,4096]{1,2,0:T(8,128)(2,1)} %copy.40, bf16[1024,4096]{1,0:T(8,128)(2,1)} %all-gather.4.cloned.1.call-done, bf16[1024,1024]{1,0:T(8,128)(2,1)S(1)} %copy-done, f32[]{:T(128)} %bitcast.7, f32[]{:T(128)} %bitcast.6, f32[]{:T(128)} %bitcast.4), kind=kOutput, calls=%fused_computation | convolution fusion | flops 8619294720 | bytes 44040204 | tf_op jit(solution)/shard_map/dot_general | solution.py:50
  217.3 0.0 copy-start.4
  217.3 0.0 reduce-scatter.5.cloned.1.call-update
  217.3 0.0 all-gather.8.cloned.1.call-start
  217.4 0.5 all-gather.8.cloned.1.call-update
  217.9 0.2 all-gather.6.cloned.1.call-start
  218.1 0.4 copy-done.4
  218.5 1.3 copy.32
  219.8 2.3 copy.34
  222.2 3.1 copy.29
  225.3 0.0 copy-start.5
  225.3 3.3 copy.33
  228.6 103.2 %reduce-scatter.5.cloned.1.call-done = f32[1024,512]{0,1:T(8,128)} async-done(((f32[1024,4096]{0,1:T(8,128)}), f32[1024,512]{0,1:T(8,128)}) %reduce-scatter.5.cloned.1.call-update) | async-done | bytes 2097168 | tf_op jit(solution)/shard_map/reduce_scatter | solution.py:65
  331.9 0.0 copy-done.5
  331.9 7.7 %divide_subtract_fusion = (f32[1024,512]{0,1:T(8,128)}, f32[1024,512]{0,1:T(8,128)}, f32[1024,512]{0,1:T(8,128)}, f32[1024,512]{0,1:T(8,128)}) fusion(f32[1024,512]{0,1:T(8,128)S(1)} %copy.34, f32[]{:T(128)S(6)} %sub.22, f32[]{:T(128)S(6)} %sub.21, f32[1024,512]{0,1:T(8,128)} %reduce-scatter.5.cloned.1.call-done, bf16[1024,512]{0,1:T(8,128)(2,1)S(1)} %copy-done.5, ...), kind=kLoop, calls=%fused_computation.3 | loop fusion | flops 8912896 | bytes 17825804 | tf_op jit(solution)/shard_map/sub | solution.py:77
  339.6 0.0 all-gather.6.cloned.1.call-update
  339.6 0.0 copy-start.2
  339.6 49.8 %all-gather.8.cloned.1.call-done = bf16[1024,4096]{1,0:T(8,128)(2,1)} async-done(((bf16[1024,512]{1,0:T(8,128)(2,1)}), bf16[1024,4096]{1,0:T(8,128)(2,1)}) %all-gather.8.cloned.1.call-update) | async-done | bytes 8388624 | tf_op jit(solution)/shard_map/all_gather | solution.py:36
  389.5 16.7 %broadcast_select_fusion = bf16[2,1024,4096]{2,1,0:T(8,128)(2,1)} fusion(bf16[2,1024,4096]{2,1,0:T(8,128)(2,1)} %param.19, pred[2]{0:T(512)(128)(4,1)S(1)} %broadcast_compare_fusion, bf16[1024,4096]{1,0:T(8,128)(2,1)} %all-gather.8.cloned.1.call-done), kind=kLoop, calls=%fused_computation.1 | loop fusion | flops 8388608 | bytes 41943040 | tf_op jit(solution)/shard_map/jit(_where)/select_n | solution.py:37
  406.2 0.0 copy-done.2
  406.2 1.8 copy.35
  408.0 2.9 copy.36
  410.9 0.0 copy-start.3
  410.9 3.0 copy.37
  413.9 0.0 copy-done.3
  413.9 1.8 copy.38
  415.7 65.8 %all-gather.6.cloned.1.call-done = f32[1024,4096]{0,1:T(8,128)} async-done(((f32[1024,512]{0,1:T(8,128)}), f32[1024,4096]{0,1:T(8,128)}) %all-gather.6.cloned.1.call-update) | async-done | bytes 16777232 | tf_op jit(solution)/shard_map/all_gather | solution.py:78
  481.6 0.0 copy-start.1
  481.6 17.6 %copy.39 = f32[1024,4096]{1,0:T(8,128)} copy(f32[1024,4096]{0,1:T(8,128)} %all-gather.6.cloned.1.call-done) | data formatting | bytes 33554432
  499.1 0.0 copy-done.1
  (3 shorter events, 0.0 us)
Async XLA Ops:
  7.2 1.6 copy-start
  7.2 33.7 %reduce-scatter.3.cloned.1.call-start = ((), (), s32[]{:S(2)}) async-start(), calls=%async_computation.2 | async-start | bytes 1310720 | tf_op jit(solution)/shard_map/reduce_scatter | solution.py:40
  8.8 32.1 %copy-start.7 = (s32[1,256]{1,0:T(1,128)S(1)}, s32[1,256]{1,0:T(1,128)}, u32[]{:S(2)}) copy-start(s32[1,256]{1,0:T(1,128)} %param.14) | copy-start | bytes 3076
  10.5 184.0 %all-gather.4.cloned.1.call-start = ((), (), s32[]{:S(2)}) async-start(), calls=%async_computation.3 | async-start | bytes 10485760 | tf_op jit(solution)/shard_map/all_gather | solution.py:52
  40.9 3.4 copy-start.6
  46.2 285.6 %reduce-scatter.5.cloned.1.call-start = ((), (), s32[]{:S(2)}) async-start(), calls=%async_computation.4 | async-start | bytes 18874368 | tf_op jit(solution)/shard_map/reduce_scatter | solution.py:65
  71.0 12.6 %copy-start.9 = (s32[2]{0:T(128)S(1)}, s32[2]{0:T(128)}, u32[]{:S(2)}) copy-start(s32[2]{0:T(128)} %param.20) | copy-start | bytes 28
  71.0 12.7 %copy-start.8 = (f32[16]{0:T(128)S(1)}, f32[16]{0:T(128)}, u32[]{:S(2)}) copy-start(f32[16]{0:T(128)} %param.21) | copy-start | bytes 196
  217.3 1.2 copy-start.4
  217.3 172.2 %all-gather.8.cloned.1.call-start = ((), (), s32[]{:S(2)}) async-start(), calls=%async_computation.6 | async-start | bytes 9437184 | tf_op jit(solution)/shard_map/all_gather | solution.py:36
  217.9 263.7 %all-gather.6.cloned.1.call-start = ((), (), s32[]{:S(2)}) async-start(), calls=%async_computation.5 | async-start | bytes 18874368 | tf_op jit(solution)/shard_map/all_gather | solution.py:78
  225.3 106.6 %copy-start.5 = (bf16[1024,512]{0,1:T(8,128)(2,1)S(1)}, bf16[1024,512]{0,1:T(8,128)(2,1)}, u32[]{:S(2)}) copy-start(bf16[1024,512]{0,1:T(8,128)(2,1)} %copy.32) | copy-start | bytes 3145732
  339.6 66.6 %copy-start.2 = (f32[1024,512]{0,1:T(8,128)S(1)}, f32[1024,512]{0,1:T(8,128)}, u32[]{:S(2)}) copy-start(f32[1024,512]{0,1:T(8,128)} %get-tuple-element.18) | copy-start | bytes 6291460
  410.9 3.0 copy-start.3
  481.6 17.6 %copy-start.1 = (bf16[1024,1024]{1,0:T(8,128)(2,1)S(1)}, bf16[1024,1024]{1,0:T(8,128)(2,1)}, u32[]{:S(2)}) copy-start(bf16[1024,1024]{1,0:T(8,128)(2,1)} %param.13) | copy-start | bytes 6291460
Sparse Core Ops, SparseCore 0:
  10.9 29.9 reduce-scatter.2
  46.4 148.1 all-gather.3
  217.4 114.3 reduce-scatter.4
  333.6 55.8 all-gather.7
  391.8 89.7 all-gather.5
where the time goes:
time: 507 us; the launch traced here: 506 us
  waiting for transfers between devices  360 us (71%)
  local copies, waits for them, and re-layouts  75.7 us (15%)
  matrix products  27.7 us (5%)
  other arithmetic  26.8 us (5%)
  between operations  15.3 us (3%)
    all_gather x1, waiting for transfers between devices, body(): lax.all_gather(scaled, 'fsdp', axis=0, tiled=True)  110 us
    reduce_scatter x1, waiting for transfers between devices, body(): lax.psum_scatter(gradient + noise_scale * history_part, 'dp', scatter_dim...  103 us
    all_gather x1, waiting for transfers between devices, body(): gathered_weights = lax.all_gather(new_weights, 'dp', axis=1, tiled=True)  65.8 us
    unnamed x31, local copies, waits for them, and re-layouts  62.9 us
    all_gather x1, waiting for transfers between devices, body(): full_fresh = lax.all_gather(fresh_noise, 'dp', axis=1, tiled=True)  49.8 us
    reduce_scatter x1, waiting for transfers between devices, body(): lax.psum_scatter(partial_gram, 'fsdp', scatter_dimension=0, tiled=True)[0]  30.3 us
    dot_general x1, matrix products, body(): lax.dot_general(cotangents, lax.all_gather(scaled, 'fsdp', axis=0, tiled=...  22.8 us
    select_n x1, other arithmetic, body(): jnp.where((slot_ids == target)[:, None, None], full_fresh[None], history)  16.7 us
  transfers between devices with their start and end apart: 5, of which 5 were waited for; matrix products, arithmetic and copies ran while one was open for 16% of the time, Pallas kernels for 0%

commit v1 on v0

v1 whole, which is shorter than its diff:
```python
import jax
import jax.numpy as jnp
from jax import lax
from jax.sharding import PartitionSpec as P

D_IN = 4096
D_OUT = 4096
BAND = 16
GROUP_MOST = 64
EX_DEV = 8


def clip_bound():
    return ((GROUP_MOST * GROUP_MOST / 4.0 + GROUP_MOST) * D_IN * D_OUT) ** 0.5


def make_body(n_dp, n_fsdp, chunks):
    def body(
        activations,
        cotangents,
        group_ids,
        weights,
        first_moment,
        second_moment,
        fresh_noise,
        history,
        slot_ids,
        band_coefs,
        step_number,
        noise_mult,
    ):
        clip = clip_bound()
        tok = activations.shape[0]
        d_in = activations.shape[1]
        out_local = cotangents.shape[1]
        cols = d_in // n_dp
        width = cols // chunks
        me = lax.axis_index("fsdp")
        step_value = step_number[0]
        target = step_value % BAND

        blocks = cotangents.reshape(n_fsdp, tok, out_local)
        partial_gram = jnp.einsum("ati,asi->ats", blocks, blocks, preferred_element_type=jnp.float32)
        cotan_gram = lax.psum_scatter(partial_gram, "fsdp", scatter_dimension=0, tiled=True)[0]
        input_gram = lax.dot_general(
            activations, activations, (((1,), (1,)), ((), ())), preferred_element_type=jnp.float32
        )
        labels = group_ids[0]
        same = labels[:, None] == labels[None, :]
        row_terms = jnp.sum(jnp.where(same, input_gram * cotan_gram, 0.0), axis=1)
        squared = jnp.sum(jnp.where(same, row_terms[None, :], 0.0), axis=1)
        factor = clip / jnp.maximum(jnp.sqrt(squared), clip)
        factors = lax.all_gather(factor, "fsdp", axis=0, tiled=False)

        lags = (step_value - slot_ids - 1) % BAND + 1
        columns = jnp.arange(BAND, dtype=jnp.int32)
        lag_weight = jnp.sum(
            jnp.where(columns[None, :] == lags[:, None], band_coefs[None, :], 0.0), axis=1
        )
        noise_scale = noise_mult[0] * clip

        act4 = activations.reshape(tok, n_dp, chunks, width)
        hist5 = history.reshape(history.shape[0], out_local, n_dp, chunks, width)

        def partial(block, src):
            src = jnp.clip(src, 0, n_fsdp - 1)
            fac = lax.dynamic_index_in_dim(factors, src, axis=0, keepdims=False)
            scaled = (block.astype(jnp.float32) * fac[:, None, None]).astype(jnp.bfloat16)
            cot = lax.dynamic_slice_in_dim(cotangents, src * tok, tok, axis=0)
            return jnp.einsum("to,tdw->dow", cot, scaled, preferred_element_type=jnp.float32)

        reduced = []
        for c in range(chunks):
            own = act4[:, :, c, :]
            acc = partial(own, me)
            right_msg = own
            left_msg = own
            for k in range(1, n_fsdp):
                right_msg = lax.ppermute(
                    right_msg, "fsdp", [(f, f + 1) for f in range(k - 1, n_fsdp - 1)]
                )
                left_msg = lax.ppermute(
                    left_msg, "fsdp", [(f, f - 1) for f in range(1, n_fsdp - k + 1)]
                )
                acc = acc + partial(right_msg, me - k) + partial(left_msg, me + k)
            hist_c = hist5[:, :, :, c, :]
            history_part = jnp.zeros(hist_c.shape[1:], jnp.float32)
            for position in range(hist_c.shape[0]):
                history_part = history_part + lag_weight[position] * hist_c[position].astype(jnp.float32)
            payload = acc + noise_scale * jnp.transpose(history_part, (1, 0, 2))
            reduced.append(lax.psum_scatter(payload, "dp", scatter_dimension=0, tiled=True)[0])
        combined = jnp.concatenate(reduced, axis=1)

        full_fresh = lax.all_gather(fresh_noise, "dp", axis=1, tiled=True)
        new_history = jnp.where((slot_ids == target)[:, None, None], full_fresh[None], history)

        examples = EX_DEV * n_dp * n_fsdp
        noisy_mean = (
            combined + noise_scale * band_coefs[0] * fresh_noise.astype(jnp.float32)
        ) / examples
        new_first = 0.9 * first_moment + 0.1 * noisy_mean
        new_second = 0.999 * second_moment + 0.001 * noisy_mean * noisy_mean
        step_float = step_value.astype(jnp.float32)
        corrected_first = new_first / (1.0 - jnp.power(jnp.float32(0.9), step_float))
        corrected_second = new_second / (1.0 - jnp.power(jnp.float32(0.999), step_float))
        new_weights = weights - 0.002 * corrected_first / (jnp.sqrt(corrected_second) + 1e-08)
        gathered_weights = lax.all_gather(new_weights, "dp", axis=1, tiled=True)
        return (new_weights, new_first, new_second, noisy_mean, gathered_weights, new_history)

    return body


def solution(mesh):
    n_dp = mesh.shape["dp"]
    n_fsdp = mesh.shape["fsdp"]
    cols = D_IN // n_dp
    chunks = max(1, min(4, cols // 128))
    in_specs = (
        P(("dp", "fsdp"), None),
        P("dp", "fsdp"),
        P(("dp", "fsdp"), None),
        P("fsdp", "dp"),
        P("fsdp", "dp"),
        P("fsdp", "dp"),
        P("fsdp", "dp"),
        P("dp", "fsdp", None),
        P("dp"),
        P(),
        P(),
        P(),
    )
    out_specs = (
        P("fsdp", "dp"),
        P("fsdp", "dp"),
        P("fsdp", "dp"),
        P("fsdp", "dp"),
        P("fsdp", None),
        P("dp", "fsdp", None),
    )
    return jax.shard_map(
        make_body(n_dp, n_fsdp, chunks),
        mesh=mesh,
        in_specs=in_specs,
        out_specs=out_specs,
        check_vma=False,
    )
```

time: 507 us -> 511 us (level)
  waiting for transfers between devices: 360 us -> 243 us
  matrix products: 27.7 us -> 81.3 us
  starting transfers between devices: 0.38 us -> 38.5 us
  blocking collectives: 0 us -> 17.5 us
  local copies, waits for them, and re-layouts: 75.7 us -> 89.2 us
    all_gather x1 -> x0, waiting for transfers between devices: 110 us -> none  [body(): lax.all_gather(scaled, 'fsdp', axis=0, tiled=True)]
    ppermute x0 -> x24, waiting for transfers between devices: none -> 88.6 us  [the longest x12 54.6 us: body(): lax.ppermute(left_msg, 'fsdp', [(f, f - 1) for f in range(1, n_fsdp - k +...]
    reduce_scatter x1 -> x4, waiting for transfers between devices: 103 us -> 38.9 us  [body(): lax.psum_scatter(payload, 'dp', scatter_dimension=0, tiled=True)[0]]
    dot_general x1 -> x28, matrix products: 22.8 us -> 76.6 us  [partial(): jnp.einsum('to,tdw->dow', cot, scaled, preferred_element_type=jnp.float32)]
    ppermute x0 -> x24, starting transfers between devices: none -> 38.2 us  [the longest x12 22.4 us: body(): lax.ppermute(right_msg, 'fsdp', [(f, f + 1) for f in range(k - 1, n_fsdp...]
    reduce_scatter x1, waiting for transfers between devices: 30.3 us -> 0.02 us  [body(): lax.psum_scatter(partial_gram, 'fsdp', scatter_dimension=0, tiled=True)[0]]
    all_gather x0 -> x1, blocking collectives: none -> 17.5 us  [body(): factors = lax.all_gather(factor, 'fsdp', axis=0, tiled=False)]
    unnamed x31 -> x28, local copies, waits for them, and re-layouts: 62.9 us -> 75.4 us
  transfers between devices with their start and end apart: 5 -> 31, of which waited for: 5 -> 17; matrix products, arithmetic and copies ran while one was open for 16% -> 32% of each run, Pallas kernels for 0% -> 0%
where the time goes in v1:
time: 511 us; the launch traced here: 509 us
  waiting for transfers between devices  243 us (48%)
  local copies, waits for them, and re-layouts  89.2 us (17%)
  matrix products  81.3 us (16%)
  starting transfers between devices  38.5 us (8%)
  other arithmetic  23.3 us (5%)
  blocking collectives  17.5 us (3%)
  between operations  16 us (3%)
    dot_general x28, matrix products, partial(): jnp.einsum('to,tdw->dow', cot, scaled, preferred_element_type=jnp.float32)  76.6 us
    all_gather x1, waiting for transfers between devices, body(): gathered_weights = lax.all_gather(new_weights, 'dp', axis=1, tiled=True)  75.4 us
    unnamed x28, local copies, waits for them, and re-layouts  75.4 us
    ppermute x12, waiting for transfers between devices, body(): lax.ppermute(left_msg, 'fsdp', [(f, f - 1) for f in range(1, n_fsdp - k +...  54.6 us
    all_gather x1, waiting for transfers between devices, body(): full_fresh = lax.all_gather(fresh_noise, 'dp', axis=1, tiled=True)  39.7 us
    reduce_scatter x4, waiting for transfers between devices, body(): lax.psum_scatter(payload, 'dp', scatter_dimension=0, tiled=True)[0]  38.9 us
    ppermute x12, waiting for transfers between devices, body(): lax.ppermute(right_msg, 'fsdp', [(f, f + 1) for f in range(k - 1, n_fsdp...  34 us
    ppermute x12, starting transfers between devices, body(): lax.ppermute(right_msg, 'fsdp', [(f, f + 1) for f in range(k - 1, n_fsdp...  22.4 us
  transfers between devices with their start and end apart: 31, of which 17 were waited for; matrix products, arithmetic and copies ran while one was open for 32% of the time, Pallas kernels for 0%

profile of v1, /device:TPU:0, one launch (start us, length us, event | category | flops | bytes accessed | tf_op | source)
XLA Modules:
  0.0 509.1 jit_solution(526049879207980190)
XLA Ops:
  7.2 1.5 copy-done
  8.8 1.7 fusion.152
  10.5 4.4 reshape.113
  15.0 8.8 %fusion.150 = (bf16[256,8,1,128]{3,2,1,0:T(2,128)(2,1)}, bf16[256,8,1,128]{3,2,1,0:T(2,128)(2,1)}, bf16[256,8,1,128]{3,2,1,0:T(2,128)(2,1)}, bf16[256,8,1,128]{3,2,1,0:T(2,128)(2,1)S(1)}) fusion(bf16[256,8,4,128]{3,2,1,0:T(4,128)(2,1)} %reshape.113), kind=kLoop, calls=%fused_computation.211 | loop fusion | bytes 4194304 | tf_op jit(solution)/shard_map/slice | solution.py:74
  23.7 3.5 copy.102
  27.2 5.8 %collective-permute-start = (bf16[256,8,128]{0,2,1:T(8,128)(2,1)}, bf16[256,8,128]{0,2,1:T(8,128)(2,1)}, u32[]{:S(2)}, u32[]{:S(2)}) collective-permute-start(bf16[256,8,128]{0,2,1:T(8,128)(2,1)} %bitcast.176), channel_id=1, source_target_pairs={{0,1},{1,2},{2,3},{4,5},{5,6},{6,7},{8,9},{9,10},{10,11},{12,13},{... | collective-permute-start | bytes 1572872 | tf_op jit(solution)/shard_map/ppermute | solution.py:79
  34.3 13.5 %collective-permute-done = bf16[256,8,128]{0,2,1:T(8,128)(2,1)} collective-permute-done((bf16[256,8,128]{0,2,1:T(8,128)(2,1)}, bf16[256,8,128]{0,2,1:T(8,128)(2,1)}, u32[]{:S(2)}, u32[]{:S(2)}) %collective-permute-start) | collective-permute-done | bytes 524320 | tf_op jit(solution)/shard_map/ppermute | solution.py:79
  47.7 1.5 collective-permute-start.2
  52.6 21.2 %copy.81 = bf16[2,1024,4096]{1,2,0:T(8,128)(2,1)} copy(bf16[2,1024,4096]{2,1,0:T(8,128)(2,1)} %param.19) | data formatting | bytes 33554432 | tf_op args[7]
  74.6 1.5 collective-permute-start.4
  77.5 3.0 fusion.1
  80.7 17.5 %all-gather.1 = f32[4,1,256]{2,1,0:T(1,128)S(1)} all-gather(f32[1,1,256]{2,1,0:T(1,128)S(1)} %bitcast.216), channel_id=2, replica_groups=mesh['dp'=8,'fsdp'=4] {'fsdp'}, dimensions={0}, use_global_device_ids=true | all-gather | bytes 5120 | tf_op jit(solution)/shard_map/all_gather | solution.py:53
  98.9 1.8 fusion.5
  100.7 1.8 fusion.6
  102.5 1.8 fusion.3
  104.2 3.7 fusion.4
  107.9 3.8 fusion.7
  111.7 8.9 %bitcast_add_fusion.3 = f32[8,1024,128]{1,2,0:T(8,128)} fusion(f32[8,128,1024]{2,1,0:T(8,128)} %fusion.7, f32[8,128,1024]{2,1,0:T(8,128)S(1)} %fusion.6, f32[8,128,1024]{2,1,0:T(8,128)S(1)} %fusion.5, f32[8,128,1024]{2,1,0:T(8,128)} %fusion.4, f32[8,128,1024]{2,1,0:T(8,128)S(1)} %fusion.2, f32[8,128,1024]{2,1,0:T(8,128)S(1)} %fusion.3, ...), kind=kOutput, calls=%fused_computation.4 | convolution fusion | flops 551288832 | bytes 34604048 | tf_op jit(solution)/shard_map/to,tdw->dow/dot_general | solution.py:70
  120.7 3.5 copy.105
  124.1 2.0 collective-permute-start.6
  126.2 1.3 collective-permute-start.7
  127.5 8.6 %collective-permute-done.6 = bf16[256,8,128]{0,2,1:T(8,128)(2,1)S(1)} collective-permute-done((bf16[256,8,128]{0,2,1:T(8,128)(2,1)}, bf16[256,8,128]{0,2,1:T(8,128)(2,1)S(1)}, u32[]{:S(2)}, u32[]{:S(2)}) %collective-permute-start.6) | collective-permute-done | bytes 524320 | tf_op jit(solution)/shard_map/ppermute | solution.py:79
  136.7 3.3 collective-permute-done.7
  142.1 10.8 %collective-permute-done.9 = bf16[256,8,128]{0,2,1:T(8,128)(2,1)S(1)} collective-permute-done((bf16[256,8,128]{0,2,1:T(8,128)(2,1)S(1)}, bf16[256,8,128]{0,2,1:T(8,128)(2,1)S(1)}, u32[]{:S(2)}, u32[]{:S(2)}) %collective-permute-start.9) | collective-permute-done | bytes 524320 | tf_op jit(solution)/shard_map/ppermute | solution.py:82
  152.9 1.5 collective-permute-start.11
  154.4 1.8 fusion.9
  158.3 2.7 fusion.11
  161.0 2.7 fusion.14
  165.0 8.8 %bitcast_add_fusion.2 = f32[8,1024,128]{1,2,0:T(8,128)} fusion(f32[8,128,1024]{2,1,0:T(8,128)} %fusion.14, f32[8,128,1024]{2,1,0:T(8,128)S(1)} %fusion.13, f32[8,128,1024]{2,1,0:T(8,128)S(1)} %fusion.12, f32[8,128,1024]{2,1,0:T(8,128)} %fusion.11, f32[8,128,1024]{2,1,0:T(8,128)S(1)} %fusion.9, f32[8,128,1024]{2,1,0:T(8,128)S(1)} %fusion.10, ...), kind=kOutput, calls=%fused_computation.3 | convolution fusion | flops 551288832 | bytes 34604048 | tf_op jit(solution)/shard_map/to,tdw->dow/dot_general | solution.py:70
  173.8 3.5 copy.108
  177.3 3.3 collective-permute-start.12
  180.6 1.3 collective-permute-start.13
  181.9 6.3 %collective-permute-done.12 = bf16[256,8,128]{0,2,1:T(8,128)(2,1)S(1)} collective-permute-done((bf16[256,8,128]{0,2,1:T(8,128)(2,1)}, bf16[256,8,128]{0,2,1:T(8,128)(2,1)S(1)}, u32[]{:S(2)}, u32[]{:S(2)}) %collective-permute-start.12) | collective-permute-done | bytes 524320 | tf_op jit(solution)/shard_map/ppermute | solution.py:79
  188.9 4.0 collective-permute-done.13
  194.9 10.9 %collective-permute-done.15 = bf16[256,8,128]{0,2,1:T(8,128)(2,1)S(1)} collective-permute-done((bf16[256,8,128]{0,2,1:T(8,128)(2,1)S(1)}, bf16[256,8,128]{0,2,1:T(8,128)(2,1)S(1)}, u32[]{:S(2)}, u32[]{:S(2)}) %collective-permute-start.15) | collective-permute-done | bytes 524320 | tf_op jit(solution)/shard_map/ppermute | solution.py:82
  207.1 1.8 fusion.16
  211.1 2.7 fusion.18
  213.8 2.7 fusion.21
  216.9 8.7 %bitcast_add_fusion.1 = f32[8,1024,128]{1,2,0:T(8,128)} fusion(f32[8,128,1024]{2,1,0:T(8,128)} %fusion.21, f32[8,128,1024]{2,1,0:T(8,128)S(1)} %fusion.20, f32[8,128,1024]{2,1,0:T(8,128)S(1)} %fusion.19, f32[8,128,1024]{2,1,0:T(8,128)} %fusion.18, f32[8,128,1024]{2,1,0:T(8,128)S(1)} %fusion.16, f32[8,128,1024]{2,1,0:T(8,128)S(1)} %fusion.17, ...), kind=kOutput, calls=%fused_computation.2 | convolution fusion | flops 551288832 | bytes 34604048 | tf_op jit(solution)/shard_map/to,tdw->dow/dot_general | solution.py:70
  225.7 2.0 copy.111
  227.7 4.2 collective-permute-start.18
  231.9 1.3 collective-permute-start.19
  233.2 5.7 %collective-permute-done.18 = bf16[256,8,128]{0,2,1:T(8,128)(2,1)S(1)} collective-permute-done((bf16[256,8,128]{0,2,1:T(8,128)(2,1)}, bf16[256,8,128]{0,2,1:T(8,128)(2,1)S(1)}, u32[]{:S(2)}, u32[]{:S(2)}) %collective-permute-start.18) | collective-permute-done | bytes 524320 | tf_op jit(solution)/shard_map/ppermute | solution.py:79
  239.6 9.1 %collective-permute-done.19 = bf16[256,8,128]{0,2,1:T(8,128)(2,1)S(1)} collective-permute-done((bf16[256,8,128]{0,2,1:T(8,128)(2,1)}, bf16[256,8,128]{0,2,1:T(8,128)(2,1)S(1)}, u32[]{:S(2)}, u32[]{:S(2)}) %collective-permute-start.19) | collective-permute-done | bytes 524320 | tf_op jit(solution)/shard_map/ppermute | solution.py:82
  250.7 13.8 %collective-permute-done.21 = bf16[256,8,128]{0,2,1:T(8,128)(2,1)S(1)} collective-permute-done((bf16[256,8,128]{0,2,1:T(8,128)(2,1)S(1)}, bf16[256,8,128]{0,2,1:T(8,128)(2,1)S(1)}, u32[]{:S(2)}, u32[]{:S(2)}) %collective-permute-start.21) | collective-permute-done | bytes 524320 | tf_op jit(solution)/shard_map/ppermute | solution.py:82
  264.5 1.5 collective-permute-start.23
  266.1 1.8 fusion.23
  270.0 2.7 fusion.25
  272.7 2.7 fusion.28
  275.6 8.7 %bitcast_add_fusion = f32[8,1024,128]{1,2,0:T(8,128)} fusion(f32[8,128,1024]{2,1,0:T(8,128)} %fusion.28, f32[8,128,1024]{2,1,0:T(8,128)S(1)} %fusion.27, f32[8,128,1024]{2,1,0:T(8,128)S(1)} %fusion.26, f32[8,128,1024]{2,1,0:T(8,128)} %fusion.25, f32[8,128,1024]{2,1,0:T(8,128)S(1)} %fusion.23, f32[8,128,1024]{2,1,0:T(8,128)S(1)} %fusion.24, ...), kind=kOutput, calls=%fused_computation.1 | convolution fusion | flops 551288832 | bytes 34604048 | tf_op jit(solution)/shard_map/to,tdw->dow/dot_general | solution.py:70
  285.5 1.3 copy.93
  286.9 2.9 copy.78
  289.8 3.2 copy.94
  293.0 3.1 copy.95
  296.1 38.8 %reduce-scatter.14.cloned.1.call-done = f32[1,1024,128]{1,2,0:T(8,128)} async-done(((f32[8,1024,128]{1,2,0:T(8,128)}), f32[1,1024,128]{1,2,0:T(8,128)}) %reduce-scatter.14.cloned.1.call-update) | async-done | bytes 524304 | tf_op jit(solution)/shard_map/reduce_scatter | solution.py:91
  334.9 6.2 %divide_subtract_fusion = (f32[1024,512]{0,1:T(8,128)}, f32[1024,512]{0,1:T(8,128)}, f32[1024,512]{0,1:T(8,128)}, f32[1024,512]{0,1:T(8,128)}) fusion(f32[1024,512]{0,1:T(8,128)} %copy.95, f32[]{:T(128)S(6)} %sub.43, f32[]{:T(128)S(6)} %sub.42, bf16[1024,512]{0,1:T(8,128)(2,1)S(1)} %copy-done.2, f32[]{:T(128)S(6)} %mul.452, f32[1024,128]{0,1:T(8,128)} %bitcast.187, ...), kind=kLoop, calls=%fused_computation.14 | loop fusion | flops 10485760 | bytes 17825804 | tf_op jit(solution)/shard_map/sub | solution.py:106
  341.1 2.9 copy.96
  344.0 3.0 copy.97
  347.1 2.9 copy.98
  350.0 2.9 copy.99
  352.9 39.7 %all-gather.7.cloned.1.call-done = bf16[1024,4096]{1,0:T(8,128)(2,1)} async-done(((bf16[1024,512]{1,0:T(8,128)(2,1)}), bf16[1024,4096]{1,0:T(8,128)(2,1)}) %all-gather.7.cloned.1.call-update) | async-done | bytes 8388624 | tf_op jit(solution)/shard_map/all_gather | solution.py:94
  392.6 16.8 %broadcast_select_fusion = bf16[2,1024,4096]{2,1,0:T(8,128)(2,1)} fusion(bf16[2,1024,4096]{2,1,0:T(8,128)(2,1)} %param.19, pred[2]{0:T(512)(128)(4,1)S(1)} %broadcast_compare_fusion, bf16[1024,4096]{1,0:T(8,128)(2,1)} %all-gather.7.cloned.1.call-done), kind=kLoop, calls=%fused_computation | loop fusion | flops 8388608 | bytes 41943040 | tf_op jit(solution)/shard_map/jit(_where)/select_n | solution.py:95
  409.4 75.4 %all-gather.5.cloned.1.call-done = f32[1024,4096]{0,1:T(8,128)} async-done(((f32[1024,512]{0,1:T(8,128)}), f32[1024,4096]{0,1:T(8,128)}) %all-gather.5.cloned.1.call-update) | async-done | bytes 16777232 | tf_op jit(solution)/shard_map/all_gather | solution.py:107
  484.8 17.4 %copy.100 = f32[1024,4096]{1,0:T(8,128)} copy(f32[1024,4096]{0,1:T(8,128)} %all-gather.5.cloned.1.call-done) | data formatting | bytes 33554432
  (75 shorter events, 25.4 us)
Async XLA Ops:
  7.2 1.6 copy-start
  7.2 70.2 %reduce-scatter.6.cloned.1.call-start = ((), (), s32[]{:S(2)}) async-start(), calls=%async_computation.5 | async-start | bytes 1310720 | tf_op jit(solution)/shard_map/reduce_scatter | solution.py:44
  10.5 285.6 %reduce-scatter.8.cloned.1.call-start = ((), (), s32[]{:S(2)}) async-start(), calls=%async_computation.6 | async-start | bytes 4718592 | tf_op jit(solution)/shard_map/reduce_scatter | solution.py:91
  27.2 20.5 %collective-permute-start = (bf16[256,8,128]{0,2,1:T(8,128)(2,1)}, bf16[256,8,128]{0,2,1:T(8,128)(2,1)}, u32[]{:S(2)}, u32[]{:S(2)}) collective-permute-start(bf16[256,8,128]{0,2,1:T(8,128)(2,1)} %bitcast.176), channel_id=1, source_target_pairs={{0,1},{1,2},{2,3},{4,5},{5,6},{6,7},{8,9},{9,10},{10,11},{12,13},{... | collective-permute-start | bytes 1572872 | tf_op jit(solution)/shard_map/ppermute | solution.py:79
  33.0 16.9 %collective-permute-start.1 = (bf16[256,8,128]{0,2,1:T(8,128)(2,1)}, bf16[256,8,128]{0,2,1:T(8,128)(2,1)}, u32[]{:S(2)}, u32[]{:S(2)}) collective-permute-start(bf16[256,8,128]{0,2,1:T(8,128)(2,1)} %bitcast.177), channel_id=1, source_target_pairs={{1,0},{2,1},{3,2},{5,4},{6,5},{7,6},{9,8},{10,9},{11,10},{13,12},{... | collective-permute-start | bytes 1572872 | tf_op jit(solution)/shard_map/ppermute | solution.py:82
  47.7 26.9 %collective-permute-start.2 = (bf16[256,8,128]{0,2,1:T(8,128)(2,1)}, bf16[256,8,128]{0,2,1:T(8,128)(2,1)}, u32[]{:S(2)}, u32[]{:S(2)}) collective-permute-start(bf16[256,8,128]{0,2,1:T(8,128)(2,1)} %collective-permute-done), channel_id=1, source_target_pairs={{1,2},{2,3},{5,6},{6,7},{9,10},{10,11},{13,14},{14,15},{17,18},{18... | collective-permute-start | bytes 1572872 | tf_op jit(solution)/shard_map/ppermute | solution.py:79
  49.9 26.2 %collective-permute-start.3 = (bf16[256,8,128]{0,2,1:T(8,128)(2,1)}, bf16[256,8,128]{0,2,1:T(8,128)(2,1)}, u32[]{:S(2)}, u32[]{:S(2)}) collective-permute-start(bf16[256,8,128]{0,2,1:T(8,128)(2,1)} %collective-permute-done.1), channel_id=1, source_target_pairs={{1,0},{2,1},{5,4},{6,5},{9,8},{10,9},{13,12},{14,13},{17,16},{18,1... | collective-permute-start | bytes 1572872 | tf_op jit(solution)/shard_map/ppermute | solution.py:82
  52.5 21.2 %copy-start.6 = (s32[2]{0:T(128)S(1)}, s32[2]{0:T(128)}, u32[]{:S(2)}) copy-start(s32[2]{0:T(128)} %param.20) | copy-start | bytes 28
  52.5 21.2 %copy-start.5 = (f32[16]{0:T(128)S(1)}, f32[16]{0:T(128)}, u32[]{:S(2)}) copy-start(f32[16]{0:T(128)} %param.21) | copy-start | bytes 196
  52.6 24.9 %copy-start.4 = (s32[1,256]{1,0:T(1,128)S(1)}, s32[1,256]{1,0:T(1,128)}, u32[]{:S(2)}) copy-start(s32[1,256]{1,0:T(1,128)} %param.14) | copy-start | bytes 3076
  74.6 33.3 %collective-permute-start.4 = (bf16[256,8,128]{0,2,1:T(8,128)(2,1)}, bf16[256,8,128]{0,2,1:T(8,128)(2,1)}, u32[]{:S(2)}, u32[]{:S(2)}) collective-permute-start(bf16[256,8,128]{0,2,1:T(8,128)(2,1)} %collective-permute-done.2), channel_id=1, source_target_pairs={{2,3},{6,7},{10,11},{14,15},{18,19},{22,23},{26,27},{30,31}} | collective-permute-start | bytes 1572872 | tf_op jit(solution)/shard_map/ppermute | solution.py:79
  76.1 35.6 %collective-permute-start.5 = (bf16[256,8,128]{0,2,1:T(8,128)(2,1)}, bf16[256,8,128]{0,2,1:T(8,128)(2,1)}, u32[]{:S(2)}, u32[]{:S(2)}) collective-permute-start(bf16[256,8,128]{0,2,1:T(8,128)(2,1)} %collective-permute-done.3), channel_id=1, source_target_pairs={{1,0},{5,4},{9,8},{13,12},{17,16},{21,20},{25,24},{29,28}} | collective-permute-start | bytes 1572872 | tf_op jit(solution)/shard_map/ppermute | solution.py:82
  77.4 20.8 %copy-start.3 = (bf16[256,8,1,128]{0,3,1,2:T(8,128)(2,1)S(1)}, bf16[256,8,1,128]{0,3,1,2:T(8,128)(2,1)}, u32[]{:S(2)}) copy-start(bf16[256,8,1,128]{0,3,1,2:T(8,128)(2,1)} %copy.102) | copy-start | bytes 1572868
  120.6 175.5 %reduce-scatter.10.cloned.1.call-start = ((), (), s32[]{:S(2)}) async-start(), calls=%async_computation.7 | async-start | bytes 4718592 | tf_op jit(solution)/shard_map/reduce_scatter | solution.py:91
  124.1 11.9 %collective-permute-start.6 = (bf16[256,8,128]{0,2,1:T(8,128)(2,1)}, bf16[256,8,128]{0,2,1:T(8,128)(2,1)S(1)}, u32[]{:S(2)}, u32[]{:S(2)}) collective-permute-start(bf16[256,8,128]{0,2,1:T(8,128)(2,1)} %bitcast.180), channel_id=1, source_target_pairs={{0,1},{1,2},{2,3},{4,5},{5,6},{6,7},{8,9},{9,10},{10,11},{12,13},{... | collective-permute-start | bytes 1572872 | tf_op jit(solution)/shard_map/ppermute | solution.py:79
  126.2 13.9 %collective-permute-start.7 = (bf16[256,8,128]{0,2,1:T(8,128)(2,1)}, bf16[256,8,128]{0,2,1:T(8,128)(2,1)S(1)}, u32[]{:S(2)}, u32[]{:S(2)}) collective-permute-start(bf16[256,8,128]{0,2,1:T(8,128)(2,1)} %bitcast.181), channel_id=1, source_target_pairs={{1,0},{2,1},{3,2},{5,4},{6,5},{7,6},{9,8},{10,9},{11,10},{13,12},{... | collective-permute-start | bytes 1572872 | tf_op jit(solution)/shard_map/ppermute | solution.py:82
  136.0 5.3 %collective-permute-start.8 = (bf16[256,8,128]{0,2,1:T(8,128)(2,1)S(1)}, bf16[256,8,128]{0,2,1:T(8,128)(2,1)S(1)}, u32[]{:S(2)}, u32[]{:S(2)}) collective-permute-start(bf16[256,8,128]{0,2,1:T(8,128)(2,1)S(1)} %collective-permute-done.6), channel_id=1, source_target_pairs={{1,2},{2,3},{5,6},{6,7},{9,10},{10,11},{13,14},{14,15},{17,18},{18... | collective-permute-start | bytes 1572872 | tf_op jit(solution)/shard_map/ppermute | solution.py:79
  140.1 12.8 %collective-permute-start.9 = (bf16[256,8,128]{0,2,1:T(8,128)(2,1)S(1)}, bf16[256,8,128]{0,2,1:T(8,128)(2,1)S(1)}, u32[]{:S(2)}, u32[]{:S(2)}) collective-permute-start(bf16[256,8,128]{0,2,1:T(8,128)(2,1)S(1)} %collective-permute-done.7), channel_id=1, source_target_pairs={{1,0},{2,1},{5,4},{6,5},{9,8},{10,9},{13,12},{14,13},{17,16},{18,1... | collective-permute-start | bytes 1572872 | tf_op jit(solution)/shard_map/ppermute | solution.py:82
  141.4 19.6 %collective-permute-start.10 = (bf16[256,8,128]{0,2,1:T(8,128)(2,1)S(1)}, bf16[256,8,128]{0,2,1:T(8,128)(2,1)S(1)}, u32[]{:S(2)}, u32[]{:S(2)}) collective-permute-start(bf16[256,8,128]{0,2,1:T(8,128)(2,1)S(1)} %collective-permute-done.8), channel_id=1, source_target_pairs={{2,3},{6,7},{10,11},{14,15},{18,19},{22,23},{26,27},{30,31}} | collective-permute-start | bytes 1572872 | tf_op jit(solution)/shard_map/ppermute | solution.py:79
  152.9 12.1 %collective-permute-start.11 = (bf16[256,8,128]{0,2,1:T(8,128)(2,1)S(1)}, bf16[256,8,128]{0,2,1:T(8,128)(2,1)S(1)}, u32[]{:S(2)}, u32[]{:S(2)}) collective-permute-start(bf16[256,8,128]{0,2,1:T(8,128)(2,1)S(1)} %collective-permute-done.9), channel_id=1, source_target_pairs={{1,0},{5,4},{9,8},{13,12},{17,16},{21,20},{25,24},{29,28}} | collective-permute-start | bytes 1572872 | tf_op jit(solution)/shard_map/ppermute | solution.py:82
  173.8 122.3 %reduce-scatter.12.cloned.1.call-start = ((), (), s32[]{:S(2)}) async-start(), calls=%async_computation.8 | async-start | bytes 4718592 | tf_op jit(solution)/shard_map/reduce_scatter | solution.py:91
  177.3 10.9 %collective-permute-start.12 = (bf16[256,8,128]{0,2,1:T(8,128)(2,1)}, bf16[256,8,128]{0,2,1:T(8,128)(2,1)S(1)}, u32[]{:S(2)}, u32[]{:S(2)}) collective-permute-start(bf16[256,8,128]{0,2,1:T(8,128)(2,1)} %bitcast.182), channel_id=1, source_target_pairs={{0,1},{1,2},{2,3},{4,5},{5,6},{6,7},{8,9},{9,10},{10,11},{12,13},{... | collective-permute-start | bytes 1572872 | tf_op jit(solution)/shard_map/ppermute | solution.py:79
  180.6 12.3 %collective-permute-start.13 = (bf16[256,8,128]{0,2,1:T(8,128)(2,1)}, bf16[256,8,128]{0,2,1:T(8,128)(2,1)S(1)}, u32[]{:S(2)}, u32[]{:S(2)}) collective-permute-start(bf16[256,8,128]{0,2,1:T(8,128)(2,1)} %bitcast.183), channel_id=1, source_target_pairs={{1,0},{2,1},{3,2},{5,4},{6,5},{7,6},{9,8},{10,9},{11,10},{13,12},{... | collective-permute-start | bytes 1572872 | tf_op jit(solution)/shard_map/ppermute | solution.py:82
  188.2 6.0 %collective-permute-start.14 = (bf16[256,8,128]{0,2,1:T(8,128)(2,1)S(1)}, bf16[256,8,128]{0,2,1:T(8,128)(2,1)S(1)}, u32[]{:S(2)}, u32[]{:S(2)}) collective-permute-start(bf16[256,8,128]{0,2,1:T(8,128)(2,1)S(1)} %collective-permute-done.12), channel_id=1, source_target_pairs={{1,2},{2,3},{5,6},{6,7},{9,10},{10,11},{13,14},{14,15},{17,18},{18... | collective-permute-start | bytes 1572872 | tf_op jit(solution)/shard_map/ppermute | solution.py:79
  192.9 12.9 %collective-permute-start.15 = (bf16[256,8,128]{0,2,1:T(8,128)(2,1)S(1)}, bf16[256,8,128]{0,2,1:T(8,128)(2,1)S(1)}, u32[]{:S(2)}, u32[]{:S(2)}) collective-permute-start(bf16[256,8,128]{0,2,1:T(8,128)(2,1)S(1)} %collective-permute-done.13), channel_id=1, source_target_pairs={{1,0},{2,1},{5,4},{6,5},{9,8},{10,9},{13,12},{14,13},{17,16},{18,1... | collective-permute-start | bytes 1572872 | tf_op jit(solution)/shard_map/ppermute | solution.py:82
  194.2 19.6 %collective-permute-start.16 = (bf16[256,8,128]{0,2,1:T(8,128)(2,1)S(1)}, bf16[256,8,128]{0,2,1:T(8,128)(2,1)S(1)}, u32[]{:S(2)}, u32[]{:S(2)}) collective-permute-start(bf16[256,8,128]{0,2,1:T(8,128)(2,1)S(1)} %collective-permute-done.14), channel_id=1, source_target_pairs={{2,3},{6,7},{10,11},{14,15},{18,19},{22,23},{26,27},{30,31}} | collective-permute-start | bytes 1572872 | tf_op jit(solution)/shard_map/ppermute | solution.py:79
  205.8 11.1 %collective-permute-start.17 = (bf16[256,8,128]{0,2,1:T(8,128)(2,1)S(1)}, bf16[256,8,128]{0,2,1:T(8,128)(2,1)S(1)}, u32[]{:S(2)}, u32[]{:S(2)}) collective-permute-start(bf16[256,8,128]{0,2,1:T(8,128)(2,1)S(1)} %collective-permute-done.15), channel_id=1, source_target_pairs={{1,0},{5,4},{9,8},{13,12},{17,16},{21,20},{25,24},{29,28}} | collective-permute-start | bytes 1572872 | tf_op jit(solution)/shard_map/ppermute | solution.py:82
  225.6 109.3 %reduce-scatter.14.cloned.1.call-start = ((), (), s32[]{:S(2)}) async-start(), calls=%async_computation.9 | async-start | bytes 4718592 | tf_op jit(solution)/shard_map/reduce_scatter | solution.py:91
  227.7 11.2 %collective-permute-start.18 = (bf16[256,8,128]{0,2,1:T(8,128)(2,1)}, bf16[256,8,128]{0,2,1:T(8,128)(2,1)S(1)}, u32[]{:S(2)}, u32[]{:S(2)}) collective-permute-start(bf16[256,8,128]{0,2,1:T(8,128)(2,1)} %bitcast.178), channel_id=1, source_target_pairs={{0,1},{1,2},{2,3},{4,5},{5,6},{6,7},{8,9},{9,10},{10,11},{12,13},{... | collective-permute-start | bytes 1572872 | tf_op jit(solution)/shard_map/ppermute | solution.py:79
  231.9 16.8 %collective-permute-start.19 = (bf16[256,8,128]{0,2,1:T(8,128)(2,1)}, bf16[256,8,128]{0,2,1:T(8,128)(2,1)S(1)}, u32[]{:S(2)}, u32[]{:S(2)}) collective-permute-start(bf16[256,8,128]{0,2,1:T(8,128)(2,1)} %bitcast.179), channel_id=1, source_target_pairs={{1,0},{2,1},{3,2},{5,4},{6,5},{7,6},{9,8},{10,9},{11,10},{13,12},{... | collective-permute-start | bytes 1572872 | tf_op jit(solution)/shard_map/ppermute | solution.py:82
  238.9 11.1 %collective-permute-start.20 = (bf16[256,8,128]{0,2,1:T(8,128)(2,1)S(1)}, bf16[256,8,128]{0,2,1:T(8,128)(2,1)S(1)}, u32[]{:S(2)}, u32[]{:S(2)}) collective-permute-start(bf16[256,8,128]{0,2,1:T(8,128)(2,1)S(1)} %collective-permute-done.18), channel_id=1, source_target_pairs={{1,2},{2,3},{5,6},{6,7},{9,10},{10,11},{13,14},{14,15},{17,18},{18... | collective-permute-start | bytes 1572872 | tf_op jit(solution)/shard_map/ppermute | solution.py:79
  248.7 15.8 %collective-permute-start.21 = (bf16[256,8,128]{0,2,1:T(8,128)(2,1)S(1)}, bf16[256,8,128]{0,2,1:T(8,128)(2,1)S(1)}, u32[]{:S(2)}, u32[]{:S(2)}) collective-permute-start(bf16[256,8,128]{0,2,1:T(8,128)(2,1)S(1)} %collective-permute-done.19), channel_id=1, source_target_pairs={{1,0},{2,1},{5,4},{6,5},{9,8},{10,9},{13,12},{14,13},{17,16},{18,1... | collective-permute-start | bytes 1572872 | tf_op jit(solution)/shard_map/ppermute | solution.py:82
  250.0 22.7 %collective-permute-start.22 = (bf16[256,8,128]{0,2,1:T(8,128)(2,1)S(1)}, bf16[256,8,128]{0,2,1:T(8,128)(2,1)S(1)}, u32[]{:S(2)}, u32[]{:S(2)}) collective-permute-start(bf16[256,8,128]{0,2,1:T(8,128)(2,1)S(1)} %collective-permute-done.20), channel_id=1, source_target_pairs={{2,3},{6,7},{10,11},{14,15},{18,19},{22,23},{26,27},{30,31}} | collective-permute-start | bytes 1572872 | tf_op jit(solution)/shard_map/ppermute | solution.py:79
  264.5 11.1 %collective-permute-start.23 = (bf16[256,8,128]{0,2,1:T(8,128)(2,1)S(1)}, bf16[256,8,128]{0,2,1:T(8,128)(2,1)S(1)}, u32[]{:S(2)}, u32[]{:S(2)}) collective-permute-start(bf16[256,8,128]{0,2,1:T(8,128)(2,1)S(1)} %collective-permute-done.21), channel_id=1, source_target_pairs={{1,0},{5,4},{9,8},{13,12},{17,16},{21,20},{25,24},{29,28}} | collective-permute-start | bytes 1572872 | tf_op jit(solution)/shard_map/ppermute | solution.py:82
  284.3 1.2 copy-start.1
  284.3 108.3 %all-gather.7.cloned.1.call-start = ((), (), s32[]{:S(2)}) async-start(), calls=%async_computation.11 | async-start | bytes 9437184 | tf_op jit(solution)/shard_map/all_gather | solution.py:94
  284.9 199.9 %all-gather.5.cloned.1.call-start = ((), (), s32[]{:S(2)}) async-start(), calls=%async_computation.10 | async-start | bytes 18874368 | tf_op jit(solution)/shard_map/all_gather | solution.py:107
  289.8 45.1 %copy-start.2 = (bf16[1024,512]{0,1:T(8,128)(2,1)S(1)}, bf16[1024,512]{0,1:T(8,128)(2,1)}, u32[]{:S(2)}) copy-start(bf16[1024,512]{0,1:T(8,128)(2,1)} %copy.93) | copy-start | bytes 3145732
Sparse Core Ops, SparseCore 0:
  10.9 30.8 reduce-scatter.5
  120.7 49.2 reduce-scatter.7
  173.9 50.7 reduce-scatter.9
  227.8 51.1 reduce-scatter.11
  284.4 50.4 reduce-scatter.13
  336.7 55.8 all-gather.6
  395.0 89.7 all-gather.4

commit v2 on v1

v2 whole, which is shorter than its diff:
```python
import jax
import jax.numpy as jnp
from jax import lax
from jax.sharding import PartitionSpec as P

D_IN = 4096
D_OUT = 4096
BAND = 16
GROUP_MOST = 64
EX_DEV = 8


def clip_bound():
    return ((GROUP_MOST * GROUP_MOST / 4.0 + GROUP_MOST) * D_IN * D_OUT) ** 0.5


def make_body(n_dp, n_fsdp):
    def body(
        activations,
        cotangents,
        group_ids,
        weights,
        first_moment,
        second_moment,
        fresh_noise,
        history,
        slot_ids,
        band_coefs,
        step_number,
        noise_mult,
    ):
        clip = clip_bound()
        tok = activations.shape[0]
        out_local = cotangents.shape[1]
        step_value = step_number[0]
        target = step_value % BAND

        full_act = lax.all_gather(activations, "fsdp", axis=0, tiled=True)

        blocks = cotangents.reshape(n_fsdp, tok, out_local)
        partial_gram = jnp.einsum("ati,asi->ats", blocks, blocks, preferred_element_type=jnp.float32)
        received = lax.all_to_all(partial_gram, "fsdp", 0, 0, tiled=True)
        cotan_gram = received[0]
        for part in range(1, n_fsdp):
            cotan_gram = cotan_gram + received[part]
        input_gram = lax.dot_general(
            activations, activations, (((1,), (1,)), ((), ())), preferred_element_type=jnp.float32
        )
        labels = group_ids[0]
        same = labels[:, None] == labels[None, :]
        row_terms = jnp.sum(jnp.where(same, input_gram * cotan_gram, 0.0), axis=1)
        squared = jnp.sum(jnp.where(same, row_terms[None, :], 0.0), axis=1)
        factor = clip / jnp.maximum(jnp.sqrt(squared), clip)
        factors = lax.all_to_all(
            jnp.broadcast_to(factor[None], (n_fsdp, tok)), "fsdp", 0, 0, tiled=True
        ).reshape(n_fsdp * tok)

        fresh_parts = lax.all_to_all(
            jnp.broadcast_to(fresh_noise[None], (n_dp,) + fresh_noise.shape), "dp", 0, 0, tiled=True
        )
        full_fresh = jnp.transpose(fresh_parts, (1, 0, 2)).reshape(
            fresh_noise.shape[0], n_dp * fresh_noise.shape[1]
        )

        lags = (step_value - slot_ids - 1) % BAND + 1
        columns = jnp.arange(BAND, dtype=jnp.int32)
        lag_weight = jnp.sum(
            jnp.where(columns[None, :] == lags[:, None], band_coefs[None, :], 0.0), axis=1
        )
        history_part = jnp.zeros(history.shape[1:], jnp.float32)
        for position in range(history.shape[0]):
            history_part = history_part + lag_weight[position] * history[position].astype(jnp.float32)

        full_act, full_fresh = lax.optimization_barrier((full_act, full_fresh))
        scaled = (full_act.astype(jnp.float32) * factors[:, None]).astype(jnp.bfloat16)
        gradient = lax.dot_general(
            cotangents,
            scaled,
            (((0,), (0,)), ((), ())),
            preferred_element_type=jnp.float32,
        )
        new_history = jnp.where((slot_ids == target)[:, None, None], full_fresh[None], history)
        noise_scale = noise_mult[0] * clip
        combined = lax.psum_scatter(
            gradient + noise_scale * history_part, "dp", scatter_dimension=1, tiled=True
        )
        examples = EX_DEV * n_dp * n_fsdp
        noisy_mean = (
            combined + noise_scale * band_coefs[0] * fresh_noise.astype(jnp.float32)
        ) / examples
        new_first = 0.9 * first_moment + 0.1 * noisy_mean
        new_second = 0.999 * second_moment + 0.001 * noisy_mean * noisy_mean
        step_float = step_value.astype(jnp.float32)
        corrected_first = new_first / (1.0 - jnp.power(jnp.float32(0.9), step_float))
        corrected_second = new_second / (1.0 - jnp.power(jnp.float32(0.999), step_float))
        new_weights = weights - 0.002 * corrected_first / (jnp.sqrt(corrected_second) + 1e-08)
        gathered_weights = lax.all_gather(new_weights, "dp", axis=1, tiled=True)
        return (new_weights, new_first, new_second, noisy_mean, gathered_weights, new_history)

    return body


def solution(mesh):
    n_dp = mesh.shape["dp"]
    n_fsdp = mesh.shape["fsdp"]
    in_specs = (
        P(("dp", "fsdp"), None),
        P("dp", "fsdp"),
        P(("dp", "fsdp"), None),
        P("fsdp", "dp"),
        P("fsdp", "dp"),
        P("fsdp", "dp"),
        P("fsdp", "dp"),
        P("dp", "fsdp", None),
        P("dp"),
        P(),
        P(),
        P(),
    )
    out_specs = (
        P("fsdp", "dp"),
        P("fsdp", "dp"),
        P("fsdp", "dp"),
        P("fsdp", "dp"),
        P("fsdp", None),
        P("dp", "fsdp", None),
    )
    return jax.shard_map(
        make_body(n_dp, n_fsdp),
        mesh=mesh,
        in_specs=in_specs,
        out_specs=out_specs,
        check_vma=False,
    )
```

time: 511 us -> 473 us (0.926)
  matrix products: 81.3 us -> 25 us
  blocking collectives: 17.5 us -> 58.2 us
  starting transfers between devices: 38.5 us -> 8.72 us
  local copies, waits for them, and re-layouts: 89.2 us -> 102 us
    ppermute x24 -> x0, waiting for transfers between devices: 88.6 us -> none  [the longest x12 54.6 us: body(): lax.ppermute(left_msg, 'fsdp', [(f, f - 1) for f in range(1, n_fsdp - k +...]
    all_to_all x0 -> x2, waiting for transfers between devices: none -> 78.8 us  [the longest x1 78.8 us: body(): lax.all_to_all(jnp.broadcast_to(fresh_noise[None], (n_dp,) + fresh_noise....]
    reduce_scatter x5 -> x1, waiting for transfers between devices: 38.9 us -> 106 us  [body(): lax.psum_scatter(gradient + noise_scale * history_part, 'dp', scatter_dim...]
    all_to_all x0 -> x1, blocking collectives: none -> 58.2 us  [body(): received = lax.all_to_all(partial_gram, 'fsdp', 0, 0, tiled=True)]
    dot_general x28 -> x1, matrix products: 76.6 us -> 22.3 us  [body(): lax.dot_general(cotangents, scaled, (((0,), (0,)), ((), ())), preferred_e...]
    all_gather x1, waiting for transfers between devices: 39.7 us -> 0.01 us  [body(): full_act = lax.all_gather(activations, 'fsdp', axis=0, tiled=True)]
    ppermute x24 -> x0, starting transfers between devices: 38.2 us -> none  [the longest x12 22.4 us: body(): lax.ppermute(right_msg, 'fsdp', [(f, f + 1) for f in range(k - 1, n_fsdp...]
    all_gather x1, waiting for transfers between devices: 75.4 us -> 52.4 us  [body(): gathered_weights = lax.all_gather(new_weights, 'dp', axis=1, tiled=True)]
  transfers between devices with their start and end apart: 31 -> 5, of which waited for: 17 -> 3; matrix products, arithmetic and copies ran while one was open for 32% -> 22% of each run, Pallas kernels for 0% -> 0%
where the time goes in v2:
time: 473 us; the launch traced here: 471 us
  waiting for transfers between devices  238 us (50%)
  local copies, waits for them, and re-layouts  102 us (22%)
  blocking collectives  58.2 us (12%)
  matrix products  25 us (5%)
  other arithmetic  23.9 us (5%)
  between operations  15.3 us (3%)
  starting transfers between devices  8.72 us (2%)
    reduce_scatter x1, waiting for transfers between devices, body(): lax.psum_scatter(gradient + noise_scale * history_part, 'dp', scatter_dim...  106 us
    all_to_all x1, waiting for transfers between devices, body(): lax.all_to_all(jnp.broadcast_to(fresh_noise[None], (n_dp,) + fresh_noise....  78.8 us
    unnamed x31, local copies, waits for them, and re-layouts  61.2 us
    all_to_all x1, blocking collectives, body(): received = lax.all_to_all(partial_gram, 'fsdp', 0, 0, tiled=True)  58.2 us
    all_gather x1, waiting for transfers between devices, body(): gathered_weights = lax.all_gather(new_weights, 'dp', axis=1, tiled=True)  52.4 us
    dot_general x1, matrix products, body(): lax.dot_general(cotangents, scaled, (((0,), (0,)), ((), ())), preferred_e...  22.3 us
    select_n x1, other arithmetic, body(): jnp.where((slot_ids == target)[:, None, None], full_fresh[None], history)  15.8 us
    slice x1, local copies, waits for them, and re-layouts, body(): history[position].astype(jnp.float32)  12.2 us
  transfers between devices with their start and end apart: 5, of which 3 were waited for; matrix products, arithmetic and copies ran while one was open for 22% of the time, Pallas kernels for 0%

profile of v2, /device:TPU:0, one launch (start us, length us, event | category | flops | bytes accessed | tf_op | source)
XLA Modules:
  0.0 471.1 jit_solution(11738380973757858292)
XLA Ops:
  7.2 0.0 copy-start
  7.2 0.0 all-gather.3.cloned.1.call-start
  7.2 0.7 all-gather.3.cloned.1.call-update
  7.9 0.8 copy-done
  8.8 0.7 fusion.10
  9.5 0.0 copy-start.4
  9.5 58.2 %all_to_all.16 = f32[4,256,256]{1,2,0:T(8,128)} all-to-all(f32[4,256,256]{1,2,0:T(8,128)S(1)} %fusion.10), channel_id=1, replica_groups=mesh['dp'=8,'fsdp'=4] {'fsdp'}, dimensions={0} | all-to-all | bytes 2097152 | tf_op jit(solution)/shard_map/all_to_all | solution.py:42
  67.7 0.0 copy-done.4
  67.7 3.9 broadcast_in_dim.60
  71.6 0.0 copy-start.9
  71.6 0.0 copy-start.8
  71.6 5.2 %all-to-all-start = ((bf16[8,1024,512]{2,1,0:T(8,128)(2,1)}), bf16[8,1024,512]{2,1,0:T(8,128)(2,1)}, u32[]{:S(2)}, u32[]{:S(2)}) async-start(bf16[8,1024,512]{2,1,0:T(8,128)(2,1)} %broadcast_in_dim.60), calls=%async_computation | async-start | bytes 16777216 | tf_op jit(solution)/shard_map/all_to_all | solution.py:58
  77.5 0.0 copy-done.9
  77.5 0.0 copy-done.8
  77.5 0.2 fusion.5
  77.7 0.0 copy-start.6
  77.7 0.0 copy-start.7
  77.7 12.2 %fusion.8 = (bf16[1,1024,4096]{2,1,0:T(8,128)(2,1)}, bf16[1,1024,4096]{2,1,0:T(8,128)(2,1)}) fusion(bf16[2,1024,4096]{2,1,0:T(8,128)(2,1)} %param.19), kind=kLoop, calls=%fused_computation.27 | loop fusion | bytes 33554432 | tf_op jit(solution)/shard_map/slice | solution.py:72
  89.9 0.0 copy-done.6
  89.9 0.0 copy-done.7
  89.9 1.9 fusion.2
  91.9 0.1 fusion.3
  92.0 78.8 %all-to-all-done = bf16[8,1024,512]{2,1,0:T(8,128)(2,1)} async-done(((bf16[8,1024,512]{2,1,0:T(8,128)(2,1)}), bf16[8,1024,512]{2,1,0:T(8,128)(2,1)}, u32[]{:S(2)}, u32[]{:S(2)}) %all-to-all-start) | async-done | bytes 8388640 | tf_op jit(solution)/shard_map/all_to_all | solution.py:58
  170.8 0.6 broadcast_in_dim.63
  171.4 3.2 all-to-all-start.2
  174.7 0.0 reduce-scatter.2.cloned.1.call-start
  174.7 0.6 fusion.9
  175.3 11.7 %copy.72 = bf16[1,1024,4096]{1,2,0:T(8,128)(2,1)} copy(bf16[1,1024,4096]{2,1,0:T(8,128)(2,1)} %get-tuple-element.38) | data formatting | bytes 16777216
  187.0 11.9 %copy.71 = bf16[1,1024,4096]{1,2,0:T(8,128)(2,1)} copy(bf16[1,1024,4096]{2,1,0:T(8,128)(2,1)} %get-tuple-element.37) | data formatting | bytes 16777216
  199.6 11.5 %copy.57 = bf16[8,1024,512]{1,2,0:T(8,128)(2,1)} copy(bf16[8,1024,512]{2,1,0:T(8,128)(2,1)} %all-to-all-done) | data formatting | bytes 16777216 | tf_op jit(solution)/shard_map/all_to_all | solution.py:58
  211.1 0.0 all-gather.3.cloned.1.call-done
  211.1 0.0 all-to-all-done.2
  211.1 22.3 %bitcast_add_fusion = f32[1024,4096]{0,1:T(8,128)} fusion(bf16[1,1024,4096]{1,2,0:T(8,128)(2,1)} %copy.72, bf16[1,1024,4096]{1,2,0:T(8,128)(2,1)} %copy.71, bf16[1024,1024]{1,0:T(8,128)(2,1)S(1)} %copy-done, bf16[1024,4096]{1,0:T(8,128)(2,1)} %all-gather.3.cloned.1.call-done, f32[]{:T(128)} %bitcast.10, f32[]{:T(128)} %bitcast.9, f32[]{:T(128)} %bitcast.7, ...), kind=kOutput, calls=%fused_computation | convolution fusion | flops 8631877632 | bytes 44044300 | tf_op jit(solution)/shard_map/dot_general | solution.py:76
  233.4 0.0 reduce-scatter.2.cloned.1.call-update
  233.4 0.2 all-gather.5.cloned.1.call-start
  233.7 1.3 copy.61
  235.0 1.9 copy.63
  237.0 3.0 copy.56
  240.0 0.0 copy-start.5
  240.0 3.4 copy.62
  243.4 105.9 %reduce-scatter.2.cloned.1.call-done = f32[1024,512]{0,1:T(8,128)} async-done(((f32[1024,4096]{0,1:T(8,128)}), f32[1024,512]{0,1:T(8,128)}) %reduce-scatter.2.cloned.1.call-update) | async-done | bytes 2097168 | tf_op jit(solution)/shard_map/reduce_scatter | solution.py:84
  349.3 0.0 copy-done.5
  349.3 7.8 %divide_subtract_fusion = (f32[1024,512]{0,1:T(8,128)}, f32[1024,512]{0,1:T(8,128)}, f32[1024,512]{0,1:T(8,128)}, f32[1024,512]{0,1:T(8,128)}) fusion(f32[1024,512]{0,1:T(8,128)S(1)} %copy.63, f32[]{:T(128)S(6)} %sub.22, f32[]{:T(128)S(6)} %sub.21, f32[1024,512]{0,1:T(8,128)} %reduce-scatter.2.cloned.1.call-done, bf16[1024,512]{0,1:T(8,128)(2,1)S(1)} %copy-done.5, ...), kind=kLoop, calls=%fused_computation.4 | loop fusion | flops 8912896 | bytes 17825804 | tf_op jit(solution)/shard_map/sub | solution.py:96
  357.1 0.0 all-gather.5.cloned.1.call-update
  357.1 12.1 %copy.64 = bf16[1024,4096]{1,0:T(8,128)(2,1)} copy(bf16[1024,4096]{0,1:T(8,128)(2,1)} %bitcast.31) | data formatting | bytes 16777216 | tf_op jit(solution)/shard_map/optimization_barrier | solution.py:74
  369.3 0.0 copy-start.2
  369.3 15.8 %broadcast_select_fusion = bf16[2,1024,4096]{2,1,0:T(8,128)(2,1)} fusion(bf16[2,1024,4096]{2,1,0:T(8,128)(2,1)} %param.19, pred[2]{0:T(512)(128)(4,1)S(1)} %broadcast_compare_fusion, bf16[1024,4096]{1,0:T(8,128)(2,1)} %copy.64), kind=kLoop, calls=%fused_computation.2 | loop fusion | flops 8388608 | bytes 41943040 | tf_op jit(solution)/shard_map/jit(_where)/select_n | solution.py:82
  385.1 0.0 copy-done.2
  385.1 1.8 copy.65
  386.9 2.9 copy.66
  389.8 0.0 copy-start.3
  389.8 3.0 copy.67
  392.8 0.0 copy-done.3
  392.8 1.8 copy.68
  394.6 52.4 %all-gather.5.cloned.1.call-done = f32[1024,4096]{0,1:T(8,128)} async-done(((f32[1024,512]{0,1:T(8,128)}), f32[1024,4096]{0,1:T(8,128)}) %all-gather.5.cloned.1.call-update) | async-done | bytes 16777232 | tf_op jit(solution)/shard_map/all_gather | solution.py:97
  447.0 0.0 copy-start.1
  447.0 17.6 %copy.69 = f32[1024,4096]{1,0:T(8,128)} copy(f32[1024,4096]{0,1:T(8,128)} %all-gather.5.cloned.1.call-done) | data formatting | bytes 33554432
  464.6 0.0 copy-done.1
  (3 shorter events, 0.0 us)
Async XLA Ops:
  7.2 1.6 copy-start
  7.2 203.9 %all-gather.3.cloned.1.call-start = ((), (), s32[]{:S(2)}) async-start(), calls=%async_computation.4 | async-start | bytes 10485760 | tf_op jit(solution)/shard_map/all_gather | solution.py:38
  9.5 58.2 %copy-start.4 = (bf16[1024,512]{1,0:T(8,128)(2,1)S(1)}, bf16[1024,512]{1,0:T(8,128)(2,1)}, u32[]{:S(2)}) copy-start(bf16[1024,512]{1,0:T(8,128)(2,1)} %param.18) | copy-start | bytes 3145732
  71.6 5.8 %copy-start.9 = (s32[2]{0:T(128)S(1)}, s32[2]{0:T(128)}, u32[]{:S(2)}) copy-start(s32[2]{0:T(128)} %param.20) | copy-start | bytes 28
  71.6 5.9 %copy-start.8 = (f32[16]{0:T(128)S(1)}, f32[16]{0:T(128)}, u32[]{:S(2)}) copy-start(f32[16]{0:T(128)} %param.21) | copy-start | bytes 196
  71.6 99.2 %all-to-all-start = ((bf16[8,1024,512]{2,1,0:T(8,128)(2,1)}), bf16[8,1024,512]{2,1,0:T(8,128)(2,1)}, u32[]{:S(2)}, u32[]{:S(2)}) async-start(bf16[8,1024,512]{2,1,0:T(8,128)(2,1)} %broadcast_in_dim.60), calls=%async_computation | async-start | bytes 16777216 | tf_op jit(solution)/shard_map/all_to_all | solution.py:58
  77.7 12.3 %copy-start.6 = (bf16[256,4096]{1,0:T(8,128)(2,1)S(1)}, bf16[256,4096]{1,0:T(8,128)(2,1)}, u32[]{:S(2)}) copy-start(bf16[256,4096]{1,0:T(8,128)(2,1)} %param.12) | copy-start | bytes 6291460
  77.7 12.3 %copy-start.7 = (s32[1,256]{1,0:T(1,128)S(1)}, s32[1,256]{1,0:T(1,128)}, u32[]{:S(2)}) copy-start(s32[1,256]{1,0:T(1,128)} %param.14) | copy-start | bytes 3076
  171.4 39.7 %all-to-all-start.2 = ((f32[4,1,256]{2,1,0:T(1,128)}), f32[4,1,256]{2,1,0:T(1,128)S(1)}, u32[]{:S(2)}, u32[]{:S(2)}) async-start(f32[4,1,256]{2,1,0:T(1,128)} %broadcast_in_dim.63), calls=%async_computation.2 | async-start | bytes 8192 | tf_op jit(solution)/shard_map/all_to_all | solution.py:54
  174.7 174.6 %reduce-scatter.2.cloned.1.call-start = ((), (), s32[]{:S(2)}) async-start(), calls=%async_computation.5 | async-start | bytes 18874368 | tf_op jit(solution)/shard_map/reduce_scatter | solution.py:84
  233.4 213.6 %all-gather.5.cloned.1.call-start = ((), (), s32[]{:S(2)}) async-start(), calls=%async_computation.6 | async-start | bytes 18874368 | tf_op jit(solution)/shard_map/all_gather | solution.py:97
  240.0 109.3 %copy-start.5 = (bf16[1024,512]{0,1:T(8,128)(2,1)S(1)}, bf16[1024,512]{0,1:T(8,128)(2,1)}, u32[]{:S(2)}) copy-start(bf16[1024,512]{0,1:T(8,128)(2,1)} %copy.61) | copy-start | bytes 3145732
  369.3 15.8 %copy-start.2 = (f32[1024,512]{0,1:T(8,128)S(1)}, f32[1024,512]{0,1:T(8,128)}, u32[]{:S(2)}) copy-start(f32[1024,512]{0,1:T(8,128)} %get-tuple-element.34) | copy-start | bytes 6291460
  389.8 3.0 copy-start.3
  447.0 17.6 %copy-start.1 = (bf16[1024,1024]{1,0:T(8,128)(2,1)S(1)}, bf16[1024,1024]{1,0:T(8,128)(2,1)}, u32[]{:S(2)}) copy-start(bf16[1024,1024]{1,0:T(8,128)(2,1)} %param.13) | copy-start | bytes 6291460
Sparse Core Ops, SparseCore 0:
  9.6 167.4 all-gather.2
  233.5 115.7 reduce-scatter.1
  357.2 89.7 all-gather.4

commit v3 on v2

--- a/solution.py
+++ b/solution.py
@@ -35,11 +35,12 @@
         step_value = step_number[0]
         target = step_value % BAND
 
-        full_act = lax.all_gather(activations, "fsdp", axis=0, tiled=True)
-
         blocks = cotangents.reshape(n_fsdp, tok, out_local)
         partial_gram = jnp.einsum("ati,asi->ats", blocks, blocks, preferred_element_type=jnp.float32)
         received = lax.all_to_all(partial_gram, "fsdp", 0, 0, tiled=True)
+
+        gather_in, received = lax.optimization_barrier((activations, received))
+        full_act = lax.all_gather(gather_in, "fsdp", axis=0, tiled=True)
         cotan_gram = received[0]
         for part in range(1, n_fsdp):
             cotan_gram = cotan_gram + received[part]

time: 473 us -> 451 us (0.953)
  blocking collectives: 58.2 us -> 32.1 us
    all_to_all x1, blocking collectives: 58.2 us -> 32.1 us  [body(): received = lax.all_to_all(partial_gram, 'fsdp', 0, 0, tiled=True)]
    all_gather x1, waiting for transfers between devices: 0.01 us -> 5.37 us  [body(): full_act = lax.all_gather(gather_in, 'fsdp', axis=0, tiled=True)]
  transfers between devices with their start and end apart: 5 -> 5, of which waited for: 3 -> 4; matrix products, arithmetic and copies ran while one was open for 22% -> 23% of each run, Pallas kernels for 0% -> 0%
where the time goes in v3:
time: 451 us; the launch traced here: 449 us
  waiting for transfers between devices  240 us (53%)
  local copies, waits for them, and re-layouts  104 us (23%)
  blocking collectives  32.1 us (7%)
  matrix products  25 us (6%)
  other arithmetic  24 us (5%)
  between operations  15.3 us (3%)
  starting transfers between devices  8.85 us (2%)
    reduce_scatter x1, waiting for transfers between devices, body(): lax.psum_scatter(gradient + noise_scale * history_part, 'dp', scatter_dim...  105 us
    all_to_all x1, waiting for transfers between devices, body(): lax.all_to_all(jnp.broadcast_to(fresh_noise[None], (n_dp,) + fresh_noise....  78.1 us
    unnamed x31, local copies, waits for them, and re-layouts  61.9 us
    all_gather x1, waiting for transfers between devices, body(): gathered_weights = lax.all_gather(new_weights, 'dp', axis=1, tiled=True)  52.4 us
    all_to_all x1, blocking collectives, body(): received = lax.all_to_all(partial_gram, 'fsdp', 0, 0, tiled=True)  32.1 us
    dot_general x1, matrix products, body(): lax.dot_general(cotangents, scaled, (((0,), (0,)), ((), ())), preferred_e...  22.3 us
    select_n x1, other arithmetic, body(): jnp.where((slot_ids == target)[:, None, None], full_fresh[None], history)  15.8 us
    slice x1, local copies, waits for them, and re-layouts, body(): history[position].astype(jnp.float32)  12.8 us
  transfers between devices with their start and end apart: 5, of which 4 were waited for; matrix products, arithmetic and copies ran while one was open for 23% of the time, Pallas kernels for 0%

profile of v3, /device:TPU:0, one launch (start us, length us, event | category | flops | bytes accessed | tf_op | source)
XLA Modules:
  0.0 449.2 jit_solution(679602523961819349)
XLA Ops:
  7.2 0.0 copy-start
  7.2 0.0 all-gather.3.cloned.1.call-start
  7.2 1.5 copy-done
  8.8 0.7 fusion.9
  9.5 0.0 copy-start.4
  9.5 32.1 %all_to_all.16 = f32[4,256,256]{2,1,0:T(8,128)} all-to-all(f32[4,256,256]{2,1,0:T(8,128)S(1)} %fusion.9), channel_id=1, replica_groups=mesh['dp'=8,'fsdp'=4] {'fsdp'}, dimensions={0} | all-to-all | bytes 2097152 | tf_op jit(solution)/shard_map/all_to_all | solution.py:40
  41.6 0.0 all-gather.3.cloned.1.call-update
  41.7 0.0 copy-done.4
  41.7 3.9 broadcast_in_dim.60
  45.6 0.0 copy-start.9
  45.6 0.0 copy-start.8
  45.6 5.3 %all-to-all-start.1 = ((bf16[8,1024,512]{2,1,0:T(8,128)(2,1)}), bf16[8,1024,512]{2,1,0:T(8,128)(2,1)}, u32[]{:S(2)}, u32[]{:S(2)}) async-start(bf16[8,1024,512]{2,1,0:T(8,128)(2,1)} %broadcast_in_dim.60), calls=%async_computation.1 | async-start | bytes 16777216 | tf_op jit(solution)/shard_map/all_to_all | solution.py:59
  51.6 0.0 copy-done.9
  51.6 0.0 copy-done.8
  51.6 0.2 fusion.4
  51.8 0.0 copy-start.6
  51.8 0.0 copy-start.7
  51.8 12.8 %fusion.7 = (bf16[1,1024,4096]{2,1,0:T(8,128)(2,1)}, bf16[1,1024,4096]{2,1,0:T(8,128)(2,1)}) fusion(bf16[2,1024,4096]{2,1,0:T(8,128)(2,1)} %param.19), kind=kLoop, calls=%fused_computation.23 | loop fusion | bytes 33554432 | tf_op jit(solution)/shard_map/slice | solution.py:73
  64.6 0.0 copy-done.6
  64.6 0.0 copy-done.7
  64.6 2.0 fusion.2
  66.7 0.2 fusion.3
  66.9 78.1 %all-to-all-done.1 = bf16[8,1024,512]{2,1,0:T(8,128)(2,1)} async-done(((bf16[8,1024,512]{2,1,0:T(8,128)(2,1)}), bf16[8,1024,512]{2,1,0:T(8,128)(2,1)}, u32[]{:S(2)}, u32[]{:S(2)}) %all-to-all-start.1) | async-done | bytes 8388640 | tf_op jit(solution)/shard_map/all_to_all | solution.py:59
  145.0 0.6 broadcast_in_dim.63
  145.6 3.2 all-to-all-start.2
  148.8 0.0 reduce-scatter.2.cloned.1.call-start
  148.9 0.6 fusion.8
  149.4 11.7 %copy.72 = bf16[1,1024,4096]{1,2,0:T(8,128)(2,1)} copy(bf16[1,1024,4096]{2,1,0:T(8,128)(2,1)} %get-tuple-element.42) | data formatting | bytes 16777216
  161.1 11.9 %copy.71 = bf16[1,1024,4096]{1,2,0:T(8,128)(2,1)} copy(bf16[1,1024,4096]{2,1,0:T(8,128)(2,1)} %get-tuple-element.41) | data formatting | bytes 16777216
  173.7 11.5 %copy.57 = bf16[8,1024,512]{1,2,0:T(8,128)(2,1)} copy(bf16[8,1024,512]{2,1,0:T(8,128)(2,1)} %all-to-all-done.1) | data formatting | bytes 16777216 | tf_op jit(solution)/shard_map/all_to_all | solution.py:59
  185.2 5.4 %all-gather.3.cloned.1.call-done = bf16[1024,4096]{1,0:T(8,128)(2,1)} async-done(((bf16[256,4096]{1,0:T(8,128)(2,1)}), bf16[1024,4096]{1,0:T(8,128)(2,1)}) %all-gather.3.cloned.1.call-update) | async-done | bytes 8388624 | tf_op jit(solution)/shard_map/all_gather | solution.py:43
  190.6 0.0 all-to-all-done.2
  190.6 22.3 %bitcast_add_fusion = f32[1024,4096]{0,1:T(8,128)} fusion(bf16[1,1024,4096]{1,2,0:T(8,128)(2,1)} %copy.72, bf16[1,1024,4096]{1,2,0:T(8,128)(2,1)} %copy.71, bf16[1024,1024]{1,0:T(8,128)(2,1)S(1)} %copy-done, bf16[1024,4096]{1,0:T(8,128)(2,1)} %all-gather.3.cloned.1.call-done, f32[]{:T(128)} %bitcast.10, f32[]{:T(128)} %bitcast.9, f32[]{:T(128)} %bitcast.7, ...), kind=kOutput, calls=%fused_computation | convolution fusion | flops 8631877632 | bytes 44044300 | tf_op jit(solution)/shard_map/dot_general | solution.py:77
  212.9 0.0 reduce-scatter.2.cloned.1.call-update
  212.9 0.2 all-gather.5.cloned.1.call-start
  213.1 1.3 copy.61
  214.5 1.9 copy.63
  216.5 2.9 copy.56
  219.4 0.0 copy-start.5
  219.4 3.4 copy.62
  222.9 104.6 %reduce-scatter.2.cloned.1.call-done = f32[1024,512]{0,1:T(8,128)} async-done(((f32[1024,4096]{0,1:T(8,128)}), f32[1024,512]{0,1:T(8,128)}) %reduce-scatter.2.cloned.1.call-update) | async-done | bytes 2097168 | tf_op jit(solution)/shard_map/reduce_scatter | solution.py:85
  327.4 0.0 copy-done.5
  327.4 7.8 %divide_subtract_fusion = (f32[1024,512]{0,1:T(8,128)}, f32[1024,512]{0,1:T(8,128)}, f32[1024,512]{0,1:T(8,128)}, f32[1024,512]{0,1:T(8,128)}) fusion(f32[1024,512]{0,1:T(8,128)S(1)} %copy.63, f32[]{:T(128)S(6)} %sub.22, f32[]{:T(128)S(6)} %sub.21, f32[1024,512]{0,1:T(8,128)} %reduce-scatter.2.cloned.1.call-done, bf16[1024,512]{0,1:T(8,128)(2,1)S(1)} %copy-done.5, ...), kind=kLoop, calls=%fused_computation.4 | loop fusion | flops 8912896 | bytes 17825804 | tf_op jit(solution)/shard_map/sub | solution.py:97
  335.2 0.0 all-gather.5.cloned.1.call-update
  335.3 12.1 %copy.64 = bf16[1024,4096]{1,0:T(8,128)(2,1)} copy(bf16[1024,4096]{0,1:T(8,128)(2,1)} %bitcast.29) | data formatting | bytes 16777216 | tf_op jit(solution)/shard_map/optimization_barrier | solution.py:75
  347.4 0.0 copy-start.2
  347.4 15.8 %broadcast_select_fusion = bf16[2,1024,4096]{2,1,0:T(8,128)(2,1)} fusion(bf16[2,1024,4096]{2,1,0:T(8,128)(2,1)} %param.19, pred[2]{0:T(512)(128)(4,1)S(1)} %broadcast_compare_fusion, bf16[1024,4096]{1,0:T(8,128)(2,1)} %copy.64), kind=kLoop, calls=%fused_computation.2 | loop fusion | flops 8388608 | bytes 41943040 | tf_op jit(solution)/shard_map/jit(_where)/select_n | solution.py:83
  363.2 0.0 copy-done.2
  363.2 1.8 copy.65
  365.0 2.9 copy.66
  367.9 0.0 copy-start.3
  367.9 3.0 copy.67
  370.9 0.0 copy-done.3
  370.9 1.8 copy.68
  372.7 52.4 %all-gather.5.cloned.1.call-done = f32[1024,4096]{0,1:T(8,128)} async-done(((f32[1024,512]{0,1:T(8,128)}), f32[1024,4096]{0,1:T(8,128)}) %all-gather.5.cloned.1.call-update) | async-done | bytes 16777232 | tf_op jit(solution)/shard_map/all_gather | solution.py:98
  425.1 0.0 copy-start.1
  425.1 17.6 %copy.69 = f32[1024,4096]{1,0:T(8,128)} copy(f32[1024,4096]{0,1:T(8,128)} %all-gather.5.cloned.1.call-done) | data formatting | bytes 33554432
  442.7 0.0 copy-done.1
  (3 shorter events, 0.0 us)
Async XLA Ops:
  7.2 1.6 copy-start
  7.2 183.4 %all-gather.3.cloned.1.call-start = ((), (), s32[]{:S(2)}) async-start(), calls=%async_computation.4 | async-start | bytes 10485760 | tf_op jit(solution)/shard_map/all_gather | solution.py:43
  9.5 32.1 %copy-start.4 = (bf16[1024,512]{1,0:T(8,128)(2,1)S(1)}, bf16[1024,512]{1,0:T(8,128)(2,1)}, u32[]{:S(2)}) copy-start(bf16[1024,512]{1,0:T(8,128)(2,1)} %param.18) | copy-start | bytes 3145732
  45.6 6.0 %copy-start.9 = (s32[2]{0:T(128)S(1)}, s32[2]{0:T(128)}, u32[]{:S(2)}) copy-start(s32[2]{0:T(128)} %param.20) | copy-start | bytes 28
  45.6 6.0 %copy-start.8 = (f32[16]{0:T(128)S(1)}, f32[16]{0:T(128)}, u32[]{:S(2)}) copy-start(f32[16]{0:T(128)} %param.21) | copy-start | bytes 196
  45.6 99.3 %all-to-all-start.1 = ((bf16[8,1024,512]{2,1,0:T(8,128)(2,1)}), bf16[8,1024,512]{2,1,0:T(8,128)(2,1)}, u32[]{:S(2)}, u32[]{:S(2)}) async-start(bf16[8,1024,512]{2,1,0:T(8,128)(2,1)} %broadcast_in_dim.60), calls=%async_computation.1 | async-start | bytes 16777216 | tf_op jit(solution)/shard_map/all_to_all | solution.py:59
  51.8 12.8 %copy-start.6 = (bf16[256,4096]{1,0:T(8,128)(2,1)S(1)}, bf16[256,4096]{1,0:T(8,128)(2,1)}, u32[]{:S(2)}) copy-start(bf16[256,4096]{1,0:T(8,128)(2,1)} %param.12) | copy-start | bytes 6291460
  51.8 12.8 %copy-start.7 = (s32[1,256]{1,0:T(1,128)S(1)}, s32[1,256]{1,0:T(1,128)}, u32[]{:S(2)}) copy-start(s32[1,256]{1,0:T(1,128)} %param.14) | copy-start | bytes 3076
  145.6 45.1 %all-to-all-start.2 = ((f32[4,1,256]{2,1,0:T(1,128)}), f32[4,1,256]{2,1,0:T(1,128)S(1)}, u32[]{:S(2)}, u32[]{:S(2)}) async-start(f32[4,1,256]{2,1,0:T(1,128)} %broadcast_in_dim.63), calls=%async_computation.2 | async-start | bytes 8192 | tf_op jit(solution)/shard_map/all_to_all | solution.py:55
  148.8 178.6 %reduce-scatter.2.cloned.1.call-start = ((), (), s32[]{:S(2)}) async-start(), calls=%async_computation.5 | async-start | bytes 18874368 | tf_op jit(solution)/shard_map/reduce_scatter | solution.py:85
  212.9 212.2 %all-gather.5.cloned.1.call-start = ((), (), s32[]{:S(2)}) async-start(), calls=%async_computation.6 | async-start | bytes 18874368 | tf_op jit(solution)/shard_map/all_gather | solution.py:98
  219.4 108.0 %copy-start.5 = (bf16[1024,512]{0,1:T(8,128)(2,1)S(1)}, bf16[1024,512]{0,1:T(8,128)(2,1)}, u32[]{:S(2)}) copy-start(bf16[1024,512]{0,1:T(8,128)(2,1)} %copy.61) | copy-start | bytes 3145732
  347.4 15.8 %copy-start.2 = (f32[1024,512]{0,1:T(8,128)S(1)}, f32[1024,512]{0,1:T(8,128)}, u32[]{:S(2)}) copy-start(f32[1024,512]{0,1:T(8,128)} %get-tuple-element.38) | copy-start | bytes 6291460
  367.9 3.0 copy-start.3
  425.1 17.6 %copy-start.1 = (bf16[1024,1024]{1,0:T(8,128)(2,1)S(1)}, bf16[1024,1024]{1,0:T(8,128)(2,1)}, u32[]{:S(2)}) copy-start(bf16[1024,1024]{1,0:T(8,128)(2,1)} %param.13) | copy-start | bytes 6291460
Sparse Core Ops, SparseCore 0:
  41.8 148.7 all-gather.2
  213.0 114.3 reduce-scatter.1
  335.3 89.7 all-gather.4

commit v4 on v3

--- a/solution.py
+++ b/solution.py
@@ -74,17 +74,28 @@
 
         full_act, full_fresh = lax.optimization_barrier((full_act, full_fresh))
         scaled = (full_act.astype(jnp.float32) * factors[:, None]).astype(jnp.bfloat16)
-        gradient = lax.dot_general(
-            cotangents,
-            scaled,
-            (((0,), (0,)), ((), ())),
-            preferred_element_type=jnp.float32,
-        )
         new_history = jnp.where((slot_ids == target)[:, None, None], full_fresh[None], history)
         noise_scale = noise_mult[0] * clip
-        combined = lax.psum_scatter(
-            gradient + noise_scale * history_part, "dp", scatter_dimension=1, tiled=True
+
+        split = out_local - out_local // 4
+        d_in = scaled.shape[1]
+        cols = d_in // n_dp
+
+        def payload(lo, hi):
+            grad = lax.dot_general(
+                cotangents[:, lo:hi], scaled, (((0,), (0,)), ((), ())), preferred_element_type=jnp.float32
+            )
+            return grad + noise_scale * history_part[lo:hi]
+
+        reduced_first = lax.psum_scatter(payload(0, split), "dp", scatter_dimension=1, tiled=True)
+        second_part = jnp.transpose(
+            payload(split, out_local).reshape(out_local - split, n_dp, cols), (1, 0, 2)
         )
+        exchanged = lax.all_to_all(second_part, "dp", 0, 0, tiled=True)
+        reduced_second = exchanged[0]
+        for part in range(1, n_dp):
+            reduced_second = reduced_second + exchanged[part]
+        combined = jnp.concatenate([reduced_first, reduced_second], axis=0)
         examples = EX_DEV * n_dp * n_fsdp
         noisy_mean = (
             combined + noise_scale * band_coefs[0] * fresh_noise.astype(jnp.float32)

time: 451 us -> 453 us (level)
  waiting for transfers between devices: 240 us -> 216 us
  other arithmetic: 24 us -> 39.2 us
  matrix products: 25 us -> 33.2 us
  starting transfers between devices: 8.85 us -> 13.4 us
    reduce_scatter x1, waiting for transfers between devices: 105 us -> 20.8 us  [body(): lax.psum_scatter(payload(0, split), 'dp', scatter_dimension=1, tiled=True)]
    all_to_all x0 -> x1, waiting for transfers between devices: none -> 73.5 us  [body(): exchanged = lax.all_to_all(second_part, 'dp', 0, 0, tiled=True)]
    all_to_all x1, waiting for transfers between devices: 78.1 us -> 54.1 us  [body(): lax.all_to_all(jnp.broadcast_to(fresh_noise[None], (n_dp,) + fresh_noise....]
    add x0 -> x2, other arithmetic: none -> 17.3 us  [the longest x1 14 us: body(): history_part + lag_weight[position] * history[position].astype(jnp.float32)]
    all_gather x1, waiting for transfers between devices: 5.37 us -> 15.5 us  [body(): full_act = lax.all_gather(gather_in, 'fsdp', axis=0, tiled=True)]
    dot_general x1 -> x2, matrix products: 22.3 us -> 28.2 us  [payload(): lax.dot_general(cotangents[:, lo:hi], scaled, (((0,), (0,)), ((), ())), p...]
    all_to_all x0 -> x1, starting transfers between devices: none -> 4.82 us  [body(): exchanged = lax.all_to_all(second_part, 'dp', 0, 0, tiled=True)]
    unnamed x31 -> x29, local copies, waits for them, and re-layouts: 61.9 us -> 60.1 us
  transfers between devices with their start and end apart: 5 -> 6, of which waited for: 4 -> 5; matrix products, arithmetic and copies ran while one was open for 23% -> 29% of each run, Pallas kernels for 0% -> 0%
where the time goes in v4:
time: 453 us; the launch traced here: 451 us
  waiting for transfers between devices  216 us (48%)
  local copies, waits for them, and re-layouts  101 us (22%)
  other arithmetic  39.2 us (9%)
  matrix products  33.2 us (7%)
  blocking collectives  32.1 us (7%)
  between operations  15.3 us (3%)
  starting transfers between devices  13.4 us (3%)
    all_to_all x1, waiting for transfers between devices, body(): exchanged = lax.all_to_all(second_part, 'dp', 0, 0, tiled=True)  73.5 us
    unnamed x29, local copies, waits for them, and re-layouts  60.1 us
    all_to_all x1, waiting for transfers between devices, body(): lax.all_to_all(jnp.broadcast_to(fresh_noise[None], (n_dp,) + fresh_noise....  54.1 us
    all_gather x1, waiting for transfers between devices, body(): gathered_weights = lax.all_gather(new_weights, 'dp', axis=1, tiled=True)  52.4 us
    all_to_all x1, blocking collectives, body(): received = lax.all_to_all(partial_gram, 'fsdp', 0, 0, tiled=True)  32.1 us
    dot_general x2, matrix products, payload(): lax.dot_general(cotangents[:, lo:hi], scaled, (((0,), (0,)), ((), ())), p...  28.2 us
    reduce_scatter x1, waiting for transfers between devices, body(): lax.psum_scatter(payload(0, split), 'dp', scatter_dimension=1, tiled=True)  20.8 us
    select_n x1, other arithmetic, body(): jnp.where((slot_ids == target)[:, None, None], full_fresh[None], history)  15.8 us
  transfers between devices with their start and end apart: 6, of which 5 were waited for; matrix products, arithmetic and copies ran while one was open for 29% of the time, Pallas kernels for 0%

profile of v4, /device:TPU:0, one launch (start us, length us, event | category | flops | bytes accessed | tf_op | source)
XLA Modules:
  0.0 450.8 jit_solution(10317764111864455236)
XLA Ops:
  7.2 0.0 all-gather.3.cloned.1.call-start
  7.2 3.0 fusion.15
  10.2 0.0 copy-start.3
  10.2 32.1 %all_to_all.21 = f32[4,256,256]{2,1,0:T(8,128)} all-to-all(f32[4,256,256]{2,1,0:T(8,128)S(1)} %fusion.15), channel_id=1, replica_groups=mesh['dp'=8,'fsdp'=4] {'fsdp'}, dimensions={0} | all-to-all | bytes 2097152 | tf_op jit(solution)/shard_map/all_to_all | solution.py:40
  42.3 0.0 all-gather.3.cloned.1.call-update
  42.3 0.0 copy-done.3
  42.3 3.9 broadcast_in_dim.60
  46.3 5.2 %all-to-all-start.1 = ((bf16[8,1024,512]{2,1,0:T(8,128)(2,1)}), bf16[8,1024,512]{2,1,0:T(8,128)(2,1)}, u32[]{:S(2)}, u32[]{:S(2)}) async-start(bf16[8,1024,512]{2,1,0:T(8,128)(2,1)} %broadcast_in_dim.60), calls=%async_computation.1 | async-start | bytes 16777216 | tf_op jit(solution)/shard_map/all_to_all | solution.py:59
  52.1 12.2 %fusion.13 = (bf16[1,1024,4096]{2,1,0:T(8,128)(2,1)}, bf16[1,1024,4096]{2,1,0:T(8,128)(2,1)}) fusion(bf16[2,1024,4096]{2,1,0:T(8,128)(2,1)} %param.19), kind=kLoop, calls=%fused_computation.39 | loop fusion | bytes 33554432 | tf_op jit(solution)/shard_map/slice | solution.py:73
  64.4 11.9 %copy.72 = bf16[1,1024,4096]{1,2,0:T(8,128)(2,1)} copy(bf16[1,1024,4096]{2,1,0:T(8,128)(2,1)} %get-tuple-element.42) | data formatting | bytes 16777216
  76.2 0.0 copy-start.8
  76.2 0.0 copy-start.7
  76.2 0.0 copy-start.5
  76.2 0.0 copy-start.6
  76.2 12.1 %copy.71 = bf16[1,1024,4096]{1,2,0:T(8,128)(2,1)} copy(bf16[1,1024,4096]{2,1,0:T(8,128)(2,1)} %get-tuple-element.41) | data formatting | bytes 16777216
  88.3 0.0 copy-done.8
  88.4 0.0 copy-done.7
  88.4 0.2 fusion.10
  88.5 0.6 fusion.14
  89.1 0.0 copy-done.5
  89.1 0.0 copy-done.6
  89.1 2.0 fusion.6
  91.1 0.2 fusion.9
  91.3 54.1 %all-to-all-done.1 = bf16[8,1024,512]{2,1,0:T(8,128)(2,1)} async-done(((bf16[8,1024,512]{2,1,0:T(8,128)(2,1)}), bf16[8,1024,512]{2,1,0:T(8,128)(2,1)}, u32[]{:S(2)}, u32[]{:S(2)}) %all-to-all-start.1) | async-done | bytes 8388640 | tf_op jit(solution)/shard_map/all_to_all | solution.py:59
  145.5 0.6 broadcast_in_dim.63
  146.1 3.2 all-to-all-start.2
  149.3 0.0 reduce-scatter.2.cloned.1.call-start
  149.4 14.0 %multiply_add_fusion = f32[1,1024,4096]{1,2,0:T(8,128)} fusion(bf16[1,1024,4096]{1,2,0:T(8,128)(2,1)} %copy.72, bf16[1,1024,4096]{1,2,0:T(8,128)(2,1)} %copy.71, f32[]{:T(128)} %bitcast.10, f32[]{:T(128)} %bitcast.9), kind=kLoop, calls=%fused_computation | loop fusion | flops 20971520 | bytes 33554440 | tf_op jit(solution)/shard_map/add | solution.py:73
  164.1 0.0 copy-start.1
  164.1 11.7 %copy.57 = bf16[8,1024,512]{1,2,0:T(8,128)(2,1)} copy(bf16[8,1024,512]{2,1,0:T(8,128)(2,1)} %all-to-all-done.1) | data formatting | bytes 16777216 | tf_op jit(solution)/shard_map/all_to_all | solution.py:59
  175.8 15.5 %all-gather.3.cloned.1.call-done = bf16[1024,4096]{1,0:T(8,128)(2,1)} async-done(((bf16[256,4096]{1,0:T(8,128)(2,1)}), bf16[1024,4096]{1,0:T(8,128)(2,1)}) %all-gather.3.cloned.1.call-update) | async-done | bytes 8388624 | tf_op jit(solution)/shard_map/all_gather | solution.py:43
  191.3 0.0 all-to-all-done.2
  191.3 0.0 copy-done.1
  191.3 17.0 %fusion.1 = f32[768,4096]{0,1:T(8,128)} fusion(f32[1,1024,4096]{1,2,0:T(8,128)} %multiply_add_fusion, f32[]{:T(128)} %bitcast.7, bf16[1024,4096]{1,0:T(8,128)(2,1)} %all-gather.3.cloned.1.call-done, f32[1024]{0:T(1024)S(1)} %bitcast.45, bf16[1024,1024]{1,0:T(8,128)(2,1)S(1)} %copy-done.1), kind=kOutput, calls=%fused_computation.5 | convolution fusion | flops 6461325312 | bytes 35131396 | tf_op jit(solution)/shard_map/dot_general | solution.py:85
  208.3 0.0 reduce-scatter.2.cloned.1.call-update
  208.3 11.3 %fusion.2 = f32[256,4096]{0,1:T(8,128)} fusion(f32[1,1024,4096]{1,2,0:T(8,128)} %multiply_add_fusion, bf16[1024,4096]{1,0:T(8,128)(2,1)} %all-gather.3.cloned.1.call-done, f32[1024]{0:T(1024)S(1)} %bitcast.46, f32[]{:T(128)} %bitcast.7, bf16[1024,1024]{1,0:T(8,128)(2,1)S(1)} %copy-done.1), kind=kOutput, calls=%fused_computation.7 | convolution fusion | flops 2162163712 | bytes 17305604 | tf_op jit(solution)/shard_map/dot_general | solution.py:85
  219.6 4.8 %all-to-all-start.3 = ((f32[8,256,512]{1,2,0:T(8,128)}), f32[8,256,512]{1,2,0:T(8,128)}, u32[]{:S(2)}, u32[]{:S(2)}) async-start(f32[8,256,512]{1,2,0:T(8,128)} %bitcast.44), calls=%async_computation.4 | async-start | bytes 8388608 | tf_op jit(solution)/shard_map/all_to_all | solution.py:94
  224.4 0.0 all-gather.5.cloned.1.call-start
  224.4 1.3 copy.61
  225.8 2.0 copy.63
  227.9 2.9 copy.56
  230.8 2.9 copy.62
  233.7 0.0 copy-start.4
  233.7 73.5 %all-to-all-done.3 = f32[8,256,512]{1,2,0:T(8,128)} async-done(((f32[8,256,512]{1,2,0:T(8,128)}), f32[8,256,512]{1,2,0:T(8,128)}, u32[]{:S(2)}, u32[]{:S(2)}) %all-to-all-start.3) | async-done | bytes 4194336 | tf_op jit(solution)/shard_map/all_to_all | solution.py:94
  307.2 3.2 fusion.7
  310.4 20.8 %reduce-scatter.2.cloned.1.call-done = f32[768,512]{0,1:T(8,128)} async-done(((f32[768,4096]{0,1:T(8,128)}), f32[768,512]{0,1:T(8,128)}) %reduce-scatter.2.cloned.1.call-update) | async-done | bytes 1572880 | tf_op jit(solution)/shard_map/reduce_scatter | solution.py:90
  331.1 0.0 copy-done.4
  331.1 5.8 %divide_subtract_fusion = (f32[1024,512]{0,1:T(8,128)}, f32[1024,512]{0,1:T(8,128)}, f32[1024,512]{0,1:T(8,128)}, f32[1024,512]{0,1:T(8,128)}) fusion(f32[1024,512]{0,1:T(8,128)S(1)} %copy.63, f32[]{:T(128)S(6)} %sub.22, f32[]{:T(128)S(6)} %sub.21, bf16[1024,512]{0,1:T(8,128)(2,1)S(1)} %copy-done.4, f32[]{:T(128)S(6)} %mul.111, f32[256,512]{0,1:T(8,128)} %fusion.7, ...), kind=kLoop, calls=%fused_computation.11 | loop fusion | flops 9437184 | bytes 17825804 | tf_op jit(solution)/shard_map/sub | solution.py:108
  336.9 0.0 all-gather.5.cloned.1.call-update
  337.0 12.1 %copy.64 = bf16[1024,4096]{1,0:T(8,128)(2,1)} copy(bf16[1024,4096]{0,1:T(8,128)(2,1)} %bitcast.42) | data formatting | bytes 16777216 | tf_op jit(solution)/shard_map/optimization_barrier | solution.py:75
  349.1 0.0 copy-start
  349.1 15.8 %broadcast_select_fusion = bf16[2,1024,4096]{2,1,0:T(8,128)(2,1)} fusion(bf16[2,1024,4096]{2,1,0:T(8,128)(2,1)} %param.19, pred[2]{0:T(512)(128)(4,1)S(1)} %broadcast_compare_fusion, bf16[1024,4096]{1,0:T(8,128)(2,1)} %copy.64), kind=kLoop, calls=%fused_computation.2 | loop fusion | flops 8388608 | bytes 41943040 | tf_op jit(solution)/shard_map/jit(_where)/select_n | solution.py:77
  364.9 0.0 copy-done
  364.9 1.8 copy.65
  366.7 2.9 copy.66
  369.6 0.0 copy-start.2
  369.6 3.0 copy.67
  372.6 0.0 copy-done.2
  372.6 1.8 copy.68
  374.4 52.4 %all-gather.5.cloned.1.call-done = f32[1024,4096]{0,1:T(8,128)} async-done(((f32[1024,512]{0,1:T(8,128)}), f32[1024,4096]{0,1:T(8,128)}) %all-gather.5.cloned.1.call-update) | async-done | bytes 16777232 | tf_op jit(solution)/shard_map/all_gather | solution.py:109
  426.8 17.4 %copy.69 = f32[1024,4096]{1,0:T(8,128)} copy(f32[1024,4096]{0,1:T(8,128)} %all-gather.5.cloned.1.call-done) | data formatting | bytes 33554432
  (3 shorter events, 0.0 us)
Async XLA Ops:
  7.2 184.1 %all-gather.3.cloned.1.call-start = ((), (), s32[]{:S(2)}) async-start(), calls=%async_computation.5 | async-start | bytes 10485760 | tf_op jit(solution)/shard_map/all_gather | solution.py:43
  10.2 32.1 %copy-start.3 = (bf16[1024,512]{1,0:T(8,128)(2,1)S(1)}, bf16[1024,512]{1,0:T(8,128)(2,1)}, u32[]{:S(2)}) copy-start(bf16[1024,512]{1,0:T(8,128)(2,1)} %param.18) | copy-start | bytes 3145732
  46.3 99.2 %all-to-all-start.1 = ((bf16[8,1024,512]{2,1,0:T(8,128)(2,1)}), bf16[8,1024,512]{2,1,0:T(8,128)(2,1)}, u32[]{:S(2)}, u32[]{:S(2)}) async-start(bf16[8,1024,512]{2,1,0:T(8,128)(2,1)} %broadcast_in_dim.60), calls=%async_computation.1 | async-start | bytes 16777216 | tf_op jit(solution)/shard_map/all_to_all | solution.py:59
  76.2 12.1 %copy-start.8 = (s32[2]{0:T(128)S(1)}, s32[2]{0:T(128)}, u32[]{:S(2)}) copy-start(s32[2]{0:T(128)} %param.20) | copy-start | bytes 28
  76.2 12.1 %copy-start.7 = (f32[16]{0:T(128)S(1)}, f32[16]{0:T(128)}, u32[]{:S(2)}) copy-start(f32[16]{0:T(128)} %param.21) | copy-start | bytes 196
  76.2 12.9 %copy-start.5 = (bf16[256,4096]{1,0:T(8,128)(2,1)S(1)}, bf16[256,4096]{1,0:T(8,128)(2,1)}, u32[]{:S(2)}) copy-start(bf16[256,4096]{1,0:T(8,128)(2,1)} %param.12) | copy-start | bytes 6291460
  76.2 12.9 %copy-start.6 = (s32[1,256]{1,0:T(1,128)S(1)}, s32[1,256]{1,0:T(1,128)}, u32[]{:S(2)}) copy-start(s32[1,256]{1,0:T(1,128)} %param.14) | copy-start | bytes 3076
  146.1 45.2 %all-to-all-start.2 = ((f32[4,1,256]{2,1,0:T(1,128)}), f32[4,1,256]{2,1,0:T(1,128)S(1)}, u32[]{:S(2)}, u32[]{:S(2)}) async-start(f32[4,1,256]{2,1,0:T(1,128)} %broadcast_in_dim.63), calls=%async_computation.2 | async-start | bytes 8192 | tf_op jit(solution)/shard_map/all_to_all | solution.py:55
  149.3 181.8 %reduce-scatter.2.cloned.1.call-start = ((), (), s32[]{:S(2)}) async-start(), calls=%async_computation.6 | async-start | bytes 14155776 | tf_op jit(solution)/shard_map/reduce_scatter | solution.py:90
  164.1 27.2 %copy-start.1 = (bf16[1024,1024]{1,0:T(8,128)(2,1)S(1)}, bf16[1024,1024]{1,0:T(8,128)(2,1)}, u32[]{:S(2)}) copy-start(bf16[1024,1024]{1,0:T(8,128)(2,1)} %param.13) | copy-start | bytes 6291460
  219.6 87.6 %all-to-all-start.3 = ((f32[8,256,512]{1,2,0:T(8,128)}), f32[8,256,512]{1,2,0:T(8,128)}, u32[]{:S(2)}, u32[]{:S(2)}) async-start(f32[8,256,512]{1,2,0:T(8,128)} %bitcast.44), calls=%async_computation.4 | async-start | bytes 8388608 | tf_op jit(solution)/shard_map/all_to_all | solution.py:94
  224.4 202.4 %all-gather.5.cloned.1.call-start = ((), (), s32[]{:S(2)}) async-start(), calls=%async_computation.7 | async-start | bytes 18874368 | tf_op jit(solution)/shard_map/all_gather | solution.py:109
  233.7 97.5 %copy-start.4 = (bf16[1024,512]{0,1:T(8,128)(2,1)S(1)}, bf16[1024,512]{0,1:T(8,128)(2,1)}, u32[]{:S(2)}) copy-start(bf16[1024,512]{0,1:T(8,128)(2,1)} %copy.61) | copy-start | bytes 3145732
  349.1 15.8 %copy-start = (f32[1024,512]{0,1:T(8,128)S(1)}, f32[1024,512]{0,1:T(8,128)}, u32[]{:S(2)}) copy-start(f32[1024,512]{0,1:T(8,128)} %get-tuple-element.38) | copy-start | bytes 6291460
  369.6 3.0 copy-start.2
Sparse Core Ops, SparseCore 0:
  42.4 148.7 all-gather.2
  208.4 122.6 reduce-scatter.1
  337.0 89.7 all-gather.4

commit v5 on v3

--- a/solution.py
+++ b/solution.py
@@ -40,7 +40,6 @@
         received = lax.all_to_all(partial_gram, "fsdp", 0, 0, tiled=True)
 
         gather_in, received = lax.optimization_barrier((activations, received))
-        full_act = lax.all_gather(gather_in, "fsdp", axis=0, tiled=True)
         cotan_gram = received[0]
         for part in range(1, n_fsdp):
             cotan_gram = cotan_gram + received[part]
@@ -56,12 +55,7 @@
             jnp.broadcast_to(factor[None], (n_fsdp, tok)), "fsdp", 0, 0, tiled=True
         ).reshape(n_fsdp * tok)
 
-        fresh_parts = lax.all_to_all(
-            jnp.broadcast_to(fresh_noise[None], (n_dp,) + fresh_noise.shape), "dp", 0, 0, tiled=True
-        )
-        full_fresh = jnp.transpose(fresh_parts, (1, 0, 2)).reshape(
-            fresh_noise.shape[0], n_dp * fresh_noise.shape[1]
-        )
+        full_fresh = lax.all_gather(fresh_noise, "dp", axis=1, tiled=True)
 
         lags = (step_value - slot_ids - 1) % BAND + 1
         columns = jnp.arange(BAND, dtype=jnp.int32)
@@ -71,20 +65,30 @@
         history_part = jnp.zeros(history.shape[1:], jnp.float32)
         for position in range(history.shape[0]):
             history_part = history_part + lag_weight[position] * history[position].astype(jnp.float32)
+        noise_scale = noise_mult[0] * clip
 
-        full_act, full_fresh = lax.optimization_barrier((full_act, full_fresh))
-        scaled = (full_act.astype(jnp.float32) * factors[:, None]).astype(jnp.bfloat16)
-        gradient = lax.dot_general(
-            cotangents,
-            scaled,
-            (((0,), (0,)), ((), ())),
-            preferred_element_type=jnp.float32,
-        )
+        d_in = activations.shape[1]
+        cols = d_in // n_dp
+        chunks = 2
+        width = cols // chunks
+        act4 = gather_in.reshape(tok, n_dp, chunks, width)
+        history4 = history_part.reshape(out_local, n_dp, chunks, width)
+        reduced = []
+        for c in range(chunks):
+            own = act4[:, :, c, :]
+            rows = lax.all_to_all(
+                jnp.broadcast_to(own[None], (n_fsdp,) + own.shape), "fsdp", 0, 0, tiled=True
+            ).reshape(n_fsdp * tok, n_dp * width)
+            if c == 0:
+                rows, full_fresh = lax.optimization_barrier((rows, full_fresh))
+            scaled = (rows.astype(jnp.float32) * factors[:, None]).astype(jnp.bfloat16)
+            grad = lax.dot_general(
+                cotangents, scaled, (((0,), (0,)), ((), ())), preferred_element_type=jnp.float32
+            )
+            payload = grad + noise_scale * history4[:, :, c, :].reshape(out_local, n_dp * width)
+            reduced.append(lax.psum_scatter(payload, "dp", scatter_dimension=1, tiled=True))
+        combined = jnp.concatenate(reduced, axis=1)
         new_history = jnp.where((slot_ids == target)[:, None, None], full_fresh[None], history)
-        noise_scale = noise_mult[0] * clip
-        combined = lax.psum_scatter(
-            gradient + noise_scale * history_part, "dp", scatter_dimension=1, tiled=True
-        )
         examples = EX_DEV * n_dp * n_fsdp
         noisy_mean = (
             combined + noise_scale * band_coefs[0] * fresh_noise.astype(jnp.float32)

time: 451 us -> 494 us (1.095)
  local copies, waits for them, and re-layouts: 104 us -> 157 us
  waiting for transfers between devices: 240 us -> 193 us
  other arithmetic: 24 us -> 54 us
  starting transfers between devices: 8.85 us -> 14.2 us
    reduce_scatter x1 -> x2, waiting for transfers between devices: 105 us -> 59 us  [body(): lax.psum_scatter(payload, 'dp', scatter_dimension=1, tiled=True)]
    unnamed x31 -> x25, local copies, waits for them, and re-layouts: 61.9 us -> 95.9 us
    add x0 -> x1, local copies, waits for them, and re-layouts: none -> 22 us  [body(): history_part + lag_weight[position] * history[position].astype(jnp.float32)]
    mul x0 -> x2, other arithmetic: none -> 17.6 us  [body(): noise_scale * history4[:, :, c, :].reshape(out_local, n_dp * width)]
    slice x1 -> x4, local copies, waits for them, and re-layouts: 12.8 us -> 28.8 us  [the longest x1 22.1 us: body(): history4[:, :, c, :].reshape(out_local, n_dp * width)]
    add x0 -> x1, other arithmetic: none -> 13.8 us  [body(): history_part + lag_weight[position] * history[position].astype(jnp.float32)]
    all_to_all x1 -> x0, local copies, waits for them, and re-layouts: 11.5 us -> none  [body(): lax.all_to_all(jnp.broadcast_to(fresh_noise[None], (n_dp,) + fresh_noise....]
    all_gather x1, waiting for transfers between devices: 52.4 us -> 62.2 us  [body(): gathered_weights = lax.all_gather(new_weights, 'dp', axis=1, tiled=True)]
  transfers between devices with their start and end apart: 5 -> 7, of which waited for: 4 -> 4; matrix products, arithmetic and copies ran while one was open for 23% -> 43% of each run, Pallas kernels for 0% -> 0%
where the time goes in v5:
time: 494 us; the launch traced here: 491 us
  waiting for transfers between devices  193 us (39%)
  local copies, waits for them, and re-layouts  157 us (32%)
  other arithmetic  54 us (11%)
  blocking collectives  32 us (6%)
  matrix products  26.4 us (5%)
  between operations  15.3 us (3%)
  starting transfers between devices  14.2 us (3%)
    unnamed x25, local copies, waits for them, and re-layouts  95.9 us
    all_to_all x2, waiting for transfers between devices, body(): lax.all_to_all(jnp.broadcast_to(own[None], (n_fsdp,) + own.shape), 'fsdp'...  70.9 us
    all_gather x1, waiting for transfers between devices, body(): gathered_weights = lax.all_gather(new_weights, 'dp', axis=1, tiled=True)  62.2 us
    reduce_scatter x2, waiting for transfers between devices, body(): lax.psum_scatter(payload, 'dp', scatter_dimension=1, tiled=True)  59 us
    all_to_all x1, blocking collectives, body(): received = lax.all_to_all(partial_gram, 'fsdp', 0, 0, tiled=True)  32 us
    dot_general x2, matrix products, body(): lax.dot_general(cotangents, scaled, (((0,), (0,)), ((), ())), preferred_e...  22.4 us
    slice x1, local copies, waits for them, and re-layouts, body(): history4[:, :, c, :].reshape(out_local, n_dp * width)  22.1 us
    add x1, local copies, waits for them, and re-layouts, body(): history_part + lag_weight[position] * history[position].astype(jnp.float32)  22 us
  transfers between devices with their start and end apart: 7, of which 4 were waited for; matrix products, arithmetic and copies ran while one was open for 43% of the time, Pallas kernels for 0%

profile of v5, /device:TPU:0, one launch (start us, length us, event | category | flops | bytes accessed | tf_op | source)
XLA Modules:
  0.0 491.3 jit_solution(10790112673069763241)
XLA Ops:
  7.2 0.0 copy-start
  7.2 0.0 all-gather.3.cloned.1.call-start
  7.2 0.7 all-gather.3.cloned.1.call-update
  7.9 0.8 copy-done
  8.8 0.7 fusion.11
  9.5 32.0 %all_to_all.21 = f32[4,256,256]{2,1,0:T(8,128)} all-to-all(f32[4,256,256]{2,1,0:T(8,128)S(1)} %fusion.11), channel_id=1, replica_groups=mesh['dp'=8,'fsdp'=4] {'fsdp'}, dimensions={0} | all-to-all | bytes 2097152 | tf_op jit(solution)/shard_map/all_to_all | solution.py:40
  41.5 4.1 copy.58
  45.6 3.0 fusion.9
  48.6 1.9 copy.62
  50.5 2.2 broadcast_in_dim.76
  52.7 0.0 copy-start.5
  52.8 0.0 copy-start.4
  52.8 5.1 %all-to-all-start.3 = ((bf16[4,256,8,256]{3,2,1,0:T(8,128)(2,1)}), bf16[4,256,8,256]{3,2,1,0:T(8,128)(2,1)}, u32[]{:S(2)}, u32[]{:S(2)}) async-start(bf16[4,256,8,256]{3,2,1,0:T(8,128)(2,1)} %broadcast_in_dim.76), calls=%async_computation.4 | async-start | bytes 8388608 | tf_op jit(solution)/shard_map/all_to_all | solution.py:79
  59.2 0.0 copy-done.5
  59.2 0.0 copy-done.4
  59.2 0.2 fusion.5
  59.4 0.6 fusion.10
  60.0 13.8 %multiply_add_fusion = f32[1,1024,4096]{2,1,0:T(8,128)} fusion(bf16[2,1024,4096]{2,1,0:T(8,128)(2,1)} %param.19, f32[]{:T(128)} %bitcast.10, f32[]{:T(128)} %bitcast.9), kind=kLoop, calls=%fused_computation | loop fusion | flops 20971520 | bytes 33554440 | tf_op jit(solution)/shard_map/add | solution.py:67
  73.8 22.0 %add.67 = f32[1024,8,2,256]{3,2,1,0:T(2,128)} reshape(f32[1,1024,4096]{2,1,0:T(8,128)} %multiply_add_fusion) | data formatting | bytes 33554432 | tf_op jit(solution)/shard_map/add | solution.py:67
  95.8 22.1 %fusion.8 = (f32[1024,8,1,256]{3,2,1,0:T(1,128)}, f32[1024,8,1,256]{3,2,1,0:T(1,128)}) fusion(f32[1024,8,2,256]{3,2,1,0:T(2,128)} %add.67), kind=kLoop, calls=%fused_computation.29 | loop fusion | bytes 33554432 | tf_op jit(solution)/shard_map/slice | solution.py:88
  117.9 0.0 copy-start.3
  117.9 20.6 %copy.74 = f32[1024,8,1,256]{0,3,1,2:T(8,128)} copy(f32[1024,8,1,256]{3,2,1,0:T(1,128)} %get-tuple-element.42) | data formatting | bytes 16777216
  138.5 0.0 copy-done.3
  138.5 3.3 fusion.3
  141.8 0.2 fusion.4
  142.0 8.5 %all-to-all-done.3 = bf16[4,256,8,256]{3,2,1,0:T(8,128)(2,1)} async-done(((bf16[4,256,8,256]{3,2,1,0:T(8,128)(2,1)}), bf16[4,256,8,256]{3,2,1,0:T(8,128)(2,1)}, u32[]{:S(2)}, u32[]{:S(2)}) %all-to-all-start.3) | async-done | bytes 4194336 | tf_op jit(solution)/shard_map/all_to_all | solution.py:79
  150.5 0.6 broadcast_in_dim.72
  151.1 3.2 all-to-all-start.2
  154.3 0.2 reduce-scatter.5.cloned.1.call-start
  154.6 8.7 %broadcast_multiply_fusion = f32[1024,8,1,256]{0,3,1,2:T(8,128)} fusion(f32[1024,8,1,256]{0,3,1,2:T(8,128)} %copy.74, f32[]{:T(128)} %bitcast.7), kind=kLoop, calls=%fused_computation.6 | loop fusion | flops 2097152 | bytes 16777220 | tf_op jit(solution)/shard_map/mul | solution.py:88
  163.3 7.5 %copy.76 = f32[128,8,8,256]{3,1,2,0:T(8,128)} copy(bf16[128,8,8,256]{3,2,1,0:T(8,128)(2,1)} %bitcast.27) | data formatting | bytes 12582912
  170.8 0.0 all-to-all-done.2
  170.8 11.8 %bitcast_add_fusion = f32[1024,2048]{0,1:T(8,128)} fusion(f32[1024,8,1,256]{0,3,1,2:T(8,128)} %broadcast_multiply_fusion, bf16[1024,1024]{1,0:T(8,128)(2,1)S(1)} %copy-done, f32[1024,2048]{1,0:T(8,128)} %bitcast.41, f32[1024]{0:T(1024)S(1)} %bitcast.46), kind=kOutput, calls=%fused_computation.2 | convolution fusion | flops 4301258752 | bytes 27267072 | tf_op jit(solution)/shard_map/dot_general | solution.py:85
  182.6 0.0 reduce-scatter.5.cloned.1.call-update
  182.6 1.9 copy.59
  184.5 2.2 broadcast_in_dim.69
  186.7 5.3 %all-to-all-start.1 = ((bf16[4,256,8,256]{3,2,1,0:T(8,128)(2,1)}), bf16[4,256,8,256]{3,2,1,0:T(8,128)(2,1)}, u32[]{:S(2)}, u32[]{:S(2)}) async-start(bf16[4,256,8,256]{3,2,1,0:T(8,128)(2,1)} %broadcast_in_dim.69), calls=%async_computation.1 | async-start | bytes 8388608 | tf_op jit(solution)/shard_map/all_to_all | solution.py:79
  191.9 0.0 reduce-scatter.3.cloned.1.call-start
  192.0 21.1 %copy.73 = f32[1024,8,1,256]{0,3,1,2:T(8,128)} copy(f32[1024,8,1,256]{3,2,1,0:T(1,128)} %get-tuple-element.41) | data formatting | bytes 16777216
  213.1 8.9 %broadcast_multiply_fusion.1 = f32[1024,8,1,256]{0,3,1,2:T(8,128)} fusion(f32[1024,8,1,256]{0,3,1,2:T(8,128)} %copy.73, f32[]{:T(128)} %bitcast.7), kind=kLoop, calls=%fused_computation.7 | loop fusion | flops 2097152 | bytes 16777220 | tf_op jit(solution)/shard_map/mul | solution.py:88
  222.0 62.4 %all-to-all-done.1 = bf16[4,256,8,256]{3,2,1,0:T(8,128)(2,1)} async-done(((bf16[4,256,8,256]{3,2,1,0:T(8,128)(2,1)}), bf16[4,256,8,256]{3,2,1,0:T(8,128)(2,1)}, u32[]{:S(2)}, u32[]{:S(2)}) %all-to-all-start.1) | async-done | bytes 4194336 | tf_op jit(solution)/shard_map/all_to_all | solution.py:79
  284.4 5.6 %copy.75 = bf16[128,8,8,256]{3,1,2,0:T(8,128)(2,1)} copy(bf16[128,8,8,256]{3,2,1,0:T(8,128)(2,1)} %bitcast.17) | data formatting | bytes 8388608
  290.0 0.0 all-gather.3.cloned.1.call-done
  290.0 10.6 %bitcast_add_fusion.1 = f32[1024,2048]{0,1:T(8,128)} fusion(f32[1024,8,1,256]{0,3,1,2:T(8,128)} %broadcast_multiply_fusion.1, bf16[1024,1024]{1,0:T(8,128)(2,1)S(1)} %copy-done, bf16[1024,2048]{1,0:T(8,128)(2,1)} %bitcast.45, f32[1024]{0:T(1024)S(1)} %bitcast.47), kind=kOutput, calls=%fused_computation.3 | convolution fusion | flops 4303355904 | bytes 23072768 | tf_op jit(solution)/shard_map/dot_general | solution.py:85
  300.5 0.0 copy-start.1
  300.5 0.0 reduce-scatter.3.cloned.1.call-update
  300.6 0.3 all-gather.5.cloned.1.call-start
  300.8 0.9 copy-done.1
  301.8 1.3 copy.64
  303.1 2.9 copy.66
  306.1 2.9 copy.57
  309.0 0.0 copy-start.2
  309.0 3.3 copy.65
  312.3 59.0 %reduce-scatter.3.cloned.1.call-done = f32[1024,256]{0,1:T(8,128)} async-done(((f32[1024,2048]{0,1:T(8,128)}), f32[1024,256]{0,1:T(8,128)}) %reduce-scatter.3.cloned.1.call-update) | async-done | bytes 1048592 | tf_op jit(solution)/shard_map/reduce_scatter | solution.py:89
  371.3 0.0 copy-done.2
  371.3 6.2 %divide_subtract_fusion = (f32[1024,512]{0,1:T(8,128)}, f32[1024,512]{0,1:T(8,128)}, f32[1024,512]{0,1:T(8,128)}, f32[1024,512]{0,1:T(8,128)}) fusion(f32[1024,512]{0,1:T(8,128)} %copy.66, f32[]{:T(128)S(6)} %sub.22, f32[]{:T(128)S(6)} %sub.21, bf16[1024,512]{0,1:T(8,128)(2,1)S(1)} %copy-done.2, f32[]{:T(128)S(6)} %mul.117, ...), kind=kLoop, calls=%fused_computation.11 | loop fusion | flops 9437184 | bytes 17825804 | tf_op jit(solution)/shard_map/sub | solution.py:101
  377.4 0.0 all-gather.5.cloned.1.call-update
  377.5 16.1 %broadcast_select_fusion = bf16[2,1024,4096]{2,1,0:T(8,128)(2,1)} fusion(bf16[2,1024,4096]{2,1,0:T(8,128)(2,1)} %param.19, pred[2]{0:T(512)(128)(4,1)S(1)} %broadcast_compare_fusion, bf16[1024,4096]{1,0:T(8,128)(2,1)} %all-gather.3.cloned.1.call-done), kind=kLoop, calls=%fused_computation.1 | loop fusion | flops 8388608 | bytes 41943040 | tf_op jit(solution)/shard_map/jit(_where)/select_n | solution.py:91
  393.6 2.9 copy.67
  396.5 2.9 copy.68
  399.3 2.9 copy.69
  402.2 2.9 copy.70
  405.1 62.2 %all-gather.5.cloned.1.call-done = f32[1024,4096]{0,1:T(8,128)} async-done(((f32[1024,512]{0,1:T(8,128)}), f32[1024,4096]{0,1:T(8,128)}) %all-gather.5.cloned.1.call-update) | async-done | bytes 16777232 | tf_op jit(solution)/shard_map/all_gather | solution.py:102
  467.3 17.4 %copy.71 = f32[1024,4096]{1,0:T(8,128)} copy(f32[1024,4096]{0,1:T(8,128)} %all-gather.5.cloned.1.call-done) | data formatting | bytes 33554432
  (4 shorter events, 0.0 us)
Async XLA Ops:
  7.2 1.6 copy-start
  7.2 282.8 %all-gather.3.cloned.1.call-start = ((), (), s32[]{:S(2)}) async-start(), calls=%async_computation.6 | async-start | bytes 9437184 | tf_op jit(solution)/shard_map/all_gather | solution.py:58
  52.7 6.4 %copy-start.5 = (s32[2]{0:T(128)S(1)}, s32[2]{0:T(128)}, u32[]{:S(2)}) copy-start(s32[2]{0:T(128)} %param.20) | copy-start | bytes 28
  52.8 6.5 %copy-start.4 = (f32[16]{0:T(128)S(1)}, f32[16]{0:T(128)}, u32[]{:S(2)}) copy-start(f32[16]{0:T(128)} %param.21) | copy-start | bytes 196
  52.8 97.7 %all-to-all-start.3 = ((bf16[4,256,8,256]{3,2,1,0:T(8,128)(2,1)}), bf16[4,256,8,256]{3,2,1,0:T(8,128)(2,1)}, u32[]{:S(2)}, u32[]{:S(2)}) async-start(bf16[4,256,8,256]{3,2,1,0:T(8,128)(2,1)} %broadcast_in_dim.76), calls=%async_computation.4 | async-start | bytes 8388608 | tf_op jit(solution)/shard_map/all_to_all | solution.py:79
  117.9 20.6 %copy-start.3 = (s32[1,256]{1,0:T(1,128)S(1)}, s32[1,256]{1,0:T(1,128)}, u32[]{:S(2)}) copy-start(s32[1,256]{1,0:T(1,128)} %param.14) | copy-start | bytes 3076
  151.1 19.7 %all-to-all-start.2 = ((f32[4,1,256]{2,1,0:T(1,128)}), f32[4,1,256]{2,1,0:T(1,128)S(1)}, u32[]{:S(2)}, u32[]{:S(2)}) async-start(f32[4,1,256]{2,1,0:T(1,128)} %broadcast_in_dim.72), calls=%async_computation.2 | async-start | bytes 8192 | tf_op jit(solution)/shard_map/all_to_all | solution.py:54
  154.3 157.9 %reduce-scatter.5.cloned.1.call-start = ((), (), s32[]{:S(2)}) async-start(), calls=%async_computation.8 | async-start | bytes 9437184 | tf_op jit(solution)/shard_map/reduce_scatter | solution.py:89
  186.7 97.7 %all-to-all-start.1 = ((bf16[4,256,8,256]{3,2,1,0:T(8,128)(2,1)}), bf16[4,256,8,256]{3,2,1,0:T(8,128)(2,1)}, u32[]{:S(2)}, u32[]{:S(2)}) async-start(bf16[4,256,8,256]{3,2,1,0:T(8,128)(2,1)} %broadcast_in_dim.69), calls=%async_computation.1 | async-start | bytes 8388608 | tf_op jit(solution)/shard_map/all_to_all | solution.py:79
  191.9 179.3 %reduce-scatter.3.cloned.1.call-start = ((), (), s32[]{:S(2)}) async-start(), calls=%async_computation.7 | async-start | bytes 9437184 | tf_op jit(solution)/shard_map/reduce_scatter | solution.py:89
  300.5 1.2 copy-start.1
  300.6 166.8 %all-gather.5.cloned.1.call-start = ((), (), s32[]{:S(2)}) async-start(), calls=%async_computation.9 | async-start | bytes 18874368 | tf_op jit(solution)/shard_map/all_gather | solution.py:102
  309.0 62.3 %copy-start.2 = (bf16[1024,512]{0,1:T(8,128)(2,1)S(1)}, bf16[1024,512]{0,1:T(8,128)(2,1)}, u32[]{:S(2)}) copy-start(bf16[1024,512]{0,1:T(8,128)(2,1)} %copy.64) | copy-start | bytes 3145732
Sparse Core Ops, SparseCore 0:
  9.9 58.5 all-gather.2
  182.7 72.6 reduce-scatter.4
  300.7 70.5 reduce-scatter.2
  377.6 89.7 all-gather.4

commit v6 on v3

--- a/solution.py
+++ b/solution.py
@@ -37,13 +37,24 @@
 
         blocks = cotangents.reshape(n_fsdp, tok, out_local)
         partial_gram = jnp.einsum("ati,asi->ats", blocks, blocks, preferred_element_type=jnp.float32)
-        received = lax.all_to_all(partial_gram, "fsdp", 0, 0, tiled=True)
+        me = lax.axis_index("fsdp")
+        cotan_gram = lax.dynamic_index_in_dim(partial_gram, me, axis=0, keepdims=False)
+        for k in range(1, n_fsdp):
+            to_right = lax.dynamic_index_in_dim(
+                partial_gram, jnp.minimum(me + k, n_fsdp - 1), axis=0, keepdims=False
+            )
+            to_left = lax.dynamic_index_in_dim(
+                partial_gram, jnp.maximum(me - k, 0), axis=0, keepdims=False
+            )
+            cotan_gram = cotan_gram + lax.ppermute(
+                to_right, "fsdp", [(f, f + k) for f in range(n_fsdp - k)]
+            )
+            cotan_gram = cotan_gram + lax.ppermute(
+                to_left, "fsdp", [(f, f - k) for f in range(k, n_fsdp)]
+            )
 
-        gather_in, received = lax.optimization_barrier((activations, received))
+        gather_in, cotan_gram = lax.optimization_barrier((activations, cotan_gram))
         full_act = lax.all_gather(gather_in, "fsdp", axis=0, tiled=True)
-        cotan_gram = received[0]
-        for part in range(1, n_fsdp):
-            cotan_gram = cotan_gram + received[part]
         input_gram = lax.dot_general(
             activations, activations, (((1,), (1,)), ((), ())), preferred_element_type=jnp.float32
         )

time: 451 us -> 462 us (1.024)
  blocking collectives: 32.1 us -> 0 us
  starting transfers between devices: 8.85 us -> 32.4 us
  local copies, waits for them, and re-layouts: 104 us -> 112 us
  waiting for transfers between devices: 240 us -> 248 us
    all_to_all x1 -> x0, blocking collectives: 32.1 us -> none  [body(): received = lax.all_to_all(partial_gram, 'fsdp', 0, 0, tiled=True)]
    ppermute x0 -> x6, starting transfers between devices: none -> 23.6 us  [the longest x3 19.7 us: body(): lax.ppermute(to_right, 'fsdp', [(f, f + k) for f in range(n_fsdp - k)])]
    squeeze x0 -> x8, local copies, waits for them, and re-layouts: none -> 10.2 us  [the longest x4 4.93 us: body(): lax.dynamic_index_in_dim(partial_gram, jnp.minimum(me + k, n_fsdp - 1), a...]
    ppermute x0 -> x6, waiting for transfers between devices: none -> 8.5 us  [the longest x3 8.49 us: body(): lax.ppermute(to_left, 'fsdp', [(f, f - k) for f in range(k, n_fsdp)])]
    unnamed x31 -> x35, local copies, waits for them, and re-layouts: 61.9 us -> 62.1 us
  transfers between devices with their start and end apart: 5 -> 11, of which waited for: 4 -> 6; matrix products, arithmetic and copies ran while one was open for 23% -> 24% of each run, Pallas kernels for 0% -> 0%
where the time goes in v6:
time: 462 us; the launch traced here: 460 us
  waiting for transfers between devices  248 us (54%)
  local copies, waits for them, and re-layouts  112 us (24%)
  starting transfers between devices  32.4 us (7%)
  matrix products  26.3 us (6%)
  other arithmetic  25.6 us (6%)
  between operations  15.4 us (3%)
    reduce_scatter x1, waiting for transfers between devices, body(): lax.psum_scatter(gradient + noise_scale * history_part, 'dp', scatter_dim...  105 us
    all_to_all x1, waiting for transfers between devices, body(): lax.all_to_all(jnp.broadcast_to(fresh_noise[None], (n_dp,) + fresh_noise....  77.7 us
    unnamed x35, local copies, waits for them, and re-layouts  62.1 us
    all_gather x1, waiting for transfers between devices, body(): gathered_weights = lax.all_gather(new_weights, 'dp', axis=1, tiled=True)  53 us
    dot_general x1, matrix products, body(): lax.dot_general(cotangents, scaled, (((0,), (0,)), ((), ())), preferred_e...  22.3 us
    ppermute x3, starting transfers between devices, body(): lax.ppermute(to_right, 'fsdp', [(f, f + k) for f in range(n_fsdp - k)])  19.7 us
    select_n x1, other arithmetic, body(): jnp.where((slot_ids == target)[:, None, None], full_fresh[None], history)  15.8 us
    slice x1, local copies, waits for them, and re-layouts, body(): history[position].astype(jnp.float32)  11.8 us
  transfers between devices with their start and end apart: 11, of which 6 were waited for; matrix products, arithmetic and copies ran while one was open for 24% of the time, Pallas kernels for 0%

profile of v6, /device:TPU:0, one launch (start us, length us, event | category | flops | bytes accessed | tf_op | source)
XLA Modules:
  0.0 460.1 jit_solution(12407802142575094647)
XLA Ops:
  7.2 0.0 copy-start
  7.2 0.0 all-gather.3.cloned.1.call-start
  7.2 1.5 copy-done
  8.8 0.7 fusion.8
  9.5 1.2 dynamic-slice_bitcast_fusion.5
  10.7 1.1 copy.86
  11.8 5.0 %collective-permute-start = (f32[256,256]{0,1:T(8,128)S(1)}, f32[256,256]{0,1:T(8,128)S(1)}, u32[]{:S(2)}, u32[]{:S(2)}) collective-permute-start(f32[256,256]{0,1:T(8,128)S(1)} %copy.86), channel_id=1, source_target_pairs={{0,1},{1,2},{2,3},{4,5},{5,6},{6,7},{8,9},{9,10},{10,11},{12,13},{... | collective-permute-start | bytes 786440 | tf_op jit(solution)/shard_map/ppermute | solution.py:49
  16.8 1.8 copy.88
  18.6 1.3 collective-permute-start.1
  19.9 1.8 copy.89
  21.7 6.2 %collective-permute-start.2 = (f32[256,256]{0,1:T(8,128)}, f32[256,256]{0,1:T(8,128)}, u32[]{:S(2)}, u32[]{:S(2)}) collective-permute-start(f32[256,256]{0,1:T(8,128)} %copy.89), channel_id=1, source_target_pairs={{0,2},{1,3},{4,6},{5,7},{8,10},{9,11},{12,14},{13,15},{16,18},{17,... | collective-permute-start | bytes 786440 | tf_op jit(solution)/shard_map/ppermute | solution.py:49
  27.9 1.8 copy.90
  29.7 1.3 collective-permute-start.3
  31.0 0.8 copy.91
  31.8 8.5 %collective-permute-start.4 = (f32[256,256]{0,1:T(8,128)}, f32[256,256]{0,1:T(8,128)}, u32[]{:S(2)}, u32[]{:S(2)}) collective-permute-start(f32[256,256]{0,1:T(8,128)} %copy.91), channel_id=1, source_target_pairs={{0,3},{4,7},{8,11},{12,15},{16,19},{20,23},{24,27},{28,31}} | collective-permute-start | bytes 786440 | tf_op jit(solution)/shard_map/ppermute | solution.py:49
  40.3 0.8 copy.92
  41.2 0.0 collective-permute-done
  41.2 1.3 collective-permute-start.5
  42.5 0.8 copy.87
  43.3 0.0 collective-permute-done.1
  43.3 0.0 collective-permute-done.2
  43.3 2.3 collective-permute-done.3
  45.6 0.0 collective-permute-done.4
  45.6 6.2 %collective-permute-done.5 = f32[256,256]{0,1:T(8,128)} collective-permute-done((f32[256,256]{0,1:T(8,128)}, f32[256,256]{0,1:T(8,128)}, u32[]{:S(2)}, u32[]{:S(2)}) %collective-permute-start.5) | collective-permute-done | bytes 262176 | tf_op jit(solution)/shard_map/ppermute | solution.py:52
  51.8 1.5 add_add_fusion
  53.4 0.0 all-gather.3.cloned.1.call-update
  53.4 4.0 broadcast_in_dim.60
  57.4 5.3 %all-to-all-start = ((bf16[8,1024,512]{2,1,0:T(8,128)(2,1)}), bf16[8,1024,512]{2,1,0:T(8,128)(2,1)}, u32[]{:S(2)}, u32[]{:S(2)}) async-start(bf16[8,1024,512]{2,1,0:T(8,128)(2,1)} %broadcast_in_dim.60), calls=%async_computation | async-start | bytes 16777216 | tf_op jit(solution)/shard_map/all_to_all | solution.py:70
  63.4 0.2 fusion.3
  63.6 3.3 fusion.9
  66.9 0.0 copy-start.9
  66.9 11.8 %fusion.6 = (bf16[1,1024,4096]{2,1,0:T(8,128)(2,1)}, bf16[1,1024,4096]{2,1,0:T(8,128)(2,1)}) fusion(bf16[2,1024,4096]{2,1,0:T(8,128)(2,1)} %param.19), kind=kLoop, calls=%fused_computation.30 | loop fusion | bytes 33554432 | tf_op jit(solution)/shard_map/slice | solution.py:84
  78.7 0.1 fusion.1
  78.9 0.2 fusion.2
  79.0 77.7 %all-to-all-done = bf16[8,1024,512]{2,1,0:T(8,128)(2,1)} async-done(((bf16[8,1024,512]{2,1,0:T(8,128)(2,1)}), bf16[8,1024,512]{2,1,0:T(8,128)(2,1)}, u32[]{:S(2)}, u32[]{:S(2)}) %all-to-all-start) | async-done | bytes 8388640 | tf_op jit(solution)/shard_map/all_to_all | solution.py:70
  156.7 0.6 broadcast_in_dim.63
  157.3 3.2 all-to-all-start.1
  160.6 0.0 reduce-scatter.2.cloned.1.call-start
  160.6 0.6 fusion.7
  161.2 11.9 %copy.105 = bf16[1,1024,4096]{1,2,0:T(8,128)(2,1)} copy(bf16[1,1024,4096]{2,1,0:T(8,128)(2,1)} %get-tuple-element.47) | data formatting | bytes 16777216
  173.1 12.0 %copy.106 = bf16[1,1024,4096]{1,2,0:T(8,128)(2,1)} copy(bf16[1,1024,4096]{2,1,0:T(8,128)(2,1)} %get-tuple-element.48) | data formatting | bytes 16777216
  185.7 11.4 %copy.93 = bf16[8,1024,512]{1,2,0:T(8,128)(2,1)} copy(bf16[8,1024,512]{2,1,0:T(8,128)(2,1)} %all-to-all-done) | data formatting | bytes 16777216 | tf_op jit(solution)/shard_map/all_to_all | solution.py:70
  197.1 4.3 all-gather.3.cloned.1.call-done
  201.5 0.0 all-to-all-done.1
  201.5 22.3 %bitcast_add_fusion = f32[1024,4096]{0,1:T(8,128)} fusion(bf16[1,1024,4096]{1,2,0:T(8,128)(2,1)} %copy.106, bf16[1,1024,4096]{1,2,0:T(8,128)(2,1)} %copy.105, bf16[1024,1024]{1,0:T(8,128)(2,1)S(1)} %copy-done, bf16[1024,4096]{1,0:T(8,128)(2,1)} %all-gather.3.cloned.1.call-done, f32[]{:T(128)} %bitcast.16, f32[]{:T(128)} %bitcast.15, f32[]{:T(128)} %bitcast.13, ...), kind=kOutput, calls=%fused_computation | convolution fusion | flops 8631877632 | bytes 44044300 | tf_op jit(solution)/shard_map/dot_general | solution.py:88
  223.7 0.0 reduce-scatter.2.cloned.1.call-update
  223.7 0.2 all-gather.5.cloned.1.call-start
  224.0 1.3 copy.96
  225.4 1.9 copy.85
  227.4 2.9 copy.97
  230.3 3.4 copy.98
  233.7 104.6 %reduce-scatter.2.cloned.1.call-done = f32[1024,512]{0,1:T(8,128)} async-done(((f32[1024,4096]{0,1:T(8,128)}), f32[1024,512]{0,1:T(8,128)}) %reduce-scatter.2.cloned.1.call-update) | async-done | bytes 2097168 | tf_op jit(solution)/shard_map/reduce_scatter | solution.py:96
  338.3 0.0 copy-done.5
  338.3 7.8 %divide_subtract_fusion = (f32[1024,512]{0,1:T(8,128)}, f32[1024,512]{0,1:T(8,128)}, f32[1024,512]{0,1:T(8,128)}, f32[1024,512]{0,1:T(8,128)}) fusion(f32[1024,512]{0,1:T(8,128)} %copy.98, f32[]{:T(128)S(6)} %sub.34, f32[]{:T(128)S(6)} %sub.33, f32[1024,512]{0,1:T(8,128)} %reduce-scatter.2.cloned.1.call-done, bf16[1024,512]{0,1:T(8,128)(2,1)S(1)} %copy-done.5, ...), kind=kLoop, calls=%fused_computation.4 | loop fusion | flops 8912896 | bytes 17825804 | tf_op jit(solution)/shard_map/sub | solution.py:108
  346.1 0.0 all-gather.5.cloned.1.call-update
  346.1 11.5 %copy.99 = bf16[1024,4096]{1,0:T(8,128)(2,1)} copy(bf16[1024,4096]{0,1:T(8,128)(2,1)} %bitcast.41) | data formatting | bytes 16777216 | tf_op jit(solution)/shard_map/optimization_barrier | solution.py:86
  357.6 15.8 %broadcast_select_fusion = bf16[2,1024,4096]{2,1,0:T(8,128)(2,1)} fusion(bf16[2,1024,4096]{2,1,0:T(8,128)(2,1)} %param.19, pred[2]{0:T(512)(128)(4,1)S(1)} %broadcast_compare_fusion, bf16[1024,4096]{1,0:T(8,128)(2,1)} %copy.99), kind=kLoop, calls=%fused_computation.2 | loop fusion | flops 8388608 | bytes 41943040 | tf_op jit(solution)/shard_map/jit(_where)/select_n | solution.py:94
  373.5 1.8 copy.100
  375.3 2.9 copy.101
  378.1 3.0 copy.102
  381.2 1.8 copy.103
  383.0 53.0 %all-gather.5.cloned.1.call-done = f32[1024,4096]{0,1:T(8,128)} async-done(((f32[1024,512]{0,1:T(8,128)}), f32[1024,4096]{0,1:T(8,128)}) %all-gather.5.cloned.1.call-update) | async-done | bytes 16777232 | tf_op jit(solution)/shard_map/all_gather | solution.py:109
  436.0 17.6 %copy.104 = f32[1024,4096]{1,0:T(8,128)} copy(f32[1024,4096]{0,1:T(8,128)} %all-gather.5.cloned.1.call-done) | data formatting | bytes 33554432
  453.6 0.0 copy-done.1
  (22 shorter events, 0.1 us)
Async XLA Ops:
  7.2 1.6 copy-start
  7.2 194.3 %all-gather.3.cloned.1.call-start = ((), (), s32[]{:S(2)}) async-start(), calls=%async_computation.3 | async-start | bytes 10485760 | tf_op jit(solution)/shard_map/all_gather | solution.py:57
  10.7 20.3 %copy-start.7 = (f32[256,256]{1,0:T(8,128)S(1)}, f32[256,256]{1,0:T(8,128)}, u32[]{:S(2)}) copy-start(f32[256,256]{1,0:T(8,128)} %get-tuple-element.52) | copy-start | bytes 786436
  10.7 29.7 %copy-start.6 = (f32[256,256]{1,0:T(8,128)S(1)}, f32[256,256]{1,0:T(8,128)}, u32[]{:S(2)}) copy-start(f32[256,256]{1,0:T(8,128)} %get-tuple-element.51) | copy-start | bytes 786436
  11.8 29.4 %collective-permute-start = (f32[256,256]{0,1:T(8,128)S(1)}, f32[256,256]{0,1:T(8,128)S(1)}, u32[]{:S(2)}, u32[]{:S(2)}) collective-permute-start(f32[256,256]{0,1:T(8,128)S(1)} %copy.86), channel_id=1, source_target_pairs={{0,1},{1,2},{2,3},{4,5},{5,6},{6,7},{8,9},{9,10},{10,11},{12,13},{... | collective-permute-start | bytes 786440 | tf_op jit(solution)/shard_map/ppermute | solution.py:49
  18.6 24.7 %collective-permute-start.1 = (f32[256,256]{0,1:T(8,128)}, f32[256,256]{0,1:T(8,128)}, u32[]{:S(2)}, u32[]{:S(2)}) collective-permute-start(f32[256,256]{0,1:T(8,128)} %copy.88), channel_id=1, source_target_pairs={{1,0},{2,1},{3,2},{5,4},{6,5},{7,6},{9,8},{10,9},{11,10},{13,12},{... | collective-permute-start | bytes 786440 | tf_op jit(solution)/shard_map/ppermute | solution.py:52
  21.7 21.7 %collective-permute-start.2 = (f32[256,256]{0,1:T(8,128)}, f32[256,256]{0,1:T(8,128)}, u32[]{:S(2)}, u32[]{:S(2)}) collective-permute-start(f32[256,256]{0,1:T(8,128)} %copy.89), channel_id=1, source_target_pairs={{0,2},{1,3},{4,6},{5,7},{8,10},{9,11},{12,14},{13,15},{16,18},{17,... | collective-permute-start | bytes 786440 | tf_op jit(solution)/shard_map/ppermute | solution.py:49
  29.7 15.9 %collective-permute-start.3 = (f32[256,256]{0,1:T(8,128)}, f32[256,256]{0,1:T(8,128)}, u32[]{:S(2)}, u32[]{:S(2)}) collective-permute-start(f32[256,256]{0,1:T(8,128)} %copy.90), channel_id=1, source_target_pairs={{2,0},{3,1},{6,4},{7,5},{10,8},{11,9},{14,12},{15,13},{18,16},{19,... | collective-permute-start | bytes 786440 | tf_op jit(solution)/shard_map/ppermute | solution.py:52
  31.8 13.8 %collective-permute-start.4 = (f32[256,256]{0,1:T(8,128)}, f32[256,256]{0,1:T(8,128)}, u32[]{:S(2)}, u32[]{:S(2)}) collective-permute-start(f32[256,256]{0,1:T(8,128)} %copy.91), channel_id=1, source_target_pairs={{0,3},{4,7},{8,11},{12,15},{16,19},{20,23},{24,27},{28,31}} | collective-permute-start | bytes 786440 | tf_op jit(solution)/shard_map/ppermute | solution.py:49
  41.2 1.3 copy-start.8
  41.2 10.6 %collective-permute-start.5 = (f32[256,256]{0,1:T(8,128)}, f32[256,256]{0,1:T(8,128)}, u32[]{:S(2)}, u32[]{:S(2)}) collective-permute-start(f32[256,256]{0,1:T(8,128)} %copy.92), channel_id=1, source_target_pairs={{3,0},{7,4},{11,8},{15,12},{19,16},{23,20},{27,24},{31,28}} | collective-permute-start | bytes 786440 | tf_op jit(solution)/shard_map/ppermute | solution.py:52
  43.3 10.1 %copy-start.4 = (bf16[1024,512]{1,0:T(8,128)(2,1)S(1)}, bf16[1024,512]{1,0:T(8,128)(2,1)}, u32[]{:S(2)}) copy-start(bf16[1024,512]{1,0:T(8,128)(2,1)} %param.18) | copy-start | bytes 3145732
  57.4 6.0 %copy-start.11 = (s32[2]{0:T(128)S(1)}, s32[2]{0:T(128)}, u32[]{:S(2)}) copy-start(s32[2]{0:T(128)} %param.20) | copy-start | bytes 28
  57.4 6.0 %copy-start.10 = (f32[16]{0:T(128)S(1)}, f32[16]{0:T(128)}, u32[]{:S(2)}) copy-start(f32[16]{0:T(128)} %param.21) | copy-start | bytes 196
  57.4 99.3 %all-to-all-start = ((bf16[8,1024,512]{2,1,0:T(8,128)(2,1)}), bf16[8,1024,512]{2,1,0:T(8,128)(2,1)}, u32[]{:S(2)}, u32[]{:S(2)}) async-start(bf16[8,1024,512]{2,1,0:T(8,128)(2,1)} %broadcast_in_dim.60), calls=%async_computation | async-start | bytes 16777216 | tf_op jit(solution)/shard_map/all_to_all | solution.py:70
  66.9 11.8 %copy-start.9 = (s32[1,256]{1,0:T(1,128)S(1)}, s32[1,256]{1,0:T(1,128)}, u32[]{:S(2)}) copy-start(s32[1,256]{1,0:T(1,128)} %param.14) | copy-start | bytes 3076
  157.3 44.1 %all-to-all-start.1 = ((f32[4,1,256]{2,1,0:T(1,128)}), f32[4,1,256]{2,1,0:T(1,128)S(1)}, u32[]{:S(2)}, u32[]{:S(2)}) async-start(f32[4,1,256]{2,1,0:T(1,128)} %broadcast_in_dim.63), calls=%async_computation.1 | async-start | bytes 8192 | tf_op jit(solution)/shard_map/all_to_all | solution.py:66
  160.6 177.7 %reduce-scatter.2.cloned.1.call-start = ((), (), s32[]{:S(2)}) async-start(), calls=%async_computation.4 | async-start | bytes 18874368 | tf_op jit(solution)/shard_map/reduce_scatter | solution.py:96
  223.7 212.2 %all-gather.5.cloned.1.call-start = ((), (), s32[]{:S(2)}) async-start(), calls=%async_computation.5 | async-start | bytes 18874368 | tf_op jit(solution)/shard_map/all_gather | solution.py:109
  230.3 108.0 %copy-start.5 = (bf16[1024,512]{0,1:T(8,128)(2,1)S(1)}, bf16[1024,512]{0,1:T(8,128)(2,1)}, u32[]{:S(2)}) copy-start(bf16[1024,512]{0,1:T(8,128)(2,1)} %copy.96) | copy-start | bytes 3145732
  357.6 15.8 %copy-start.2 = (f32[1024,512]{0,1:T(8,128)S(1)}, f32[1024,512]{0,1:T(8,128)}, u32[]{:S(2)}) copy-start(f32[1024,512]{0,1:T(8,128)} %get-tuple-element.44) | copy-start | bytes 6291460
  378.1 3.0 copy-start.3
  436.0 17.6 %copy-start.1 = (bf16[1024,1024]{1,0:T(8,128)(2,1)S(1)}, bf16[1024,1024]{1,0:T(8,128)(2,1)}, u32[]{:S(2)}) copy-start(bf16[1024,1024]{1,0:T(8,128)(2,1)} %param.13) | copy-start | bytes 6291460
Sparse Core Ops, SparseCore 0:
  53.5 147.8 all-gather.2
  223.9 114.3 reduce-scatter.1
  346.2 89.7 all-gather.4

commit v7 on v3

--- a/solution.py
+++ b/solution.py
@@ -2,6 +2,7 @@
 import jax.numpy as jnp
 from jax import lax
 from jax.sharding import PartitionSpec as P
+from jax.experimental.layout import Layout, with_layout_constraint
 
 D_IN = 4096
 D_OUT = 4096
@@ -95,7 +96,11 @@
         corrected_first = new_first / (1.0 - jnp.power(jnp.float32(0.9), step_float))
         corrected_second = new_second / (1.0 - jnp.power(jnp.float32(0.999), step_float))
         new_weights = weights - 0.002 * corrected_first / (jnp.sqrt(corrected_second) + 1e-08)
-        gathered_weights = lax.all_gather(new_weights, "dp", axis=1, tiled=True)
+        row_major = Layout(major_to_minor=(0, 1))
+        gathered_weights = with_layout_constraint(
+            lax.all_gather(with_layout_constraint(new_weights, row_major), "dp", axis=1, tiled=True),
+            row_major,
+        )
         return (new_weights, new_first, new_second, noisy_mean, gathered_weights, new_history)
 
     return body

time: 451 us -> 444 us (0.984)
  local copies, waits for them, and re-layouts: 104 us -> 41.8 us
  waiting for transfers between devices: 240 us -> 295 us
    unnamed x31 -> x15, local copies, waits for them, and re-layouts: 61.9 us -> 13.4 us
    all_gather x1, waiting for transfers between devices: 5.37 us -> 28.9 us  [body(): full_act = lax.all_gather(gather_in, 'fsdp', axis=0, tiled=True)]
    slice x1 -> x0, local copies, waits for them, and re-layouts: 12.8 us -> none  [body(): history[position].astype(jnp.float32)]
    all_to_all x1, waiting for transfers between devices: 78.1 us -> 89.2 us  [body(): lax.all_to_all(jnp.broadcast_to(fresh_noise[None], (n_dp,) + fresh_noise....]
    all_gather x1, waiting for transfers between devices: 52.4 us -> 62.5 us  [body(): lax.all_gather(with_layout_constraint(new_weights, row_major), 'dp', axis...]
    reduce_scatter x1, waiting for transfers between devices: 105 us -> 114 us  [body(): lax.psum_scatter(gradient + noise_scale * history_part, 'dp', scatter_dim...]
  transfers between devices with their start and end apart: 5 -> 5, of which waited for: 4 -> 4; matrix products, arithmetic and copies ran while one was open for 23% -> 11% of each run, Pallas kernels for 0% -> 0%
where the time goes in v7:
time: 444 us
  waiting for transfers between devices  295 us (66%)
  local copies, waits for them, and re-layouts  41.8 us (9%)
  blocking collectives  32.1 us (7%)
  matrix products  27.2 us (6%)
  other arithmetic  23.5 us (5%)
  between operations  15.3 us (3%)
  starting transfers between devices  8.86 us (2%)
    reduce_scatter x1, waiting for transfers between devices, body(): lax.psum_scatter(gradient + noise_scale * history_part, 'dp', scatter_dim...  114 us
    all_to_all x1, waiting for transfers between devices, body(): lax.all_to_all(jnp.broadcast_to(fresh_noise[None], (n_dp,) + fresh_noise....  89.2 us
    all_gather x1, waiting for transfers between devices, body(): lax.all_gather(with_layout_constraint(new_weights, row_major), 'dp', axis...  62.5 us
    all_to_all x1, blocking collectives, body(): received = lax.all_to_all(partial_gram, 'fsdp', 0, 0, tiled=True)  32.1 us
    all_gather x1, waiting for transfers between devices, body(): full_act = lax.all_gather(gather_in, 'fsdp', axis=0, tiled=True)  28.9 us
    dot_general x1, matrix products, body(): lax.dot_general(cotangents, scaled, (((0,), (0,)), ((), ())), preferred_e...  22.7 us
    select_n x1, other arithmetic, body(): jnp.where((slot_ids == target)[:, None, None], full_fresh[None], history)  15.6 us
    unnamed x15, local copies, waits for them, and re-layouts  13.4 us
  transfers between devices with their start and end apart: 5, of which 4 were waited for; matrix products, arithmetic and copies ran while one was open for 11% of the time, Pallas kernels for 0%

profile of v7, /device:TPU:0, one launch (start us, length us, event | category | flops | bytes accessed | tf_op | source)
XLA Modules:
  0.0 443.5 jit_solution(329876365676123322)
XLA Ops:
  7.2 0.0 copy-start
  7.2 0.0 all-gather.3.cloned.1.call-start
  7.2 1.5 copy-done
  8.8 0.7 fusion.8
  9.5 0.0 copy-start.2
  9.5 32.1 %all_to_all.16 = f32[4,256,256]{2,1,0:T(8,128)} all-to-all(f32[4,256,256]{2,1,0:T(8,128)S(1)} %fusion.8), channel_id=1, replica_groups=mesh['dp'=8,'fsdp'=4] {'fsdp'}, dimensions={0} | all-to-all | bytes 2097152 | tf_op jit(solution)/shard_map/all_to_all | solution.py:41
  41.6 0.0 all-gather.3.cloned.1.call-update
  41.7 0.0 copy-done.2
  41.7 4.1 broadcast_in_dim.60
  45.8 0.0 copy-start.6
  45.8 0.0 copy-start.5
  45.8 0.0 copy-start.4
  45.8 5.3 %all-to-all-start.1 = ((bf16[8,1024,512]{2,1,0:T(8,128)(2,1)}), bf16[8,1024,512]{2,1,0:T(8,128)(2,1)}, u32[]{:S(2)}, u32[]{:S(2)}) async-start(bf16[8,1024,512]{2,1,0:T(8,128)(2,1)} %broadcast_in_dim.60), calls=%async_computation.1 | async-start | bytes 16777216 | tf_op jit(solution)/shard_map/all_to_all | solution.py:60
  51.8 0.0 copy-done.6
  51.8 0.0 copy-done.5
  51.8 0.2 fusion.4
  52.0 0.0 copy-done.4
  52.0 3.8 fusion.2
  55.7 0.2 fusion.3
  55.9 89.2 %all-to-all-done.1 = bf16[8,1024,512]{2,1,0:T(8,128)(2,1)} async-done(((bf16[8,1024,512]{2,1,0:T(8,128)(2,1)}), bf16[8,1024,512]{2,1,0:T(8,128)(2,1)}, u32[]{:S(2)}, u32[]{:S(2)}) %all-to-all-start.1) | async-done | bytes 8388640 | tf_op jit(solution)/shard_map/all_to_all | solution.py:60
  145.1 0.6 broadcast_in_dim.63
  145.7 3.2 all-to-all-start.2
  149.0 0.0 reduce-scatter.2.cloned.1.call-start
  149.0 0.6 fusion.7
  150.3 11.4 %copy.26 = bf16[8,1024,512]{1,2,0:T(8,128)(2,1)} copy(bf16[8,1024,512]{2,1,0:T(8,128)(2,1)} %all-to-all-done.1) | data formatting | bytes 16777216 | tf_op jit(solution)/shard_map/all_to_all | solution.py:60
  161.6 28.9 %all-gather.3.cloned.1.call-done = bf16[1024,4096]{1,0:T(8,128)(2,1)} async-done(((bf16[256,4096]{1,0:T(8,128)(2,1)}), bf16[1024,4096]{1,0:T(8,128)(2,1)}) %all-gather.3.cloned.1.call-update) | async-done | bytes 8388624 | tf_op jit(solution)/shard_map/all_gather | solution.py:44
  190.6 0.0 all-to-all-done.2
  190.6 22.7 %bitcast_add_fusion = f32[1024,4096]{1,0:T(8,128)} fusion(bf16[1024,1024]{1,0:T(8,128)(2,1)S(1)} %copy-done, bf16[1024,4096]{1,0:T(8,128)(2,1)} %all-gather.3.cloned.1.call-done, bf16[2,1024,4096]{2,1,0:T(8,128)(2,1)} %param.19, f32[]{:T(128)} %bitcast.10, f32[]{:T(128)} %bitcast.9, f32[]{:T(128)} %bitcast.7, f32[1024]{0:T(1024)S(1)} %bitcast.30), kind=kOutput, calls=%fused_computation | convolution fusion | flops 8631877632 | bytes 44044300 | tf_op jit(solution)/shard_map/dot_general | solution.py:78
  213.3 0.0 copy-start.3
  213.3 0.0 reduce-scatter.2.cloned.1.call-update
  213.3 0.2 all-gather.5.cloned.1.call-start
  213.7 114.1 %reduce-scatter.2.cloned.1.call-done = f32[1024,512]{1,0:T(8,128)} async-done(((f32[1024,4096]{1,0:T(8,128)}), f32[1024,512]{1,0:T(8,128)}) %reduce-scatter.2.cloned.1.call-update) | async-done | bytes 2097168 | tf_op jit(solution)/shard_map/reduce_scatter | solution.py:86
  327.7 0.0 copy-done.3
  327.7 7.5 %divide_subtract_fusion = (f32[1024,512]{1,0:T(8,128)}, f32[1024,512]{1,0:T(8,128)}, f32[1024,512]{1,0:T(8,128)}, f32[1024,512]{1,0:T(8,128)}) fusion(f32[1024,512]{1,0:T(8,128)S(1)} %copy-done.3, f32[]{:T(128)S(6)} %sub.22, f32[]{:T(128)S(6)} %sub.21, f32[1024,512]{1,0:T(8,128)} %reduce-scatter.2.cloned.1.call-done, bf16[1024,512]{1,0:T(8,128)(2,1)S(1)} %copy-done.2, ...), kind=kLoop, calls=%fused_computation.4 | loop fusion | flops 8912896 | bytes 17825804 | tf_op jit(solution)/shard_map/sub | solution.py:98
  335.2 0.0 all-gather.5.cloned.1.call-update
  335.3 11.7 %copy.29 = bf16[1024,4096]{1,0:T(8,128)(2,1)} copy(bf16[1024,4096]{0,1:T(8,128)(2,1)} %bitcast.29) | data formatting | bytes 16777216 | tf_op jit(solution)/shard_map/optimization_barrier | solution.py:76
  347.0 15.6 %broadcast_select_fusion = bf16[2,1024,4096]{2,1,0:T(8,128)(2,1)} fusion(bf16[2,1024,4096]{2,1,0:T(8,128)(2,1)} %param.19, pred[2]{0:T(512)(128)(4,1)S(1)} %broadcast_compare_fusion, bf16[1024,4096]{1,0:T(8,128)(2,1)} %copy.29), kind=kLoop, calls=%fused_computation.2 | loop fusion | flops 8388608 | bytes 41943040 | tf_op jit(solution)/shard_map/jit(_where)/select_n | solution.py:84
  362.6 62.5 %all-gather.5.cloned.1.call-done = f32[1024,4096]{1,0:T(8,128)} async-done(((f32[1024,512]{1,0:T(8,128)}), f32[1024,4096]{1,0:T(8,128)}) %all-gather.5.cloned.1.call-update) | async-done | bytes 16777232 | tf_op jit(solution)/shard_map/all_gather | solution.py:101
  425.1 0.0 copy-start.1
  425.1 11.9 %copy.35 = f32[1024,4096]{1,0:T(8,128)} copy(f32[1024,4096]{1,0:T(8,128)} %all-gather.5.cloned.1.call-done) | data formatting | bytes 33554432
  437.0 0.0 copy-done.1
  (3 shorter events, 0.0 us)
Async XLA Ops:
  7.2 1.6 copy-start
  7.2 183.4 %all-gather.3.cloned.1.call-start = ((), (), s32[]{:S(2)}) async-start(), calls=%async_computation.4 | async-start | bytes 10485760 | tf_op jit(solution)/shard_map/all_gather | solution.py:44
  9.5 32.1 %copy-start.2 = (bf16[1024,512]{1,0:T(8,128)(2,1)S(1)}, bf16[1024,512]{1,0:T(8,128)(2,1)}, u32[]{:S(2)}) copy-start(bf16[1024,512]{1,0:T(8,128)(2,1)} %param.18) | copy-start | bytes 3145732
  45.8 6.0 %copy-start.6 = (s32[2]{0:T(128)S(1)}, s32[2]{0:T(128)}, u32[]{:S(2)}) copy-start(s32[2]{0:T(128)} %param.20) | copy-start | bytes 28
  45.8 6.0 %copy-start.5 = (f32[16]{0:T(128)S(1)}, f32[16]{0:T(128)}, u32[]{:S(2)}) copy-start(f32[16]{0:T(128)} %param.21) | copy-start | bytes 196
  45.8 6.2 %copy-start.4 = (s32[1,256]{1,0:T(1,128)S(1)}, s32[1,256]{1,0:T(1,128)}, u32[]{:S(2)}) copy-start(s32[1,256]{1,0:T(1,128)} %param.14) | copy-start | bytes 3076
  45.8 99.4 %all-to-all-start.1 = ((bf16[8,1024,512]{2,1,0:T(8,128)(2,1)}), bf16[8,1024,512]{2,1,0:T(8,128)(2,1)}, u32[]{:S(2)}, u32[]{:S(2)}) async-start(bf16[8,1024,512]{2,1,0:T(8,128)(2,1)} %broadcast_in_dim.60), calls=%async_computation.1 | async-start | bytes 16777216 | tf_op jit(solution)/shard_map/all_to_all | solution.py:60
  145.7 44.8 %all-to-all-start.2 = ((f32[4,1,256]{2,1,0:T(1,128)}), f32[4,1,256]{2,1,0:T(1,128)S(1)}, u32[]{:S(2)}, u32[]{:S(2)}) async-start(f32[4,1,256]{2,1,0:T(1,128)} %broadcast_in_dim.63), calls=%async_computation.2 | async-start | bytes 8192 | tf_op jit(solution)/shard_map/all_to_all | solution.py:56
  149.0 178.7 %reduce-scatter.2.cloned.1.call-start = ((), (), s32[]{:S(2)}) async-start(), calls=%async_computation.5 | async-start | bytes 18874368 | tf_op jit(solution)/shard_map/reduce_scatter | solution.py:86
  213.3 114.4 %copy-start.3 = (f32[1024,512]{1,0:T(8,128)S(1)}, f32[1024,512]{1,0:T(8,128)}, u32[]{:S(2)}) copy-start(f32[1024,512]{1,0:T(8,128)} %param.15) | copy-start | bytes 6291460
  213.3 211.8 %all-gather.5.cloned.1.call-start = ((), (), s32[]{:S(2)}) async-start(), calls=%async_computation.6 | async-start | bytes 18874368 | tf_op jit(solution)/shard_map/all_gather | solution.py:101
  425.1 11.9 %copy-start.1 = (bf16[1024,1024]{1,0:T(8,128)(2,1)S(1)}, bf16[1024,1024]{1,0:T(8,128)(2,1)}, u32[]{:S(2)}) copy-start(bf16[1024,1024]{1,0:T(8,128)(2,1)} %param.13) | copy-start | bytes 6291460
Sparse Core Ops, SparseCore 0:
  41.8 148.7 all-gather.2
  213.4 114.2 reduce-scatter.1
  335.4 89.7 all-gather.4

commit v8 on v7

--- a/solution.py
+++ b/solution.py
@@ -87,20 +87,27 @@
             gradient + noise_scale * history_part, "dp", scatter_dimension=1, tiled=True
         )
         examples = EX_DEV * n_dp * n_fsdp
-        noisy_mean = (
-            combined + noise_scale * band_coefs[0] * fresh_noise.astype(jnp.float32)
-        ) / examples
-        new_first = 0.9 * first_moment + 0.1 * noisy_mean
-        new_second = 0.999 * second_moment + 0.001 * noisy_mean * noisy_mean
         step_float = step_value.astype(jnp.float32)
-        corrected_first = new_first / (1.0 - jnp.power(jnp.float32(0.9), step_float))
-        corrected_second = new_second / (1.0 - jnp.power(jnp.float32(0.999), step_float))
-        new_weights = weights - 0.002 * corrected_first / (jnp.sqrt(corrected_second) + 1e-08)
+        first_scale = 1.0 - jnp.power(jnp.float32(0.9), step_float)
+        second_scale = 1.0 - jnp.power(jnp.float32(0.999), step_float)
+
+        def adam(combined_in):
+            noisy = (
+                combined_in + noise_scale * band_coefs[0] * fresh_noise.astype(jnp.float32)
+            ) / examples
+            first = 0.9 * first_moment + 0.1 * noisy
+            second = 0.999 * second_moment + 0.001 * noisy * noisy
+            updated = weights - 0.002 * (first / first_scale) / (jnp.sqrt(second / second_scale) + 1e-08)
+            return noisy, first, second, updated
+
+        new_weights = adam(combined)[3]
         row_major = Layout(major_to_minor=(0, 1))
         gathered_weights = with_layout_constraint(
             lax.all_gather(with_layout_constraint(new_weights, row_major), "dp", axis=1, tiled=True),
             row_major,
         )
+        combined_late, new_weights = lax.optimization_barrier((combined, new_weights))
+        noisy_mean, new_first, new_second, _ = adam(combined_late)
         return (new_weights, new_first, new_second, noisy_mean, gathered_weights, new_history)
 
     return body

time: 444 us -> 443 us (level)
  waiting for transfers between devices: 295 us -> 290 us
    all_gather x1, waiting for transfers between devices: 62.5 us -> 58.1 us  [body(): lax.all_gather(with_layout_constraint(new_weights, row_major), 'dp', axis...]
    unnamed x15 -> x19, local copies, waits for them, and re-layouts: 13.4 us -> 13.4 us
  transfers between devices with their start and end apart: 5 -> 5, of which waited for: 4 -> 4; matrix products, arithmetic and copies ran while one was open for 11% -> 12% of each run, Pallas kernels for 0% -> 0%
where the time goes in v8:
time: 443 us; the launch traced here: 442 us
  waiting for transfers between devices  290 us (65%)
  local copies, waits for them, and re-layouts  41.8 us (9%)
  blocking collectives  32.1 us (7%)
  matrix products  27.2 us (6%)
  other arithmetic  26.4 us (6%)
  between operations  15.3 us (3%)
  starting transfers between devices  8.85 us (2%)
    reduce_scatter x1, waiting for transfers between devices, body(): lax.psum_scatter(gradient + noise_scale * history_part, 'dp', scatter_dim...  114 us
    all_to_all x1, waiting for transfers between devices, body(): lax.all_to_all(jnp.broadcast_to(fresh_noise[None], (n_dp,) + fresh_noise....  89.2 us
    all_gather x1, waiting for transfers between devices, body(): lax.all_gather(with_layout_constraint(new_weights, row_major), 'dp', axis...  58.1 us
    all_to_all x1, blocking collectives, body(): received = lax.all_to_all(partial_gram, 'fsdp', 0, 0, tiled=True)  32.1 us
    all_gather x1, waiting for transfers between devices, body(): full_act = lax.all_gather(gather_in, 'fsdp', axis=0, tiled=True)  28.9 us
    dot_general x1, matrix products, body(): lax.dot_general(cotangents, scaled, (((0,), (0,)), ((), ())), preferred_e...  22.7 us
    select_n x1, other arithmetic, body(): jnp.where((slot_ids == target)[:, None, None], full_fresh[None], history)  16.6 us
    unnamed x19, local copies, waits for them, and re-layouts  13.4 us
  transfers between devices with their start and end apart: 5, of which 4 were waited for; matrix products, arithmetic and copies ran while one was open for 12% of the time, Pallas kernels for 0%

profile of v8, /device:TPU:0, one launch (start us, length us, event | category | flops | bytes accessed | tf_op | source)
XLA Modules:
  0.0 441.9 jit_solution(15408619139069186363)
XLA Ops:
  7.2 0.0 copy-start
  7.2 0.0 all-gather.3.cloned.1.call-start
  7.2 1.5 copy-done
  8.8 0.7 fusion.9
  9.5 0.0 copy-start.2
  9.5 32.1 %all_to_all.16 = f32[4,256,256]{2,1,0:T(8,128)} all-to-all(f32[4,256,256]{2,1,0:T(8,128)S(1)} %fusion.9), channel_id=1, replica_groups=mesh['dp'=8,'fsdp'=4] {'fsdp'}, dimensions={0} | all-to-all | bytes 2097152 | tf_op jit(solution)/shard_map/all_to_all | solution.py:41
  41.6 0.0 all-gather.3.cloned.1.call-update
  41.7 0.0 copy-done.2
  41.7 4.1 broadcast_in_dim.60
  45.8 0.0 copy-start.8
  45.8 0.0 copy-start.7
  45.8 0.0 copy-start.6
  45.8 5.3 %all-to-all-start.1 = ((bf16[8,1024,512]{2,1,0:T(8,128)(2,1)}), bf16[8,1024,512]{2,1,0:T(8,128)(2,1)}, u32[]{:S(2)}, u32[]{:S(2)}) async-start(bf16[8,1024,512]{2,1,0:T(8,128)(2,1)} %broadcast_in_dim.60), calls=%async_computation.1 | async-start | bytes 16777216 | tf_op jit(solution)/shard_map/all_to_all | solution.py:60
  51.7 0.0 copy-done.8
  51.8 0.0 copy-done.7
  51.8 0.2 fusion.5
  52.0 0.0 copy-done.6
  52.0 3.7 fusion.3
  55.7 0.2 fusion.4
  55.9 89.2 %all-to-all-done.1 = bf16[8,1024,512]{2,1,0:T(8,128)(2,1)} async-done(((bf16[8,1024,512]{2,1,0:T(8,128)(2,1)}), bf16[8,1024,512]{2,1,0:T(8,128)(2,1)}, u32[]{:S(2)}, u32[]{:S(2)}) %all-to-all-start.1) | async-done | bytes 8388640 | tf_op jit(solution)/shard_map/all_to_all | solution.py:60
  145.1 0.6 broadcast_in_dim.63
  145.7 3.2 all-to-all-start.2
  149.0 0.0 reduce-scatter.2.cloned.1.call-start
  149.0 0.6 fusion.8
  150.3 11.4 %copy.26 = bf16[8,1024,512]{1,2,0:T(8,128)(2,1)} copy(bf16[8,1024,512]{2,1,0:T(8,128)(2,1)} %all-to-all-done.1) | data formatting | bytes 16777216 | tf_op jit(solution)/shard_map/all_to_all | solution.py:60
  161.6 28.9 %all-gather.3.cloned.1.call-done = bf16[1024,4096]{1,0:T(8,128)(2,1)} async-done(((bf16[256,4096]{1,0:T(8,128)(2,1)}), bf16[1024,4096]{1,0:T(8,128)(2,1)}) %all-gather.3.cloned.1.call-update) | async-done | bytes 8388624 | tf_op jit(solution)/shard_map/all_gather | solution.py:44
  190.6 0.0 all-to-all-done.2
  190.6 22.7 %bitcast_add_fusion = f32[1024,4096]{1,0:T(8,128)} fusion(bf16[1024,1024]{1,0:T(8,128)(2,1)S(1)} %copy-done, bf16[1024,4096]{1,0:T(8,128)(2,1)} %all-gather.3.cloned.1.call-done, bf16[2,1024,4096]{2,1,0:T(8,128)(2,1)} %param.19, f32[]{:T(128)} %bitcast.10, f32[]{:T(128)} %bitcast.9, f32[]{:T(128)} %bitcast.7, f32[1024]{0:T(1024)S(1)} %bitcast.30), kind=kOutput, calls=%fused_computation | convolution fusion | flops 8631877632 | bytes 44044300 | tf_op jit(solution)/shard_map/dot_general | solution.py:78
  213.3 0.0 copy-start.3
  213.3 0.0 reduce-scatter.2.cloned.1.call-update
  213.3 0.2 all-gather.5.cloned.1.call-start
  213.7 114.1 %reduce-scatter.2.cloned.1.call-done = f32[1024,512]{1,0:T(8,128)} async-done(((f32[1024,4096]{1,0:T(8,128)}), f32[1024,512]{1,0:T(8,128)}) %reduce-scatter.2.cloned.1.call-update) | async-done | bytes 2097168 | tf_op jit(solution)/shard_map/reduce_scatter | solution.py:86
  327.7 0.0 copy-done.3
  327.7 5.9 %divide_subtract_fusion = f32[1024,512]{1,0:T(8,128)} fusion(f32[1024,512]{1,0:T(8,128)} %param.15, f32[1024,512]{1,0:T(8,128)} %reduce-scatter.2.cloned.1.call-done, bf16[1024,512]{1,0:T(8,128)(2,1)S(1)} %copy-done.2, f32[1024,512]{1,0:T(8,128)S(1)} %copy-done.3, f32[1024,512]{1,0:T(8,128)} %param.16, f32[]{:T(128)S(6)} %sub.22, f32[]{:T(128)S(6)} %sub.21, ...), kind=kLoop, calls=%fused_computation.6 | loop fusion | flops 8912896 | bytes 11534348 | tf_op jit(solution)/shard_map/sub | solution.py:100
  333.6 0.0 all-gather.5.cloned.1.call-update
  333.7 11.7 %copy.29 = bf16[1024,4096]{1,0:T(8,128)(2,1)} copy(bf16[1024,4096]{0,1:T(8,128)(2,1)} %bitcast.29) | data formatting | bytes 16777216 | tf_op jit(solution)/shard_map/optimization_barrier | solution.py:76
  345.4 0.0 copy-start.4
  345.4 0.0 copy-start.5
  345.4 16.6 %broadcast_select_fusion = bf16[2,1024,4096]{2,1,0:T(8,128)(2,1)} fusion(bf16[2,1024,4096]{2,1,0:T(8,128)(2,1)} %param.19, pred[2]{0:T(512)(128)(4,1)S(1)} %broadcast_compare_fusion, bf16[1024,4096]{1,0:T(8,128)(2,1)} %copy.29), kind=kLoop, calls=%fused_computation.2 | loop fusion | flops 8388608 | bytes 41943040 | tf_op jit(solution)/shard_map/jit(_where)/select_n | solution.py:84
  362.0 0.0 copy-done.4
  362.0 0.0 copy-done.5
  362.0 3.5 multiply_add_fusion
  365.5 58.1 %all-gather.5.cloned.1.call-done = f32[1024,4096]{1,0:T(8,128)} async-done(((f32[1024,512]{1,0:T(8,128)}), f32[1024,4096]{1,0:T(8,128)}) %all-gather.5.cloned.1.call-update) | async-done | bytes 16777232 | tf_op jit(solution)/shard_map/all_gather | solution.py:106
  423.5 0.0 copy-start.1
  423.5 11.9 %copy.35 = f32[1024,4096]{1,0:T(8,128)} copy(f32[1024,4096]{1,0:T(8,128)} %all-gather.5.cloned.1.call-done) | data formatting | bytes 33554432
  435.4 0.0 copy-done.1
  (3 shorter events, 0.0 us)
Async XLA Ops:
  7.2 1.6 copy-start
  7.2 183.4 %all-gather.3.cloned.1.call-start = ((), (), s32[]{:S(2)}) async-start(), calls=%async_computation.4 | async-start | bytes 10485760 | tf_op jit(solution)/shard_map/all_gather | solution.py:44
  9.5 32.1 %copy-start.2 = (bf16[1024,512]{1,0:T(8,128)(2,1)S(1)}, bf16[1024,512]{1,0:T(8,128)(2,1)}, u32[]{:S(2)}) copy-start(bf16[1024,512]{1,0:T(8,128)(2,1)} %param.18) | copy-start | bytes 3145732
  45.8 6.0 %copy-start.8 = (s32[2]{0:T(128)S(1)}, s32[2]{0:T(128)}, u32[]{:S(2)}) copy-start(s32[2]{0:T(128)} %param.20) | copy-start | bytes 28
  45.8 6.0 %copy-start.7 = (f32[16]{0:T(128)S(1)}, f32[16]{0:T(128)}, u32[]{:S(2)}) copy-start(f32[16]{0:T(128)} %param.21) | copy-start | bytes 196
  45.8 6.2 %copy-start.6 = (s32[1,256]{1,0:T(1,128)S(1)}, s32[1,256]{1,0:T(1,128)}, u32[]{:S(2)}) copy-start(s32[1,256]{1,0:T(1,128)} %param.14) | copy-start | bytes 3076
  45.8 99.3 %all-to-all-start.1 = ((bf16[8,1024,512]{2,1,0:T(8,128)(2,1)}), bf16[8,1024,512]{2,1,0:T(8,128)(2,1)}, u32[]{:S(2)}, u32[]{:S(2)}) async-start(bf16[8,1024,512]{2,1,0:T(8,128)(2,1)} %broadcast_in_dim.60), calls=%async_computation.1 | async-start | bytes 16777216 | tf_op jit(solution)/shard_map/all_to_all | solution.py:60
  145.7 44.9 %all-to-all-start.2 = ((f32[4,1,256]{2,1,0:T(1,128)}), f32[4,1,256]{2,1,0:T(1,128)S(1)}, u32[]{:S(2)}, u32[]{:S(2)}) async-start(f32[4,1,256]{2,1,0:T(1,128)} %broadcast_in_dim.63), calls=%async_computation.2 | async-start | bytes 8192 | tf_op jit(solution)/shard_map/all_to_all | solution.py:56
  149.0 178.7 %reduce-scatter.2.cloned.1.call-start = ((), (), s32[]{:S(2)}) async-start(), calls=%async_computation.5 | async-start | bytes 18874368 | tf_op jit(solution)/shard_map/reduce_scatter | solution.py:86
  213.3 114.4 %copy-start.3 = (f32[1024,512]{1,0:T(8,128)S(1)}, f32[1024,512]{1,0:T(8,128)}, u32[]{:S(2)}) copy-start(f32[1024,512]{1,0:T(8,128)} %param.17) | copy-start | bytes 6291460
  213.3 210.2 %all-gather.5.cloned.1.call-start = ((), (), s32[]{:S(2)}) async-start(), calls=%async_computation.6 | async-start | bytes 18874368 | tf_op jit(solution)/shard_map/all_gather | solution.py:106
  345.4 16.6 %copy-start.4 = (f32[1024,512]{1,0:T(8,128)S(1)}, f32[1024,512]{1,0:T(8,128)}, u32[]{:S(2)}) copy-start(f32[1024,512]{1,0:T(8,128)} %param.16) | copy-start | bytes 6291460
  345.4 16.6 %copy-start.5 = (f32[1024,512]{1,0:T(8,128)S(1)}, f32[1024,512]{1,0:T(8,128)}, u32[]{:S(2)}) copy-start(f32[1024,512]{1,0:T(8,128)} %reduce-scatter.2.cloned.1.call-done) | copy-start | bytes 6291460
  423.5 11.9 %copy-start.1 = (bf16[1024,1024]{1,0:T(8,128)(2,1)S(1)}, bf16[1024,1024]{1,0:T(8,128)(2,1)}, u32[]{:S(2)}) copy-start(bf16[1024,1024]{1,0:T(8,128)(2,1)} %param.13) | copy-start | bytes 6291460
Sparse Core Ops, SparseCore 0:
  41.8 148.7 all-gather.2
  213.4 114.2 reduce-scatter.1
  333.8 89.7 all-gather.4

commit v9 on v8

--- a/solution.py
+++ b/solution.py
@@ -74,18 +74,31 @@
             history_part = history_part + lag_weight[position] * history[position].astype(jnp.float32)
 
         full_act, full_fresh = lax.optimization_barrier((full_act, full_fresh))
-        scaled = (full_act.astype(jnp.float32) * factors[:, None]).astype(jnp.bfloat16)
-        gradient = lax.dot_general(
-            cotangents,
-            scaled,
-            (((0,), (0,)), ((), ())),
-            preferred_element_type=jnp.float32,
+        noise_scale = noise_mult[0] * clip
+
+        me = lax.axis_index("fsdp")
+        own_cot = lax.dynamic_slice_in_dim(cotangents, me * tok, tok, axis=0)
+        own_scaled = (activations.astype(jnp.float32) * factor[:, None]).astype(jnp.bfloat16)
+        base = lax.dot_general(
+            own_cot, own_scaled, (((0,), (0,)), ((), ())), preferred_element_type=jnp.float32
+        ) + noise_scale * history_part
+        base, full_fresh = lax.optimization_barrier((base, full_fresh))
+        new_history = jnp.where((slot_ids == target)[:, None, None], full_fresh[None], history)
+        others = [(me + j) % n_fsdp for j in range(1, n_fsdp)]
+        other_rows = jnp.concatenate(
+            [lax.dynamic_slice_in_dim(full_act, i * tok, tok, axis=0) for i in others], axis=0
         )
-        new_history = jnp.where((slot_ids == target)[:, None, None], full_fresh[None], history)
-        noise_scale = noise_mult[0] * clip
-        combined = lax.psum_scatter(
-            gradient + noise_scale * history_part, "dp", scatter_dimension=1, tiled=True
+        other_factors = jnp.concatenate(
+            [lax.dynamic_slice_in_dim(factors, i * tok, tok, axis=0) for i in others], axis=0
         )
+        other_cot = jnp.concatenate(
+            [lax.dynamic_slice_in_dim(cotangents, i * tok, tok, axis=0) for i in others], axis=0
+        )
+        other_scaled = (other_rows.astype(jnp.float32) * other_factors[:, None]).astype(jnp.bfloat16)
+        payload = base + lax.dot_general(
+            other_cot, other_scaled, (((0,), (0,)), ((), ())), preferred_element_type=jnp.float32
+        )
+        combined = lax.psum_scatter(payload, "dp", scatter_dimension=1, tiled=True)
         examples = EX_DEV * n_dp * n_fsdp
         step_float = step_value.astype(jnp.float32)
         first_scale = 1.0 - jnp.power(jnp.float32(0.9), step_float)

time: 443 us -> 441 us (level)
  waiting for transfers between devices: 290 us -> 273 us
  blocking collectives: 32.1 us -> 40.2 us
  matrix products: 27.2 us -> 33.2 us
  local copies, waits for them, and re-layouts: 41.8 us -> 46.5 us
    all_to_all x1, waiting for transfers between devices: 89.2 us -> 77.4 us  [body(): lax.all_to_all(jnp.broadcast_to(fresh_noise[None], (n_dp,) + fresh_noise....]
    all_to_all x0 -> x1, blocking collectives: none -> 8.11 us  [body(): lax.all_to_all(jnp.broadcast_to(factor[None], (n_fsdp, tok)), 'fsdp', 0,...]
    dynamic_slice x0 -> x3, local copies, waits for them, and re-layouts: none -> 6.79 us  [the longest x1 5.53 us: body(): lax.dynamic_slice_in_dim(full_act, i * tok, tok, axis=0)]
    dot_general x1 -> x2, matrix products: 22.7 us -> 28.2 us  [the longest x1 15 us: body(): lax.dot_general(other_cot, other_scaled, (((0,), (0,)), ((), ())), prefer...]
    all_gather x1, waiting for transfers between devices: 28.9 us -> 23.8 us  [body(): full_act = lax.all_gather(gather_in, 'fsdp', axis=0, tiled=True)]
    unnamed x19 -> x21, local copies, waits for them, and re-layouts: 13.4 us -> 11.8 us
  transfers between devices with their start and end apart: 5 -> 4, of which waited for: 4 -> 4; matrix products, arithmetic and copies ran while one was open for 12% -> 15% of each run, Pallas kernels for 0% -> 0%
where the time goes in v9:
time: 441 us; the launch traced here: 440 us
  waiting for transfers between devices  273 us (62%)
  local copies, waits for them, and re-layouts  46.5 us (11%)
  blocking collectives  40.2 us (9%)
  matrix products  33.2 us (8%)
  other arithmetic  26.3 us (6%)
  between operations  15.3 us (3%)
  starting transfers between devices  5.47 us (1%)
    reduce_scatter x1, waiting for transfers between devices, body(): combined = lax.psum_scatter(payload, 'dp', scatter_dimension=1, tiled=True)  114 us
    all_to_all x1, waiting for transfers between devices, body(): lax.all_to_all(jnp.broadcast_to(fresh_noise[None], (n_dp,) + fresh_noise....  77.4 us
    all_gather x1, waiting for transfers between devices, body(): lax.all_gather(with_layout_constraint(new_weights, row_major), 'dp', axis...  57.9 us
    all_to_all x1, blocking collectives, body(): received = lax.all_to_all(partial_gram, 'fsdp', 0, 0, tiled=True)  32.1 us
    all_gather x1, waiting for transfers between devices, body(): full_act = lax.all_gather(gather_in, 'fsdp', axis=0, tiled=True)  23.8 us
    select_n x1, other arithmetic, body(): jnp.where((slot_ids == target)[:, None, None], full_fresh[None], history)  16.6 us
    dot_general x1, matrix products, body(): lax.dot_general(other_cot, other_scaled, (((0,), (0,)), ((), ())), prefer...  15 us
    dot_general x1, matrix products, body(): lax.dot_general(own_cot, own_scaled, (((0,), (0,)), ((), ())), preferred_...  13.2 us
  transfers between devices with their start and end apart: 4, of which 4 were waited for; matrix products, arithmetic and copies ran while one was open for 15% of the time, Pallas kernels for 0%

profile of v9, /device:TPU:0, one launch (start us, length us, event | category | flops | bytes accessed | tf_op | source)
XLA Modules:
  0.0 440.2 jit_solution(14845524290273037279)
XLA Ops:
  7.2 0.0 all-gather.3.cloned.1.call-start
  7.2 3.0 fusion.24
  10.2 0.0 copy-start.5
  10.2 0.0 copy-start.7
  10.2 32.1 %all_to_all.16 = f32[4,256,256]{1,2,0:T(8,128)} all-to-all(f32[4,256,256]{1,2,0:T(8,128)S(1)} %fusion.24), channel_id=1, replica_groups=mesh['dp'=8,'fsdp'=4] {'fsdp'}, dimensions={0} | all-to-all | bytes 2097152 | tf_op jit(solution)/shard_map/all_to_all | solution.py:41
  42.3 0.0 all-gather.3.cloned.1.call-update
  42.3 0.0 copy-done.5
  42.3 0.0 copy-done.7
  42.4 0.0 copy-start.1
  42.4 2.0 fusion.14
  44.4 0.1 fusion.16
  44.6 8.1 %all_to_all.17 = f32[4,1,256]{2,1,0:T(1,128)S(1)} all-to-all(f32[4,1,256]{2,1,0:T(1,128)S(1)} %broadcast_in_dim.67), channel_id=1, replica_groups=mesh['dp'=8,'fsdp'=4] {'fsdp'}, dimensions={0} | all-to-all | bytes 8192 | tf_op jit(solution)/shard_map/all_to_all | solution.py:56
  52.7 0.0 copy-done.1
  52.7 4.1 broadcast_in_dim.66
  56.8 0.0 copy-start.9
  56.8 0.0 copy-start.8
  56.8 0.0 copy-start
  56.8 5.2 %all-to-all-start.1 = ((bf16[8,1024,512]{2,1,0:T(8,128)(2,1)}), bf16[8,1024,512]{2,1,0:T(8,128)(2,1)}, u32[]{:S(2)}, u32[]{:S(2)}) async-start(bf16[8,1024,512]{2,1,0:T(8,128)(2,1)} %broadcast_in_dim.66), calls=%async_computation.1 | async-start | bytes 16777216 | tf_op jit(solution)/shard_map/all_to_all | solution.py:60
  62.0 0.0 reduce-scatter.2.cloned.1.call-start
  63.4 0.0 copy-start.6
  63.4 0.0 copy-done.9
  63.4 0.0 copy-done.8
  63.4 0.2 fusion.18
  63.6 0.6 fusion.23
  64.2 0.0 copy-done
  64.2 1.2 constant_dynamic-slice_fusion.5
  65.4 0.0 copy-done.6
  65.4 13.2 %bitcast_add_fusion = f32[1024,4096]{1,0:T(8,128)} fusion(bf16[2,1024,4096]{2,1,0:T(8,128)(2,1)} %param.19, f32[]{:T(128)} %bitcast.6, f32[]{:T(128)} %bitcast.5, f32[]{:T(128)} %bitcast.3, bf16[256,4096]{1,0:T(8,128)(2,1)S(1)} %copy-done.6, f32[256]{0:T(256)S(1)} %maximum_divide_fusion, bf16[1024,1024]{1,0:T(8,128)(2,1)S(1)} %copy-done, s32[]{:T(128)S(6)} %select_n.59), kind=kOutput, calls=%fused_computation | convolution fusion | flops 2179989504 | bytes 36176912 | tf_op jit(solution)/shard_map/dot_general | solution.py:82
  78.6 0.1 fusion.22
  78.7 77.4 %all-to-all-done.1 = bf16[8,1024,512]{2,1,0:T(8,128)(2,1)} async-done(((bf16[8,1024,512]{2,1,0:T(8,128)(2,1)}), bf16[8,1024,512]{2,1,0:T(8,128)(2,1)}, u32[]{:S(2)}, u32[]{:S(2)}) %all-to-all-start.1) | async-done | bytes 8388640 | tf_op jit(solution)/shard_map/all_to_all | solution.py:60
  156.0 11.4 %copy.24 = bf16[8,1024,512]{1,2,0:T(8,128)(2,1)} copy(bf16[8,1024,512]{2,1,0:T(8,128)(2,1)} %all-to-all-done.1) | data formatting | bytes 16777216 | tf_op jit(solution)/shard_map/all_to_all | solution.py:60
  167.4 23.8 %all-gather.3.cloned.1.call-done = bf16[1024,4096]{1,0:T(8,128)(2,1)} async-done(((bf16[256,4096]{1,0:T(8,128)(2,1)}), bf16[1024,4096]{1,0:T(8,128)(2,1)}) %all-gather.3.cloned.1.call-update) | async-done | bytes 8388624 | tf_op jit(solution)/shard_map/all_gather | solution.py:44
  191.2 5.5 %constant_dynamic-slice_fusion.2 = (bf16[256,4096]{1,0:T(8,128)(2,1)S(1)}, bf16[256,4096]{1,0:T(8,128)(2,1)}, bf16[256,4096]{1,0:T(8,128)(2,1)}) fusion(bf16[1024,4096]{1,0:T(8,128)(2,1)} %all-gather.3.cloned.1.call-done, s32[]{:T(128)S(6)} %select_n.65, s32[]{:T(128)S(6)} %select_n.69, s32[]{:T(128)S(6)} %select_n.67), kind=kLoop, calls=%fused_computation.36 | loop fusion | bytes 12582924 | tf_op jit(solution)/shard_map/dynamic_slice | solution.py:89
  196.7 15.0 %convolution_add_fusion = f32[1024,4096]{1,0:T(8,128)} fusion(f32[1024,4096]{1,0:T(8,128)} %bitcast_add_fusion, bf16[256,4096]{1,0:T(8,128)(2,1)} %get-tuple-element.25, bf16[256,4096]{1,0:T(8,128)(2,1)} %get-tuple-element.26, bf16[256,4096]{1,0:T(8,128)(2,1)S(1)} %get-tuple-element.24, f32[768]{0:T(1024)S(1)} %pad_maximum_fusion, ...), kind=kOutput, calls=%fused_computation.3 | convolution fusion | flops 6476529664 | bytes 41421824 | tf_op jit(solution)/shard_map/dot_general | solution.py:98
  211.8 0.0 copy-start.2
  211.8 0.0 reduce-scatter.2.cloned.1.call-update
  211.8 0.2 all-gather.5.cloned.1.call-start
  212.2 114.0 %reduce-scatter.2.cloned.1.call-done = f32[1024,512]{1,0:T(8,128)} async-done(((f32[1024,4096]{1,0:T(8,128)}), f32[1024,512]{1,0:T(8,128)}) %reduce-scatter.2.cloned.1.call-update) | async-done | bytes 2097168 | tf_op jit(solution)/shard_map/reduce_scatter | solution.py:101
  326.2 0.0 copy-done.2
  326.2 5.9 %divide_subtract_fusion = f32[1024,512]{1,0:T(8,128)} fusion(f32[1024,512]{1,0:T(8,128)} %param.15, f32[1024,512]{1,0:T(8,128)} %reduce-scatter.2.cloned.1.call-done, bf16[1024,512]{1,0:T(8,128)(2,1)S(1)} %copy-done.1, f32[1024,512]{1,0:T(8,128)S(1)} %copy-done.2, f32[1024,512]{1,0:T(8,128)} %param.16, f32[]{:T(128)S(6)} %sub.22, f32[]{:T(128)S(6)} %sub.21, ...), kind=kLoop, calls=%fused_computation.13 | loop fusion | flops 8912896 | bytes 11534348 | tf_op jit(solution)/shard_map/sub | solution.py:113
  332.1 0.0 all-gather.5.cloned.1.call-update
  332.1 11.8 %copy.25 = bf16[1024,4096]{1,0:T(8,128)(2,1)} copy(bf16[1024,4096]{0,1:T(8,128)(2,1)} %bitcast.25) | data formatting | bytes 16777216 | tf_op jit(solution)/shard_map/optimization_barrier | solution.py:85
  344.0 0.0 copy-start.3
  344.0 0.0 copy-start.4
  344.0 16.6 %broadcast_select_fusion = bf16[2,1024,4096]{2,1,0:T(8,128)(2,1)} fusion(bf16[2,1024,4096]{2,1,0:T(8,128)(2,1)} %param.19, pred[2]{0:T(512)(128)(4,1)S(1)} %broadcast_compare_fusion, bf16[1024,4096]{1,0:T(8,128)(2,1)} %copy.25), kind=kLoop, calls=%fused_computation.1 | loop fusion | flops 8388608 | bytes 41943040 | tf_op jit(solution)/shard_map/jit(_where)/select_n | solution.py:86
  360.6 0.0 copy-done.3
  360.6 0.0 copy-done.4
  360.6 3.5 multiply_add_fusion
  364.1 57.9 %all-gather.5.cloned.1.call-done = f32[1024,4096]{1,0:T(8,128)} async-done(((f32[1024,512]{1,0:T(8,128)}), f32[1024,4096]{1,0:T(8,128)}) %all-gather.5.cloned.1.call-update) | async-done | bytes 16777232 | tf_op jit(solution)/shard_map/all_gather | solution.py:119
  422.0 11.7 %copy.30 = f32[1024,4096]{1,0:T(8,128)} copy(f32[1024,4096]{1,0:T(8,128)} %all-gather.5.cloned.1.call-done) | data formatting | bytes 33554432
  (5 shorter events, 0.0 us)
Async XLA Ops:
  7.2 184.0 %all-gather.3.cloned.1.call-start = ((), (), s32[]{:S(2)}) async-start(), calls=%async_computation.4 | async-start | bytes 10485760 | tf_op jit(solution)/shard_map/all_gather | solution.py:44
  10.2 32.2 %copy-start.5 = (bf16[256,4096]{1,0:T(8,128)(2,1)S(1)}, bf16[256,4096]{1,0:T(8,128)(2,1)}, u32[]{:S(2)}) copy-start(bf16[256,4096]{1,0:T(8,128)(2,1)} %param.12) | copy-start | bytes 6291460
  10.2 32.2 %copy-start.7 = (s32[1,256]{1,0:T(1,128)S(1)}, s32[1,256]{1,0:T(1,128)}, u32[]{:S(2)}) copy-start(s32[1,256]{1,0:T(1,128)} %param.14) | copy-start | bytes 3076
  42.4 10.3 %copy-start.1 = (bf16[1024,512]{1,0:T(8,128)(2,1)S(1)}, bf16[1024,512]{1,0:T(8,128)(2,1)}, u32[]{:S(2)}) copy-start(bf16[1024,512]{1,0:T(8,128)(2,1)} %param.18) | copy-start | bytes 3145732
  56.8 6.6 %copy-start.9 = (s32[2]{0:T(128)S(1)}, s32[2]{0:T(128)}, u32[]{:S(2)}) copy-start(s32[2]{0:T(128)} %param.20) | copy-start | bytes 28
  56.8 6.6 %copy-start.8 = (f32[16]{0:T(128)S(1)}, f32[16]{0:T(128)}, u32[]{:S(2)}) copy-start(f32[16]{0:T(128)} %param.21) | copy-start | bytes 196
  56.8 7.4 %copy-start = (bf16[1024,1024]{1,0:T(8,128)(2,1)S(1)}, bf16[1024,1024]{1,0:T(8,128)(2,1)}, u32[]{:S(2)}) copy-start(bf16[1024,1024]{1,0:T(8,128)(2,1)} %param.13) | copy-start | bytes 6291460
  56.8 99.2 %all-to-all-start.1 = ((bf16[8,1024,512]{2,1,0:T(8,128)(2,1)}), bf16[8,1024,512]{2,1,0:T(8,128)(2,1)}, u32[]{:S(2)}, u32[]{:S(2)}) async-start(bf16[8,1024,512]{2,1,0:T(8,128)(2,1)} %broadcast_in_dim.66), calls=%async_computation.1 | async-start | bytes 16777216 | tf_op jit(solution)/shard_map/all_to_all | solution.py:60
  62.0 264.2 %reduce-scatter.2.cloned.1.call-start = ((), (), s32[]{:S(2)}) async-start(), calls=%async_computation.5 | async-start | bytes 18874368 | tf_op jit(solution)/shard_map/reduce_scatter | solution.py:101
  63.4 2.0 copy-start.6
  211.8 114.4 %copy-start.2 = (f32[1024,512]{1,0:T(8,128)S(1)}, f32[1024,512]{1,0:T(8,128)}, u32[]{:S(2)}) copy-start(f32[1024,512]{1,0:T(8,128)} %param.17) | copy-start | bytes 6291460
  211.8 210.2 %all-gather.5.cloned.1.call-start = ((), (), s32[]{:S(2)}) async-start(), calls=%async_computation.6 | async-start | bytes 18874368 | tf_op jit(solution)/shard_map/all_gather | solution.py:119
  344.0 16.6 %copy-start.3 = (f32[1024,512]{1,0:T(8,128)S(1)}, f32[1024,512]{1,0:T(8,128)}, u32[]{:S(2)}) copy-start(f32[1024,512]{1,0:T(8,128)} %param.16) | copy-start | bytes 6291460
  344.0 16.6 %copy-start.4 = (f32[1024,512]{1,0:T(8,128)S(1)}, f32[1024,512]{1,0:T(8,128)}, u32[]{:S(2)}) copy-start(f32[1024,512]{1,0:T(8,128)} %reduce-scatter.2.cloned.1.call-done) | copy-start | bytes 6291460
Sparse Core Ops, SparseCore 0:
  42.5 148.7 all-gather.2
  211.9 114.2 reduce-scatter.1
  332.2 89.7 all-gather.4

commit v10 on v9

--- a/solution.py
+++ b/solution.py
@@ -84,17 +84,9 @@
         ) + noise_scale * history_part
         base, full_fresh = lax.optimization_barrier((base, full_fresh))
         new_history = jnp.where((slot_ids == target)[:, None, None], full_fresh[None], history)
-        others = [(me + j) % n_fsdp for j in range(1, n_fsdp)]
-        other_rows = jnp.concatenate(
-            [lax.dynamic_slice_in_dim(full_act, i * tok, tok, axis=0) for i in others], axis=0
-        )
-        other_factors = jnp.concatenate(
-            [lax.dynamic_slice_in_dim(factors, i * tok, tok, axis=0) for i in others], axis=0
-        )
-        other_cot = jnp.concatenate(
-            [lax.dynamic_slice_in_dim(cotangents, i * tok, tok, axis=0) for i in others], axis=0
-        )
-        other_scaled = (other_rows.astype(jnp.float32) * other_factors[:, None]).astype(jnp.bfloat16)
+        row_block = jnp.arange(cotangents.shape[0], dtype=jnp.int32) // tok
+        other_cot = jnp.where((row_block == me)[:, None], jnp.zeros_like(cotangents), cotangents)
+        other_scaled = (full_act.astype(jnp.float32) * factors[:, None]).astype(jnp.bfloat16)
         payload = base + lax.dot_general(
             other_cot, other_scaled, (((0,), (0,)), ((), ())), preferred_element_type=jnp.float32
         )

time: 441 us -> 440 us (level)
  blocking collectives: 40.2 us -> 32.1 us
  local copies, waits for them, and re-layouts: 46.5 us -> 39.9 us
  matrix products: 33.2 us -> 39.5 us
    all_to_all x1, waiting for transfers between devices: 77.4 us -> 88.2 us  [body(): lax.all_to_all(jnp.broadcast_to(fresh_noise[None], (n_dp,) + fresh_noise....]
    all_to_all x1 -> x0, blocking collectives: 8.11 us -> none  [body(): lax.all_to_all(jnp.broadcast_to(factor[None], (n_fsdp, tok)), 'fsdp', 0,...]
    all_gather x1, waiting for transfers between devices: 23.8 us -> 16.1 us  [body(): full_act = lax.all_gather(gather_in, 'fsdp', axis=0, tiled=True)]
    dynamic_slice x3 -> x0, local copies, waits for them, and re-layouts: 6.79 us -> none  [the longest x1 5.53 us: body(): lax.dynamic_slice_in_dim(full_act, i * tok, tok, axis=0)]
    unnamed x21 -> x17, local copies, waits for them, and re-layouts: 11.8 us -> 11.8 us
  transfers between devices with their start and end apart: 4 -> 5, of which waited for: 4 -> 4; matrix products, arithmetic and copies ran while one was open for 15% -> 15% of each run, Pallas kernels for 0% -> 0%
where the time goes in v10:
time: 440 us; the launch traced here: 439 us
  waiting for transfers between devices  277 us (63%)
  local copies, waits for them, and re-layouts  39.9 us (9%)
  matrix products  39.5 us (9%)
  blocking collectives  32.1 us (7%)
  other arithmetic  26.4 us (6%)
  between operations  15.3 us (3%)
  starting transfers between devices  8.85 us (2%)
    reduce_scatter x1, waiting for transfers between devices, body(): combined = lax.psum_scatter(payload, 'dp', scatter_dimension=1, tiled=True)  114 us
    all_to_all x1, waiting for transfers between devices, body(): lax.all_to_all(jnp.broadcast_to(fresh_noise[None], (n_dp,) + fresh_noise....  88.2 us
    all_gather x1, waiting for transfers between devices, body(): lax.all_gather(with_layout_constraint(new_weights, row_major), 'dp', axis...  58.2 us
    all_to_all x1, blocking collectives, body(): received = lax.all_to_all(partial_gram, 'fsdp', 0, 0, tiled=True)  32.1 us
    dot_general x1, matrix products, body(): lax.dot_general(other_cot, other_scaled, (((0,), (0,)), ((), ())), prefer...  19 us
    select_n x1, other arithmetic, body(): jnp.where((slot_ids == target)[:, None, None], full_fresh[None], history)  16.7 us
    all_gather x1, waiting for transfers between devices, body(): full_act = lax.all_gather(gather_in, 'fsdp', axis=0, tiled=True)  16.1 us
    dot_general x1, matrix products, body(): lax.dot_general(own_cot, own_scaled, (((0,), (0,)), ((), ())), preferred_...  14 us
  transfers between devices with their start and end apart: 5, of which 4 were waited for; matrix products, arithmetic and copies ran while one was open for 15% of the time, Pallas kernels for 0%

profile of v10, /device:TPU:0, one launch (start us, length us, event | category | flops | bytes accessed | tf_op | source)
XLA Modules:
  0.0 438.7 jit_solution(3228672578702460161)
XLA Ops:
  7.2 0.0 all-gather.3.cloned.1.call-start
  7.2 3.0 fusion.22
  10.2 0.0 copy-start
  10.2 32.1 %all_to_all.16 = f32[4,256,256]{1,2,0:T(8,128)} all-to-all(f32[4,256,256]{1,2,0:T(8,128)S(1)} %fusion.22), channel_id=1, replica_groups=mesh['dp'=8,'fsdp'=4] {'fsdp'}, dimensions={0} | all-to-all | bytes 2097152 | tf_op jit(solution)/shard_map/all_to_all | solution.py:41
  42.3 0.0 all-gather.3.cloned.1.call-update
  42.3 0.0 copy-done
  42.3 4.1 broadcast_in_dim.77
  46.5 0.0 copy-start.7
  46.5 0.0 copy-start.6
  46.5 0.0 copy-start.5
  46.5 5.3 %all-to-all-start.1 = ((bf16[8,1024,512]{2,1,0:T(8,128)(2,1)}), bf16[8,1024,512]{2,1,0:T(8,128)(2,1)}, u32[]{:S(2)}, u32[]{:S(2)}) async-start(bf16[8,1024,512]{2,1,0:T(8,128)(2,1)} %broadcast_in_dim.77), calls=%async_computation.1 | async-start | bytes 16777216 | tf_op jit(solution)/shard_map/all_to_all | solution.py:60
  53.1 0.0 copy-done.7
  53.1 0.0 copy-done.6
  53.1 0.2 fusion.16
  53.3 0.6 fusion.21
  53.9 0.0 copy-done.5
  53.9 0.0 copy-start.1
  53.9 3.5 fusion.8
  57.5 0.1 fusion.11
  57.6 88.2 %all-to-all-done.1 = bf16[8,1024,512]{2,1,0:T(8,128)(2,1)} async-done(((bf16[8,1024,512]{2,1,0:T(8,128)(2,1)}), bf16[8,1024,512]{2,1,0:T(8,128)(2,1)}, u32[]{:S(2)}, u32[]{:S(2)}) %all-to-all-start.1) | async-done | bytes 8388640 | tf_op jit(solution)/shard_map/all_to_all | solution.py:60
  145.8 0.6 broadcast_in_dim.80
  146.4 3.2 all-to-all-start.2
  149.7 0.0 reduce-scatter.2.cloned.1.call-start
  149.7 0.0 copy-done.1
  149.7 14.0 %bitcast_add_fusion = f32[1024,4096]{1,0:T(8,128)} fusion(bf16[2,1024,4096]{2,1,0:T(8,128)(2,1)} %param.19, f32[]{:T(128)} %bitcast.6, f32[]{:T(128)} %bitcast.5, f32[]{:T(128)} %bitcast.3, bf16[256,4096]{1,0:T(8,128)(2,1)} %param.12, f32[256]{0:T(256)S(1)} %maximum_divide_fusion, bf16[1024,1024]{1,0:T(8,128)(2,1)S(1)} %copy-done.1, s32[]{:T(128)S(6)} %select_n.45), kind=kOutput, calls=%fused_computation | convolution fusion | flops 2179989504 | bytes 36176912 | tf_op jit(solution)/shard_map/dot_general | solution.py:82
  163.8 11.4 %copy.24 = bf16[8,1024,512]{1,2,0:T(8,128)(2,1)} copy(bf16[8,1024,512]{2,1,0:T(8,128)(2,1)} %all-to-all-done.1) | data formatting | bytes 16777216 | tf_op jit(solution)/shard_map/all_to_all | solution.py:60
  175.1 16.1 %all-gather.3.cloned.1.call-done = bf16[1024,4096]{1,0:T(8,128)(2,1)} async-done(((bf16[256,4096]{1,0:T(8,128)(2,1)}), bf16[1024,4096]{1,0:T(8,128)(2,1)}) %all-gather.3.cloned.1.call-update) | async-done | bytes 8388624 | tf_op jit(solution)/shard_map/all_gather | solution.py:44
  191.2 0.0 all-to-all-done.2
  191.2 19.0 %fusion.2 = f32[1024,4096]{1,0:T(8,128)} fusion(f32[1024,4096]{1,0:T(8,128)} %bitcast_add_fusion, bf16[1024,4096]{1,0:T(8,128)(2,1)} %all-gather.3.cloned.1.call-done, f32[1024]{0:T(1024)S(1)} %bitcast.27, bf16[1024,1024]{1,0:T(8,128)(2,1)S(1)} %copy-done.1, pred[1024]{0:T(1024)(128)(4,1)S(1)} %fusion.12), kind=kOutput, calls=%fused_computation.5 | convolution fusion | flops 8607760384 | bytes 44045312 | tf_op jit(solution)/shard_map/dot_general | solution.py:90
  210.2 0.0 copy-start.2
  210.2 0.0 reduce-scatter.2.cloned.1.call-update
  210.2 0.2 all-gather.5.cloned.1.call-start
  210.6 114.0 %reduce-scatter.2.cloned.1.call-done = f32[1024,512]{1,0:T(8,128)} async-done(((f32[1024,4096]{1,0:T(8,128)}), f32[1024,512]{1,0:T(8,128)}) %reduce-scatter.2.cloned.1.call-update) | async-done | bytes 2097168 | tf_op jit(solution)/shard_map/reduce_scatter | solution.py:93
  324.6 0.0 copy-done.2
  324.6 5.9 %divide_subtract_fusion = f32[1024,512]{1,0:T(8,128)} fusion(f32[1024,512]{1,0:T(8,128)} %param.15, f32[1024,512]{1,0:T(8,128)} %reduce-scatter.2.cloned.1.call-done, bf16[1024,512]{1,0:T(8,128)(2,1)S(1)} %copy-done, f32[1024,512]{1,0:T(8,128)S(1)} %copy-done.2, f32[1024,512]{1,0:T(8,128)} %param.16, f32[]{:T(128)S(6)} %sub.29, f32[]{:T(128)S(6)} %sub.28, ...), kind=kLoop, calls=%fused_computation.9 | loop fusion | flops 8912896 | bytes 11534348 | tf_op jit(solution)/shard_map/sub | solution.py:105
  330.5 0.0 all-gather.5.cloned.1.call-update
  330.5 11.5 %copy.25 = bf16[1024,4096]{1,0:T(8,128)(2,1)} copy(bf16[1024,4096]{0,1:T(8,128)(2,1)} %bitcast.25) | data formatting | bytes 16777216 | tf_op jit(solution)/shard_map/optimization_barrier | solution.py:85
  342.0 0.0 copy-start.3
  342.0 0.0 copy-start.4
  342.0 16.7 %broadcast_select_fusion = bf16[2,1024,4096]{2,1,0:T(8,128)(2,1)} fusion(bf16[2,1024,4096]{2,1,0:T(8,128)(2,1)} %param.19, pred[2]{0:T(512)(128)(4,1)S(1)} %broadcast_compare_fusion, bf16[1024,4096]{1,0:T(8,128)(2,1)} %copy.25), kind=kLoop, calls=%fused_computation.2 | loop fusion | flops 8388608 | bytes 41943040 | tf_op jit(solution)/shard_map/jit(_where)/select_n | solution.py:86
  358.7 0.0 copy-done.3
  358.7 0.0 copy-done.4
  358.7 3.5 multiply_add_fusion
  362.2 58.2 %all-gather.5.cloned.1.call-done = f32[1024,4096]{1,0:T(8,128)} async-done(((f32[1024,512]{1,0:T(8,128)}), f32[1024,4096]{1,0:T(8,128)}) %all-gather.5.cloned.1.call-update) | async-done | bytes 16777232 | tf_op jit(solution)/shard_map/all_gather | solution.py:111
  420.4 11.7 %copy.30 = f32[1024,4096]{1,0:T(8,128)} copy(f32[1024,4096]{1,0:T(8,128)} %all-gather.5.cloned.1.call-done) | data formatting | bytes 33554432
  (4 shorter events, 0.0 us)
Async XLA Ops:
  7.2 184.1 %all-gather.3.cloned.1.call-start = ((), (), s32[]{:S(2)}) async-start(), calls=%async_computation.4 | async-start | bytes 10485760 | tf_op jit(solution)/shard_map/all_gather | solution.py:44
  10.2 32.1 %copy-start = (bf16[1024,512]{1,0:T(8,128)(2,1)S(1)}, bf16[1024,512]{1,0:T(8,128)(2,1)}, u32[]{:S(2)}) copy-start(bf16[1024,512]{1,0:T(8,128)(2,1)} %param.18) | copy-start | bytes 3145732
  46.5 6.6 %copy-start.7 = (s32[2]{0:T(128)S(1)}, s32[2]{0:T(128)}, u32[]{:S(2)}) copy-start(s32[2]{0:T(128)} %param.20) | copy-start | bytes 28
  46.5 6.7 %copy-start.6 = (f32[16]{0:T(128)S(1)}, f32[16]{0:T(128)}, u32[]{:S(2)}) copy-start(f32[16]{0:T(128)} %param.21) | copy-start | bytes 196
  46.5 7.4 %copy-start.5 = (s32[1,256]{1,0:T(1,128)S(1)}, s32[1,256]{1,0:T(1,128)}, u32[]{:S(2)}) copy-start(s32[1,256]{1,0:T(1,128)} %param.14) | copy-start | bytes 3076
  46.5 99.3 %all-to-all-start.1 = ((bf16[8,1024,512]{2,1,0:T(8,128)(2,1)}), bf16[8,1024,512]{2,1,0:T(8,128)(2,1)}, u32[]{:S(2)}, u32[]{:S(2)}) async-start(bf16[8,1024,512]{2,1,0:T(8,128)(2,1)} %broadcast_in_dim.77), calls=%async_computation.1 | async-start | bytes 16777216 | tf_op jit(solution)/shard_map/all_to_all | solution.py:60
  53.9 95.8 %copy-start.1 = (bf16[1024,1024]{1,0:T(8,128)(2,1)S(1)}, bf16[1024,1024]{1,0:T(8,128)(2,1)}, u32[]{:S(2)}) copy-start(bf16[1024,1024]{1,0:T(8,128)(2,1)} %param.13) | copy-start | bytes 6291460
  146.4 44.8 %all-to-all-start.2 = ((f32[4,1,256]{2,1,0:T(1,128)}), f32[4,1,256]{2,1,0:T(1,128)S(1)}, u32[]{:S(2)}, u32[]{:S(2)}) async-start(f32[4,1,256]{2,1,0:T(1,128)} %broadcast_in_dim.80), calls=%async_computation.2 | async-start | bytes 8192 | tf_op jit(solution)/shard_map/all_to_all | solution.py:56
  149.7 174.9 %reduce-scatter.2.cloned.1.call-start = ((), (), s32[]{:S(2)}) async-start(), calls=%async_computation.5 | async-start | bytes 18874368 | tf_op jit(solution)/shard_map/reduce_scatter | solution.py:93
  210.2 114.4 %copy-start.2 = (f32[1024,512]{1,0:T(8,128)S(1)}, f32[1024,512]{1,0:T(8,128)}, u32[]{:S(2)}) copy-start(f32[1024,512]{1,0:T(8,128)} %param.17) | copy-start | bytes 6291460
  210.2 210.2 %all-gather.5.cloned.1.call-start = ((), (), s32[]{:S(2)}) async-start(), calls=%async_computation.6 | async-start | bytes 18874368 | tf_op jit(solution)/shard_map/all_gather | solution.py:111
  342.0 16.7 %copy-start.3 = (f32[1024,512]{1,0:T(8,128)S(1)}, f32[1024,512]{1,0:T(8,128)}, u32[]{:S(2)}) copy-start(f32[1024,512]{1,0:T(8,128)} %param.16) | copy-start | bytes 6291460
  342.0 16.7 %copy-start.4 = (f32[1024,512]{1,0:T(8,128)S(1)}, f32[1024,512]{1,0:T(8,128)}, u32[]{:S(2)}) copy-start(f32[1024,512]{1,0:T(8,128)} %reduce-scatter.2.cloned.1.call-done) | copy-start | bytes 6291460
Sparse Core Ops, SparseCore 0:
  42.4 148.7 all-gather.2
  210.3 114.2 reduce-scatter.1
  330.6 89.7 all-gather.4
